TPU v7x, 256 devices: a whole 4x4x8 slice. The times are simulated.
256 devices in a mesh: gx: 16 (over x, y), gy: 16 (over z, core).
Axes of the slice: x: 4, y: 4, z: 8, core: 2. Of those that a mesh axis runs over, the one named last changes fastest.
Arguments:
- tokens: bfloat16 [2048, 2048], P('gy', 'gx'), may hold values from -6 to 6
- gain: bfloat16 [2048], P('gx'), may hold values from 0.5 to 1.5
- w_router: bfloat16 [2048, 8], P('gx'), may hold values from -0.25 to 0.25
- expert_query_weight: bfloat16 [8, 2048, 16, 128], P(None, 'gx', 'gy'), may hold values from -0.25 to 0.25
- key_value_weight: bfloat16 [2048, 16, 256], P('gx', 'gy'), may hold values from -0.125 to 0.125
- expert_output_weight: bfloat16 [8, 16, 128, 2048], P(None, 'gy', None, 'gx'), may hold values from -0.25 to 0.25
- cache_keys: bfloat16 [16, 16, 4096, 128], P('gx', 'gy'), may hold values from -1220 to 1220
- cached_value_slots: bfloat16 [16, 16, 4096, 128], P('gx', 'gy'), may hold values from -6 to 6
- lengths: int32 [16], replicated, may hold values from 1 to 4096, 34816 in all
- deal: int32 [16], replicated, may hold values from 0 to 15, each once
- route: int32 [2048, 2], replicated, may hold values from 0 to 7, all different within a row
Outputs:
- mixed: bfloat16 [2048, 2048], P('gy', 'gx')
Inputs may be any that keep to these rules, and one draw needn't show every extreme that they name: `lengths`: each request's cache holds between 1 and 4096 keys, and the longest holds exactly 4096. deal[r] is the cache slot of request r; every slot is used once. `route`: each token names 2 different attention experts.
All inputs are finite; a program needn't handle non-finite values.
Results may differ from a plain program's by a relative error of at most 0.01.
The roundings to bfloat16 on the way count: a program that leaves them out, or rounds other values in their place, can miss the bound.
Values may be sent and summed in bfloat16 or wider, within the bound.
No kernel may reach another device: no remote copies, remote signals or barrier semaphores. Data moves between devices by JAX's collectives and lax.ppermute only.
A program may use at most 64 MiB of HBM per device.

v0:
```python
import jax
import jax.numpy as jnp
from jax import lax
from jax.sharding import PartitionSpec as P

masked_score = -1e30
norm_eps = 1e-06


def expert_onehot(route_rows, experts):
    return (route_rows[:, :, None] == jnp.arange(experts, dtype=jnp.int32)[None, None, :]).astype(
        jnp.float32
    )


def absorb(carry_state, scores, value_rows):
    running_max, running_sum, accumulated = carry_state
    new_max = jnp.maximum(running_max, jnp.max(scores, axis=2))
    shrink = jnp.exp(running_max - new_max)
    weights = jnp.exp(scores - new_max[:, :, None])
    running_sum = running_sum * shrink + jnp.sum(weights, axis=2)
    accumulated = accumulated * shrink[:, :, None] + jnp.einsum(
        "hrk,hkd->hrd", weights.astype(jnp.bfloat16), value_rows, preferred_element_type=jnp.float32
    )
    return (new_max, running_sum, accumulated)


def per_device(
    tokens,
    gain,
    w_router,
    expert_query_weight,
    key_value_weight,
    expert_output_weight,
    cache_keys,
    cached_value_slots,
    lengths,
    deal,
    route,
):
    requests = lengths.shape[0]
    experts = expert_query_weight.shape[0]
    heads_local = expert_query_weight.shape[2]
    head_dim = expert_query_weight.shape[3]
    top_count = route.shape[1]
    gathered = lax.all_gather(tokens, "gy", axis=0, tiled=True)
    total_rows, local_width = gathered.shape
    new_len = total_rows // requests
    full_width = local_width * lax.axis_size("gx")
    slot_index = lax.axis_index("gx")
    inverse = jnp.zeros((requests,), jnp.int32).at[deal].set(jnp.arange(requests, dtype=jnp.int32))
    ordered = jnp.take(gathered.reshape(requests, new_len, local_width), inverse, axis=0).reshape(
        total_rows, local_width
    )
    slot_route = jnp.take(route.reshape(requests, new_len, top_count), inverse, axis=0).reshape(
        total_rows, top_count
    )
    widened = ordered.astype(jnp.float32)
    squares = jnp.sum(widened * widened, axis=1)
    scaled_input = (widened * gain.astype(jnp.float32)[None, :]).astype(jnp.bfloat16)
    router_part = jnp.dot(scaled_input, w_router, preferred_element_type=jnp.float32)
    query_part = jnp.einsum(
        "td,edhk->tehk", scaled_input, expert_query_weight, preferred_element_type=jnp.float32
    )
    keyval_part = jnp.einsum(
        "td,dhk->thk", scaled_input, key_value_weight, preferred_element_type=jnp.float32
    )
    my_route = lax.dynamic_slice_in_dim(slot_route, slot_index * new_len, new_len, 0)
    my_onehot = expert_onehot(my_route, experts)
    query_all, keyval_sums, router_sums, square_sums = (
        lax.psum_scatter(query_part, "gx", scatter_dimension=0, tiled=True),
        lax.psum_scatter(keyval_part, "gx", scatter_dimension=0, tiled=True),
        lax.psum_scatter(router_part, "gx", scatter_dimension=0, tiled=True),
        lax.psum_scatter(squares, "gx", scatter_dimension=0, tiled=True),
    )
    query_totals = jnp.sum(my_onehot[:, :, :, None, None] * query_all[:, None], axis=2)
    inverse_root_mean = lax.rsqrt(square_sums / full_width + norm_eps)
    logits = router_sums * inverse_root_mean[:, None]
    chosen = jnp.sum(my_onehot * logits[:, None, :], axis=2)
    gate_gap = chosen[:, 0] - chosen[:, 1]
    gate_weights = jnp.stack([jax.nn.sigmoid(gate_gap), jax.nn.sigmoid(-gate_gap)], axis=1).astype(
        jnp.bfloat16
    )
    query_matrix = (query_totals * inverse_root_mean[:, None, None, None]).astype(jnp.bfloat16)
    key_value_rows = (keyval_sums * inverse_root_mean[:, None, None]).astype(jnp.bfloat16)
    query_rows = new_len * top_count
    query_by_head = jnp.transpose(query_matrix, (2, 0, 1, 3)).reshape(
        heads_local, query_rows, head_dim
    )
    fresh_keyval = jnp.transpose(key_value_rows, (1, 0, 2))
    fresh_keys = fresh_keyval[:, :, :head_dim]
    fresh_values = fresh_keyval[:, :, head_dim:]
    length = jnp.take(lengths, jnp.take(inverse, slot_index))
    local_keys = cache_keys[0]
    local_values = cached_value_slots[0]
    cache_span = local_keys.shape[1]
    key_block = min(1024, cache_span)
    score_scale = head_dim ** (-0.5)
    initial = (
        jnp.full((heads_local, query_rows), masked_score, jnp.float32),
        jnp.zeros((heads_local, query_rows), jnp.float32),
        jnp.zeros((heads_local, query_rows, head_dim), jnp.float32),
    )

    def visit_block(block_index, carry_state):
        first_key = block_index * key_block
        key_rows = lax.dynamic_slice_in_dim(local_keys, first_key, key_block, 1)
        value_rows = lax.dynamic_slice_in_dim(local_values, first_key, key_block, 1)
        scores = (
            jnp.einsum("hrd,hkd->hrk", query_by_head, key_rows, preferred_element_type=jnp.float32)
            * score_scale
        )
        visible = first_key + jnp.arange(key_block, dtype=jnp.int32) < length
        scores = jnp.where(visible[None, None, :], scores, masked_score)
        return absorb(carry_state, scores, value_rows)

    block_count = (length + key_block - 1) // key_block
    carry_state = lax.fori_loop(0, block_count, visit_block, initial)
    fresh_scores = (
        jnp.einsum("hrd,hkd->hrk", query_by_head, fresh_keys, preferred_element_type=jnp.float32)
        * score_scale
    )
    causal = (
        jnp.arange(new_len, dtype=jnp.int32)[None, :]
        <= (jnp.arange(query_rows, dtype=jnp.int32) // top_count)[:, None]
    )
    fresh_scores = jnp.where(causal[None], fresh_scores, masked_score)
    running_max, running_sum, accumulated = absorb(carry_state, fresh_scores, fresh_values)
    attended_output = (accumulated / running_sum[:, :, None]).astype(jnp.bfloat16)
    attended_output = jnp.transpose(
        attended_output.reshape(heads_local, new_len, top_count, head_dim), (1, 2, 0, 3)
    ).reshape(new_len, top_count * heads_local * head_dim)
    all_attended, all_gates = (
        lax.all_gather(attended_output, "gx", axis=0, tiled=True),
        lax.all_gather(gate_weights, "gx", axis=0, tiled=True),
    )
    token_attended = jnp.take(
        all_attended.reshape(requests, new_len, top_count * heads_local * head_dim), deal, axis=0
    ).reshape(total_rows, top_count, heads_local, head_dim)
    token_gates = (
        jnp.take(all_gates.reshape(requests, new_len, top_count), deal, axis=0)
        .reshape(total_rows, top_count)
        .astype(jnp.float32)
    )
    wide_output = expert_output_weight.astype(jnp.float32)
    piece = token_attended.astype(jnp.float32)
    mixing = expert_onehot(route, experts) * token_gates[:, :, None]
    folded = jnp.einsum("tse,tshd->tehd", mixing, piece, precision=lax.Precision.HIGHEST)
    output_sum = lax.psum_scatter(
        jnp.einsum("tehd,ehdo->to", folded, wide_output, precision=lax.Precision.HIGHEST),
        "gy",
        scatter_dimension=0,
        tiled=True,
    )
    return output_sum.astype(jnp.bfloat16)


def solution(mesh):
    placed = (
        P("gy", "gx"),
        P("gx"),
        P("gx", None),
        P(None, "gx", "gy", None),
        P("gx", "gy", None),
        P(None, "gy", None, "gx"),
        P("gx", "gy", None, None),
        P("gx", "gy", None, None),
        P(),
        P(),
        P(),
    )
    return jax.shard_map(
        per_device, mesh=mesh, in_specs=placed, out_specs=P("gy", "gx"), check_vma=False
    )
```

profile of v0, /device:TPU:1, one launch (start us, length us, event | category | flops | bytes accessed | tf_op | source)
XLA Modules:
  0.0 425.0 jit_solution(1710121038791396708)
XLA Ops:
  6.5 0.7 compare_select_fusion.3
  7.2 0.6 scatter_custom_fusion
  7.9 0.7 convert_element_type.98
  8.6 23.0 %all_gather.9 = bf16[2048,128]{1,0:T(8,128)(2,1)S(1)} all-gather(bf16[128,128]{1,0:T(8,128)(2,1)} %param.13), channel_id=1, replica_groups=mesh['gx'=16,'gy'=16] {'gy'}, dimensions={0}, use_global_device_ids=true | all-gather | bytes 557056 | tf_op jit(solution)/shard_map/all_gather | solution.py:46
  31.5 0.6 gather_fusion.1
  32.2 0.4 fusion.24
  32.6 2.6 convolution_bitcast_fusion.2
  35.3 0.0 reduce-scatter.9.cloned.1.call-update
  35.3 0.0 reduce-scatter.7.cloned.1.call-start
  35.4 4.5 %convolution_bitcast_fusion.1 = f32[2048,8,1,128]{3,0,1,2:T(8,128)} fusion(bf16[2048,128,1]{1,0,2:T(8,128)(2,1)S(1)} %bitcast.115, bf16[8,128,1,128]{3,1,2,0:T(8,128)(2,1)S(1)} %copy-done), kind=kOutput, calls=%fused_computation.25 | convolution fusion | flops 536870912 | bytes 9175040 | tf_op jit(solution)/shard_map/td,edhk->tehk/dot_general | solution.py:62
  39.8 0.0 reduce-scatter.7.cloned.1.call-update
  39.9 0.0 reduce-scatter.5.cloned.1.call-start
  39.9 0.1 broadcast_bitcast_fusion
  40.0 0.3 bitcast_select_fusion
  40.3 0.9 fusion.29
  41.2 0.0 reduce-scatter.5.cloned.1.call-update
  41.2 0.0 all-gather.2.cloned.1.call-start
  41.3 0.6 dynamic-slice.4
  42.6 0.6 dynamic-slice.5
  43.8 0.1 dynamic-slice.8
  43.9 0.6 gather_fusion
  44.5 0.1 copy.43
  44.7 34.2 %all-reduce = f32[2048]{0:T(1024)S(1)} all-reduce(f32[2048]{0:T(1024)S(1)} %bitcast.128), channel_id=3, replica_groups=mesh['gx'=16,'gy'=16] {'gx'}, use_global_device_ids=true, to_apply=%region_3.4.clone | all-reduce | flops 2048 | bytes 16384
  79.0 0.6 dynamic-slice.6
  80.2 0.1 fusion.44
  80.3 0.1 mul.177
  80.3 0.2 mul.178
  80.5 31.2 %reduce-scatter.9.cloned.1.call-done = f32[128,1,256]{2,0,1:T(8,128)} async-done(((f32[2048,1,256]{2,0,1:T(8,128)}), f32[128,1,256]{2,0,1:T(8,128)}) %reduce-scatter.9.cloned.1.call-update) | async-done | bytes 131088 | tf_op jit(solution)/shard_map/reduce_scatter | solution.py:72
  111.7 1.0 fusion.38
  112.7 93.2 %reduce-scatter.7.cloned.1.call-done = f32[128,8,1,128]{3,0,1,2:T(8,128)} async-done(((f32[2048,8,1,128]{3,0,1,2:T(8,128)}), f32[128,8,1,128]{3,0,1,2:T(8,128)}) %reduce-scatter.7.cloned.1.call-update) | async-done | bytes 524304 | tf_op jit(solution)/shard_map/reduce_scatter | solution.py:71
  205.9 1.3 copy.44
  207.3 0.4 multiply_reduce_fusion
  207.7 0.2 multiply_convert_fusion.3
  207.9 0.1 fusion.34
  208.1 8.9 %while.16 = (s32[]{:T(128)}, f32[1,256]{1,0:T(1,128)S(1)}, f32[1,256]{1,0:T(1,128)S(1)}, f32[1,256,128]{2,1,0:T(8,128)S(1)}, s32[]{:T(128)}, /*index=5*/s32[]{:T...) while((s32[]{:T(128)}, f32[1,256]{1,0:T(1,128)S(1)}, ...), condition=%wide.region_10.11_spmd, body=%wide.region_7.10_spmd.sunk | while | flops 136120832 | bytes 4016315 | solution.py:118
  208.1 1.3 fusion.62
  209.5 0.2 fusion.63
  209.7 1.3 fusion.64
  211.1 1.3 fusion.62
  212.4 0.2 fusion.63
  212.7 1.3 fusion.64
  214.1 1.3 fusion.62
  215.4 0.2 fusion.63
  215.6 1.3 fusion.64
  217.0 0.2 fusion.50
  217.3 0.2 fusion.23
  217.5 0.6 reshape_transpose_reshape.3
  218.1 0.0 all-gather.2.cloned.1.call-update
  218.1 0.0 reduce-scatter.11.cloned.1.call-start
  218.2 0.4 copy.41
  218.6 0.1 broadcast_bitcast_fusion.1
  218.7 66.3 %reduce-scatter.5.cloned.1.call-done = f32[128,8]{0,1:T(8,128)} async-done(((f32[2048,8]{0,1:T(8,128)}), f32[128,8]{0,1:T(8,128)}) %reduce-scatter.5.cloned.1.call-update) | async-done | bytes 4112 | tf_op jit(solution)/shard_map/reduce_scatter | solution.py:73
  285.0 0.7 broadcast_multiply_fusion
  285.8 15.3 %all_gather.10 = bf16[2048,2]{0,1:T(2,128)(2,1)S(1)} all-gather(bf16[128,2]{0,1:T(2,128)(2,1)S(1)} %pad_maximum_fusion), channel_id=1, replica_groups=mesh['gx'=16,'gy'=16] {'gx'}, dimensions={0}, use_global_device_ids=true | all-gather | bytes 8704 | tf_op jit(solution)/shard_map/all_gather | solution.py:135
  301.1 0.6 gather_fusion.2
  301.7 0.4 copy.42
  302.0 32.5 %all-gather.2.cloned.1.call-done = bf16[2048,256]{1,0:T(8,128)(2,1)} async-done(((bf16[128,256]{1,0:T(8,128)(2,1)}), bf16[2048,256]{1,0:T(8,128)(2,1)}) %all-gather.2.cloned.1.call-update) | async-done | bytes 1048592 | tf_op jit(solution)/shard_map/all_gather | solution.py:134
  334.5 1.8 gather_fusion.3
  336.4 1.1 gather.40
  337.5 17.2 %fusion.18 = f32[2048,8,128]{2,1,0:T(8,128)S(1)} fusion(bf16[2048,2,128]{2,1,0:T(2,128)(2,1)} %gather.40, pred[2048]{0:T(1024)(128)(4,1)S(1)} %broadcast_bitcast_fusion.1, f32[2048,2]{1,0:T(8,128)S(1)} %copy.42, s32[2048,2]{1,0:T(8,128)S(1)} %copy.41), kind=kOutput, calls=%fused_computation.29 | convolution fusion | flops 50921472 | bytes 9472000 | tf_op jit(solution)/shard_map/tse,tshd->tehd/dot_general | solution.py:148
  354.7 5.6 %fusion.15 = f32[2048,128]{1,0:T(8,128)} fusion(f32[2048,8,128]{2,1,0:T(8,128)S(1)} %fusion.18, bf16[8,1,128,128]{3,2,1,0:T(8,128)(2,1)S(1)} %copy-done.2), kind=kOutput, calls=%fused_computation.28 | convolution fusion | flops 3221225472 | bytes 9699328 | tf_op jit(solution)/shard_map/tehd,ehdo->to/dot_general | solution.py:150
  360.4 0.0 reduce-scatter.11.cloned.1.call-update
  360.4 56.6 %reduce-scatter.11.cloned.1.call-done = f32[128,128]{1,0:T(8,128)} async-done(((f32[2048,128]{1,0:T(8,128)}), f32[128,128]{1,0:T(8,128)}) %reduce-scatter.11.cloned.1.call-update) | async-done | bytes 65552 | tf_op jit(solution)/shard_map/reduce_scatter | solution.py:149
  417.0 1.5 convert_element_type.111
  (46 shorter events, 0.3 us)
Async XLA Ops:
  6.5 28.8 %copy-start = (bf16[8,128,1,128]{3,1,2,0:T(8,128)(2,1)S(1)}, bf16[8,128,1,128]{3,1,2,0:T(8,128)(2,1)}, u32[]{:S(2)}) copy-start(bf16[8,128,1,128]{3,1,2,0:T(8,128)(2,1)} %param.16) | copy-start | bytes 786436
  6.5 105.2 %reduce-scatter.9.cloned.1.call-start = ((), (), s32[]{:S(2)}) async-start(), calls=%async_computation.6 | async-start | bytes 2228224 | tf_op jit(solution)/shard_map/reduce_scatter | solution.py:72
  35.3 170.7 %reduce-scatter.7.cloned.1.call-start = ((), (), s32[]{:S(2)}) async-start(), calls=%async_computation.5 | async-start | bytes 8912896 | tf_op jit(solution)/shard_map/reduce_scatter | solution.py:71
  35.3 5.0 %copy-start.3 = (bf16[128,8]{0,1:T(8,128)(2,1)S(1)}, bf16[128,8]{0,1:T(8,128)(2,1)}, u32[]{:S(2)}) copy-start(bf16[128,8]{0,1:T(8,128)(2,1)} %param.15) | copy-start | bytes 6148
  35.4 7.2 %copy-start.4 = (s32[16]{0:T(128)S(1)}, s32[16]{0:T(128)}, u32[]{:S(2)}) copy-start(s32[16]{0:T(128)} %param.21) | copy-start | bytes 196
  35.4 8.5 %copy-start.1 = (s32[2048,2]{0,1:T(2,128)S(1)}, s32[2048,2]{0,1:T(2,128)}, u32[]{:S(2)}) copy-start(s32[2048,2]{0,1:T(2,128)} %param.23) | copy-start | bytes 49156
  39.8 39.1 %copy-start.6 = (u32[256]{0:T(256)S(1)}, u32[256]{0:T(256)}, u32[]{:S(2)}) copy-start(u32[256]{0:T(256)} %constant.201) | copy-start | bytes 3076
  39.9 245.2 %reduce-scatter.5.cloned.1.call-start = ((), (), s32[]{:S(2)}) async-start(), calls=%async_computation.4 | async-start | bytes 69632 | tf_op jit(solution)/shard_map/reduce_scatter | solution.py:73
  41.2 293.3 %all-gather.2.cloned.1.call-start = ((), (), s32[]{:S(2)}) async-start(), calls=%async_computation.7 | async-start | bytes 1114112 | tf_op jit(solution)/shard_map/all_gather | solution.py:134
  208.1 10.5 %copy-start.5 = (s32[16]{0:T(128)S(1)}, s32[16]{0:T(128)}, u32[]{:S(2)}) copy-start(s32[16]{0:T(128)} %param.22) | copy-start | bytes 196
  218.1 198.9 %reduce-scatter.11.cloned.1.call-start = ((), (), s32[]{:S(2)}) async-start(), calls=%async_computation.8 | async-start | bytes 1114112 | tf_op jit(solution)/shard_map/reduce_scatter | solution.py:149
  337.5 17.2 %copy-start.2 = (bf16[8,1,128,128]{3,2,1,0:T(8,128)(2,1)S(1)}, bf16[8,1,128,128]{3,2,1,0:T(8,128)(2,1)}, u32[]{:S(2)}) copy-start(bf16[8,1,128,128]{3,2,1,0:T(8,128)(2,1)} %param.18) | copy-start | bytes 786436
Sparse Core Ops, SparseCore 0:
  35.4 76.2 reduce-scatter.8
  115.4 90.4 reduce-scatter.6
  209.4 75.5 reduce-scatter.4
  287.3 47.1 all-gather.1
  360.5 56.4 reduce-scatter.10
where the time goes:
time: 428 us; the launch traced here: 425 us
  waiting for transfers between devices  280 us (65%)
  blocking collectives  72.5 us (17%)
  matrix products  39.2 us (9%)
  between operations  15.4 us (4%)
  local copies, waits for them, and re-layouts  10.6 us (2%)
  other arithmetic  6.99 us (2%)
    reduce_scatter x1, waiting for transfers between devices, per_device(): lax.psum_scatter(query_part, 'gx', scatter_dimension=0, tiled=True)  93.2 us
    reduce_scatter x1, waiting for transfers between devices, per_device(): lax.psum_scatter(router_part, 'gx', scatter_dimension=0, tiled=True)  66.3 us
    reduce_scatter x1, waiting for transfers between devices, per_device(): lax.psum_scatter(jnp.einsum('tehd,ehdo->to', folded, wide_output, precisi...  56.6 us
    unnamed x1, blocking collectives  34.2 us
    all_gather x1, waiting for transfers between devices, per_device(): lax.all_gather(attended_output, 'gx', axis=0, tiled=True)  32.5 us
    reduce_scatter x1, waiting for transfers between devices, per_device(): lax.psum_scatter(keyval_part, 'gx', scatter_dimension=0, tiled=True)  31.2 us
    all_gather x1, blocking collectives, per_device(): gathered = lax.all_gather(tokens, 'gy', axis=0, tiled=True)  23 us
    dot_general x1, matrix products, per_device(): jnp.einsum('tse,tshd->tehd', mixing, piece, precision=lax.Precision.HIGHEST)  17.2 us
  transfers between devices with their start and end apart: 5, of which 5 were waited for; matrix products, arithmetic and copies ran while one was open for 6% of the time, Pallas kernels for 0%

commit v1 on v0

--- a/solution.py
+++ b/solution.py
@@ -5,12 +5,36 @@
 
 masked_score = -1e30
 norm_eps = 1e-06
+LANES = 128
 
 
 def expert_onehot(route_rows, experts):
     return (route_rows[:, :, None] == jnp.arange(experts, dtype=jnp.int32)[None, None, :]).astype(
         jnp.float32
     )
+
+
+def padded_width(width):
+    return -(-width // LANES) * LANES
+
+
+def scatter_sum(part, axis_name):
+    members = lax.axis_size(axis_name)
+    blocks = lax.all_to_all(
+        part.reshape((members, part.shape[0] // members) + part.shape[1:]),
+        axis_name,
+        0,
+        0,
+        tiled=True,
+    )
+    return jnp.sum(blocks, axis=0)
+
+
+def gather_rows(piece, axis_name):
+    members = lax.axis_size(axis_name)
+    copies = jnp.broadcast_to(piece[None], (members,) + piece.shape)
+    gathered = lax.all_to_all(copies, axis_name, 0, 0, tiled=True)
+    return gathered.reshape((members * piece.shape[0],) + piece.shape[1:])
 
 
 def absorb(carry_state, scores, value_rows):
@@ -55,28 +79,42 @@
     slot_route = jnp.take(route.reshape(requests, new_len, top_count), inverse, axis=0).reshape(
         total_rows, top_count
     )
+    slot_onehot = expert_onehot(slot_route, experts)
     widened = ordered.astype(jnp.float32)
     squares = jnp.sum(widened * widened, axis=1)
     scaled_input = (widened * gain.astype(jnp.float32)[None, :]).astype(jnp.bfloat16)
     router_part = jnp.dot(scaled_input, w_router, preferred_element_type=jnp.float32)
+    chosen_part = jnp.sum(slot_onehot * router_part[:, None, :], axis=2)
+    routed_input = scaled_input[:, None, None, :] * slot_onehot[:, :, :, None].astype(jnp.bfloat16)
     query_part = jnp.einsum(
-        "td,edhk->tehk", scaled_input, expert_query_weight, preferred_element_type=jnp.float32
+        "tsed,edhk->tshk", routed_input, expert_query_weight, preferred_element_type=jnp.float32
     )
     keyval_part = jnp.einsum(
         "td,dhk->thk", scaled_input, key_value_weight, preferred_element_type=jnp.float32
     )
-    my_route = lax.dynamic_slice_in_dim(slot_route, slot_index * new_len, new_len, 0)
-    my_onehot = expert_onehot(my_route, experts)
-    query_all, keyval_sums, router_sums, square_sums = (
-        lax.psum_scatter(query_part, "gx", scatter_dimension=0, tiled=True),
-        lax.psum_scatter(keyval_part, "gx", scatter_dimension=0, tiled=True),
-        lax.psum_scatter(router_part, "gx", scatter_dimension=0, tiled=True),
-        lax.psum_scatter(squares, "gx", scatter_dimension=0, tiled=True),
-    )
-    query_totals = jnp.sum(my_onehot[:, :, :, None, None] * query_all[:, None], axis=2)
+    query_cols = top_count * heads_local * head_dim
+    keyval_cols = heads_local * 2 * head_dim
+    small_cols = top_count + 1
+    packed_cols = query_cols + keyval_cols + padded_width(small_cols)
+    packed = jnp.concatenate(
+        [
+            query_part.reshape(total_rows, query_cols),
+            keyval_part.reshape(total_rows, keyval_cols),
+            chosen_part,
+            squares[:, None],
+            jnp.zeros((total_rows, padded_width(small_cols) - small_cols), jnp.float32),
+        ],
+        axis=1,
+    )
+    summed = scatter_sum(packed, "gx")
+    query_totals = summed[:, :query_cols].reshape(new_len, top_count, heads_local, head_dim)
+    keyval_sums = summed[:, query_cols : query_cols + keyval_cols].reshape(
+        new_len, heads_local, 2 * head_dim
+    )
+    chosen_sums = summed[:, query_cols + keyval_cols : query_cols + keyval_cols + top_count]
+    square_sums = summed[:, query_cols + keyval_cols + top_count]
     inverse_root_mean = lax.rsqrt(square_sums / full_width + norm_eps)
-    logits = router_sums * inverse_root_mean[:, None]
-    chosen = jnp.sum(my_onehot * logits[:, None, :], axis=2)
+    chosen = chosen_sums * inverse_root_mean[:, None]
     gate_gap = chosen[:, 0] - chosen[:, 1]
     gate_weights = jnp.stack([jax.nn.sigmoid(gate_gap), jax.nn.sigmoid(-gate_gap)], axis=1).astype(
         jnp.bfloat16
@@ -129,29 +167,30 @@
     attended_output = (accumulated / running_sum[:, :, None]).astype(jnp.bfloat16)
     attended_output = jnp.transpose(
         attended_output.reshape(heads_local, new_len, top_count, head_dim), (1, 2, 0, 3)
-    ).reshape(new_len, top_count * heads_local * head_dim)
-    all_attended, all_gates = (
-        lax.all_gather(attended_output, "gx", axis=0, tiled=True),
-        lax.all_gather(gate_weights, "gx", axis=0, tiled=True),
-    )
-    token_attended = jnp.take(
-        all_attended.reshape(requests, new_len, top_count * heads_local * head_dim), deal, axis=0
-    ).reshape(total_rows, top_count, heads_local, head_dim)
-    token_gates = (
-        jnp.take(all_gates.reshape(requests, new_len, top_count), deal, axis=0)
-        .reshape(total_rows, top_count)
-        .astype(jnp.float32)
-    )
-    wide_output = expert_output_weight.astype(jnp.float32)
-    piece = token_attended.astype(jnp.float32)
-    mixing = expert_onehot(route, experts) * token_gates[:, :, None]
-    folded = jnp.einsum("tse,tshd->tehd", mixing, piece, precision=lax.Precision.HIGHEST)
-    output_sum = lax.psum_scatter(
-        jnp.einsum("tehd,ehdo->to", folded, wide_output, precision=lax.Precision.HIGHEST),
-        "gy",
-        scatter_dimension=0,
-        tiled=True,
-    )
+    ).reshape(new_len, query_cols)
+    shipped = jnp.concatenate(
+        [
+            attended_output,
+            gate_weights,
+            jnp.zeros((new_len, padded_width(top_count) - top_count), jnp.bfloat16),
+        ],
+        axis=1,
+    )
+    all_shipped = gather_rows(shipped, "gx")
+    by_request = jnp.take(
+        all_shipped.reshape(requests, new_len, all_shipped.shape[1]), deal, axis=0
+    ).reshape(total_rows, all_shipped.shape[1])
+    token_attended = by_request[:, :query_cols].reshape(total_rows, top_count, heads_local, head_dim)
+    token_gates = by_request[:, query_cols : query_cols + top_count].astype(jnp.float32)
+    onehot = expert_onehot(route, experts)
+    routed_attended = token_attended[:, :, None, :, :] * onehot[:, :, :, None, None].astype(
+        jnp.bfloat16
+    )
+    projected = jnp.einsum(
+        "tsehk,ehko->tso", routed_attended, expert_output_weight, preferred_element_type=jnp.float32
+    )
+    mixed_part = jnp.sum(token_gates[:, :, None] * projected, axis=1)
+    output_sum = scatter_sum(mixed_part, "gy")
     return output_sum.astype(jnp.bfloat16)
 
 

time: 428 us -> 227 us (0.53)
  waiting for transfers between devices: 280 us -> 91.7 us
  starting transfers between devices: 0.17 us -> 23.8 us
  matrix products: 39.2 us -> 18.5 us
  between operations: 15.4 us -> 1.64 us
  blocking collectives: 72.5 us -> 58.9 us
  local copies, waits for them, and re-layouts: 10.6 us -> 21.8 us
    reduce_scatter x4 -> x0, waiting for transfers between devices: 247 us -> none  [the longest x1 93.2 us: per_device(): lax.psum_scatter(query_part, 'gx', scatter_dimension=0, tiled=True)]
    all_to_all x0 -> x2, waiting for transfers between devices: none -> 91.7 us  [the longest x1 71.2 us: scatter_sum(): lax.all_to_all(part.reshape((members, part.shape[0] // members) + part.sh...]
    all_to_all x0 -> x1, blocking collectives: none -> 35.9 us  [scatter_sum(): lax.all_to_all(part.reshape((members, part.shape[0] // members) + part.sh...]
    unnamed x1 -> x0, blocking collectives: 34.2 us -> none
    all_gather x1 -> x0, waiting for transfers between devices: 32.5 us -> none  [per_device(): lax.all_gather(attended_output, 'gx', axis=0, tiled=True)]
    all_to_all x0 -> x2, starting transfers between devices: none -> 23.8 us  [the longest x1 16.9 us: gather_rows(): gathered = lax.all_to_all(copies, axis_name, 0, 0, tiled=True)]
    all_gather x1 -> x0, blocking collectives: 15.3 us -> none  [per_device(): lax.all_gather(gate_weights, 'gx', axis=0, tiled=True)]
    dot_general x3 -> x2, matrix products: 27.3 us -> 13.4 us  [the longest x1 7.28 us: per_device(): jnp.einsum('tsed,edhk->tshk', routed_input, expert_query_weight, preferre...]
  transfers between devices with their start and end apart: 5 -> 2, of which waited for: 5 -> 2; matrix products, arithmetic and copies ran while one was open for 6% -> 1% of each run, Pallas kernels for 0% -> 0%
where the time goes in v1:
time: 227 us; the launch traced here: 223 us
  waiting for transfers between devices  91.7 us (40%)
  blocking collectives  58.9 us (26%)
  starting transfers between devices  23.8 us (10%)
  local copies, waits for them, and re-layouts  21.8 us (10%)
  matrix products  18.5 us (8%)
  other arithmetic  6.71 us (3%)
    all_to_all x1, waiting for transfers between devices, scatter_sum(): lax.all_to_all(part.reshape((members, part.shape[0] // members) + part.sh...  71.2 us
    all_to_all x1, blocking collectives, scatter_sum(): lax.all_to_all(part.reshape((members, part.shape[0] // members) + part.sh...  35.9 us
    all_gather x1, blocking collectives, per_device(): gathered = lax.all_gather(tokens, 'gy', axis=0, tiled=True)  23 us
    all_to_all x1, waiting for transfers between devices, gather_rows(): gathered = lax.all_to_all(copies, axis_name, 0, 0, tiled=True)  20.6 us
    all_to_all x1, starting transfers between devices, gather_rows(): gathered = lax.all_to_all(copies, axis_name, 0, 0, tiled=True)  16.9 us
    concatenate x3, local copies, waits for them, and re-layouts, per_device(): jnp.concatenate([query_part.reshape(total_rows, query_cols), keyval_part....  11.1 us
    dot_general x1, matrix products, per_device(): jnp.einsum('tsed,edhk->tshk', routed_input, expert_query_weight, preferre...  7.28 us
    all_to_all x1, starting transfers between devices, scatter_sum(): lax.all_to_all(part.reshape((members, part.shape[0] // members) + part.sh...  6.93 us
  transfers between devices with their start and end apart: 2, of which 2 were waited for; matrix products, arithmetic and copies ran while one was open for 1% of the time, Pallas kernels for 0%

profile of v1, /device:TPU:1, one launch (start us, length us, event | category | flops | bytes accessed | tf_op | source)
XLA Modules:
  0.0 223.2 jit_solution(9612935956510603218)
XLA Ops:
  0.0 0.0 copy-start
  0.0 0.7 compare_select_fusion.1
  0.7 0.6 scatter_custom_fusion
  1.4 23.0 %all_gather.3 = bf16[2048,128]{1,0:T(8,128)(2,1)S(1)} all-gather(bf16[128,128]{1,0:T(8,128)(2,1)} %param.13), channel_id=1, replica_groups=mesh['gx'=16,'gy'=16] {'gy'}, dimensions={0}, use_global_device_ids=true | all-gather | bytes 557056 | tf_op jit(solution)/shard_map/all_gather | solution.py:70
  24.4 0.1 broadcast_bitcast_fusion
  24.4 0.7 convert_element_type.105
  25.1 0.6 gather_fusion
  25.8 0.0 copy-done.1
  25.8 0.6 gather_fusion.1
  26.4 0.4 fusion.35
  26.8 0.3 multiply_convert_fusion
  27.2 0.0 copy-done
  27.2 7.3 %fusion.15 = f32[2048,2,128,1]{0,2,3,1:T(8,128)S(1)} fusion(bf16[2048,2,8]{0,2,1:T(8,128)(2,1)S(1)} %convert_convert_fusion.1, bf16[2048,128]{1,0:T(8,128)(2,1)S(1)} %multiply_convert_fusion, bf16[8,128,1,128]{3,1,2,0:T(8,128)(2,1)S(1)} %copy-done), kind=kOutput, calls=%fused_computation.24 | convolution fusion | flops 1077936128 | bytes 2949120 | tf_op jit(solution)/shard_map/tsed,edhk->tshk/dot_general | solution.py:89
  34.5 0.4 copy.73
  34.9 0.0 copy-start.4
  34.9 0.0 copy-start.3
  34.9 1.9 copy.61
  36.8 0.0 copy-done.4
  36.8 0.2 fusion.56
  37.0 0.1 select_reduce_fusion
  37.1 1.4 copy.60
  38.5 0.0 copy-done.3
  38.5 1.9 fusion.36
  40.3 1.4 copy.62
  41.8 1.1 broadcast_in_dim.131
  42.8 0.0 copy-done.2
  42.8 7.7 %concatenate.17 = f32[16,128,640]{2,1,0:T(8,128)} concatenate(f32[16,128,256]{2,1,0:T(8,128)S(1)} %copy-done.2, f32[16,128,256]{2,1,0:T(8,128)} %fusion.36, f32[16,128,2]{2,1,0:T(8,128)} %bitcast.114, f32[16,128,1]{2,1,0:T(8,128)} %copy.62, f32[16,128,125]{2,1,0:T(8,128)} %broadcast_in_dim.131), dimensions={2} | concatenate | bytes 10485760 | tf_op jit(solution)/shard_map/concatenate | solution.py:99
  50.6 6.9 %all-to-all-start = ((f32[16,128,640]{2,1,0:T(8,128)}), f32[16,128,640]{2,1,0:T(8,128)}, u32[]{:S(2)}, u32[]{:S(2)}) async-start(f32[16,128,640]{2,1,0:T(8,128)} %concatenate.17), calls=%async_computation | async-start | bytes 10485760 | tf_op jit(solution)/shard_map/all_to_all | solution.py:23
  57.5 0.6 dynamic-slice.4
  58.8 0.0 copy-done.6
  58.9 0.6 dynamic-slice.5
  60.0 0.1 pad.7.clone
  60.1 71.2 %all-to-all-done = f32[16,128,640]{2,1,0:T(8,128)} async-done(((f32[16,128,640]{2,1,0:T(8,128)}), f32[16,128,640]{2,1,0:T(8,128)}, u32[]{:S(2)}, u32[]{:S(2)}) %all-to-all-start) | async-done | bytes 5242912 | tf_op jit(solution)/shard_map/all_to_all | solution.py:23
  131.3 2.8 %reduce_sum.69 = f32[128,640]{1,0:T(8,128)S(1)} reduce(f32[16,128,640]{2,1,0:T(8,128)} %all-to-all-done, f32[]{:T(128)} %constant.121.clone.1), dimensions={0}, to_apply=%region_3.4 | reduce | flops 1228800 | bytes 5570564 | tf_op jit(solution)/shard_map/reduce_sum | solution.py:30
  134.0 0.2 fusion.48
  134.2 0.1 fusion.45
  134.4 0.1 mul.165.clone
  134.4 0.1 mul.166
  134.6 0.1 multiply_convert_fusion.2
  134.7 3.0 %while.16 = (s32[]{:T(128)}, f32[1,256]{1,0:T(1,128)S(1)}, f32[1,256]{1,0:T(1,128)S(1)}, f32[1,256,128]{2,1,0:T(8,128)S(1)}, s32[]{:T(128)}, /*index=5*/s32[]{:T...) while((s32[]{:T(128)}, f32[1,256]{1,0:T(1,128)S(1)}, ...), condition=%wide.region_7.8_spmd, body=%wide.region_4.7_spmd.sunk | while | flops 136120832 | bytes 4016315 | solution.py:156
  134.8 1.3 fusion.67
  136.1 0.2 fusion.68
  136.3 1.3 fusion.69
  137.7 0.2 fusion.55
  138.0 0.2 fusion.33
  138.2 0.1 copy.72
  138.3 0.1 copy.65
  138.5 0.1 copy.66
  138.6 0.1 maximum_maximum_fusion
  138.7 0.0 copy-start.7
  138.7 1.4 broadcast_in_dim.134
  140.1 16.9 %all-to-all-start.1 = ((bf16[16,128,384]{2,1,0:T(8,128)(2,1)}), bf16[16,128,384]{2,1,0:T(8,128)(2,1)S(1)}, u32[]{:S(2)}, u32[]{:S(2)}) async-start(bf16[16,128,384]{2,1,0:T(8,128)(2,1)} %broadcast_in_dim.134), calls=%async_computation.1 | async-start | bytes 3145728 | tf_op jit(solution)/shard_map/all_to_all | solution.py:36
  157.1 0.1 broadcast_bitcast_fusion.1
  157.1 20.6 %all-to-all-done.1 = bf16[16,128,384]{2,1,0:T(8,128)(2,1)S(1)} async-done(((bf16[16,128,384]{2,1,0:T(8,128)(2,1)}), bf16[16,128,384]{2,1,0:T(8,128)(2,1)S(1)}, u32[]{:S(2)}, u32[]{:S(2)}) %all-to-all-start.1) | async-done | bytes 1572896 | tf_op jit(solution)/shard_map/all_to_all | solution.py:36
  177.7 0.9 gather_fusion.2
  178.6 0.8 copy.67
  179.4 0.2 broadcast_select_fusion
  179.5 0.0 copy-start.5
  179.6 0.1 slice.63
  179.7 0.7 copy.68
  180.3 0.1 copy-done.5
  180.5 6.1 %fusion.27 = f32[2048,128]{1,0:T(8,128)S(1)} fusion(bf16[2048,2,8]{0,2,1:T(8,128)(2,1)S(1)} %convert_convert_fusion, bf16[2048,2,128]{2,0,1:T(8,128)(2,1)S(1)} %copy.68, f32[2048,2]{0,1:T(2,128)S(1)} %slice_convert_fusion, bf16[8,1,128,128]{3,2,1,0:T(8,128)(2,1)S(1)} %copy-done.5), kind=kOutput, calls=%fused_computation.33 | convolution fusion | flops 1078722560 | bytes 2441216 | tf_op jit(solution)/shard_map/tsehk,ehko->tso/dot_general | solution.py:189
  186.6 35.9 %all_to_all.15 = f32[16,128,128]{2,1,0:T(8,128)S(1)} all-to-all(f32[16,128,128]{2,1,0:T(8,128)S(1)} %bitcast.120), channel_id=1, replica_groups=mesh['gx'=16,'gy'=16] {'gy'}, dimensions={0} | all-to-all | bytes 2097152 | tf_op jit(solution)/shard_map/all_to_all | solution.py:23
  222.5 0.7 reduce_sum.73
  (32 shorter events, 0.3 us)
Async XLA Ops:
  0.0 27.2 %copy-start = (bf16[8,128,1,128]{3,1,2,0:T(8,128)(2,1)S(1)}, bf16[8,128,1,128]{3,1,2,0:T(8,128)(2,1)}, u32[]{:S(2)}) copy-start(bf16[8,128,1,128]{3,1,2,0:T(8,128)(2,1)} %param.16) | copy-start | bytes 786436
  0.0 25.8 %copy-start.1 = (s32[2048,2]{0,1:T(2,128)S(1)}, s32[2048,2]{0,1:T(2,128)}, u32[]{:S(2)}) copy-start(s32[2048,2]{0,1:T(2,128)} %param.23) | copy-start | bytes 49156
  34.9 1.9 copy-start.4
  34.9 3.6 %copy-start.3 = (bf16[128,1,256]{2,0,1:T(8,128)(2,1)S(1)}, bf16[128,1,256]{2,0,1:T(8,128)(2,1)}, u32[]{:S(2)}) copy-start(bf16[128,1,256]{2,0,1:T(8,128)(2,1)} %param.17) | copy-start | bytes 196612
  38.5 4.4 %copy-start.2 = (f32[16,128,256]{2,1,0:T(8,128)S(1)}, f32[16,128,256]{2,1,0:T(8,128)}, u32[]{:S(2)}) copy-start(f32[16,128,256]{2,1,0:T(8,128)} %copy.61) | copy-start | bytes 6291460
  50.6 8.3 %copy-start.6 = (s32[16]{0:T(128)S(1)}, s32[16]{0:T(128)}, u32[]{:S(2)}) copy-start(s32[16]{0:T(128)} %param.21) | copy-start | bytes 196
  50.6 80.7 %all-to-all-start = ((f32[16,128,640]{2,1,0:T(8,128)}), f32[16,128,640]{2,1,0:T(8,128)}, u32[]{:S(2)}, u32[]{:S(2)}) async-start(f32[16,128,640]{2,1,0:T(8,128)} %concatenate.17), calls=%async_computation | async-start | bytes 10485760 | tf_op jit(solution)/shard_map/all_to_all | solution.py:23
  138.7 18.3 %copy-start.7 = (s32[16]{0:T(128)S(1)}, s32[16]{0:T(128)}, u32[]{:S(2)}) copy-start(s32[16]{0:T(128)} %param.22) | copy-start | bytes 196
  140.1 37.6 %all-to-all-start.1 = ((bf16[16,128,384]{2,1,0:T(8,128)(2,1)}), bf16[16,128,384]{2,1,0:T(8,128)(2,1)S(1)}, u32[]{:S(2)}, u32[]{:S(2)}) async-start(bf16[16,128,384]{2,1,0:T(8,128)(2,1)} %broadcast_in_dim.134), calls=%async_computation.1 | async-start | bytes 3145728 | tf_op jit(solution)/shard_map/all_to_all | solution.py:36
  179.5 1.0 copy-start.5

commit v2 on v1

--- a/solution.py
+++ b/solution.py
@@ -1,6 +1,8 @@
 import jax
 import jax.numpy as jnp
 from jax import lax
+from jax.experimental import pallas as pl
+from jax.experimental.pallas import tpu as pltpu
 from jax.sharding import PartitionSpec as P
 
 masked_score = -1e30
@@ -35,6 +37,68 @@
     copies = jnp.broadcast_to(piece[None], (members,) + piece.shape)
     gathered = lax.all_to_all(copies, axis_name, 0, 0, tiled=True)
     return gathered.reshape((members * piece.shape[0],) + piece.shape[1:])
+
+
+def pack_kernel(order_ref, tok_ref, gain_ref, router_ref, query_ref, keyval_ref, route_ref, out_ref):
+    rows, width = tok_ref.shape
+    experts = query_ref.shape[0]
+    head_dim = query_ref.shape[2]
+    keyval_cols = keyval_ref.shape[1]
+    widened = tok_ref[...].astype(jnp.float32)
+    squares = jnp.sum(widened * widened, axis=1, keepdims=True)
+    scaled = (widened * gain_ref[...].astype(jnp.float32)).astype(jnp.bfloat16)
+    logits = jnp.dot(scaled, router_ref[...], preferred_element_type=jnp.float32)
+    first = route_ref[:, 0:1]
+    second = route_ref[:, 1:2]
+    expert_lane = lax.broadcasted_iota(jnp.int32, logits.shape, 1)
+    chosen_first = jnp.sum(jnp.where(expert_lane == first, logits, 0.0), axis=1, keepdims=True)
+    chosen_second = jnp.sum(jnp.where(expert_lane == second, logits, 0.0), axis=1, keepdims=True)
+    query_first = jnp.zeros((rows, head_dim), jnp.float32)
+    query_second = jnp.zeros((rows, head_dim), jnp.float32)
+    for expert in range(experts):
+        projected = jnp.dot(scaled, query_ref[expert], preferred_element_type=jnp.float32)
+        query_first = query_first + jnp.where(first == expert, projected, 0.0)
+        query_second = query_second + jnp.where(second == expert, projected, 0.0)
+    keyval = jnp.dot(scaled, keyval_ref[...], preferred_element_type=jnp.float32)
+    lane = lax.broadcasted_iota(jnp.int32, (rows, LANES), 1)
+    small = jnp.where(
+        lane == 0,
+        chosen_first,
+        jnp.where(lane == 1, chosen_second, jnp.where(lane == 2, squares, 0.0)),
+    )
+    out_ref[:, 0:head_dim] = query_first
+    out_ref[:, head_dim : 2 * head_dim] = query_second
+    out_ref[:, 2 * head_dim : 2 * head_dim + keyval_cols] = keyval
+    out_ref[:, 2 * head_dim + keyval_cols :] = small
+
+
+def packed_partials(order, gathered, gain, w_router, query_weight, keyval_weight, route):
+    total_rows, width = gathered.shape
+    requests = order.shape[0]
+    rows = total_rows // requests
+    experts, _, head_dim = query_weight.shape
+    keyval_cols = keyval_weight.shape[1]
+    packed_cols = 2 * head_dim + keyval_cols + LANES
+    flops = 2 * total_rows * width * (experts * head_dim + keyval_cols + w_router.shape[1])
+    moved = 2 * total_rows * width + 4 * total_rows * packed_cols + 2 * query_weight.size
+    return pl.pallas_call(
+        pack_kernel,
+        out_shape=jax.ShapeDtypeStruct((total_rows, packed_cols), jnp.float32),
+        grid_spec=pltpu.PrefetchScalarGridSpec(
+            num_scalar_prefetch=1,
+            grid=(requests,),
+            in_specs=[
+                pl.BlockSpec((rows, width), lambda s, order_ref: (order_ref[s], 0)),
+                pl.BlockSpec((1, width), lambda s, order_ref: (0, 0)),
+                pl.BlockSpec(w_router.shape, lambda s, order_ref: (0, 0)),
+                pl.BlockSpec(query_weight.shape, lambda s, order_ref: (0, 0, 0)),
+                pl.BlockSpec(keyval_weight.shape, lambda s, order_ref: (0, 0)),
+                pl.BlockSpec((rows, route.shape[1]), lambda s, order_ref: (order_ref[s], 0)),
+            ],
+            out_specs=pl.BlockSpec((rows, packed_cols), lambda s, order_ref: (s, 0)),
+        ),
+        cost_estimate=pl.CostEstimate(flops=flops, transcendentals=0, bytes_accessed=moved),
+    )(order, gathered, gain.reshape(1, width), w_router, query_weight, keyval_weight, route)
 
 
 def absorb(carry_state, scores, value_rows):
@@ -73,39 +137,18 @@
     full_width = local_width * lax.axis_size("gx")
     slot_index = lax.axis_index("gx")
     inverse = jnp.zeros((requests,), jnp.int32).at[deal].set(jnp.arange(requests, dtype=jnp.int32))
-    ordered = jnp.take(gathered.reshape(requests, new_len, local_width), inverse, axis=0).reshape(
-        total_rows, local_width
-    )
-    slot_route = jnp.take(route.reshape(requests, new_len, top_count), inverse, axis=0).reshape(
-        total_rows, top_count
-    )
-    slot_onehot = expert_onehot(slot_route, experts)
-    widened = ordered.astype(jnp.float32)
-    squares = jnp.sum(widened * widened, axis=1)
-    scaled_input = (widened * gain.astype(jnp.float32)[None, :]).astype(jnp.bfloat16)
-    router_part = jnp.dot(scaled_input, w_router, preferred_element_type=jnp.float32)
-    chosen_part = jnp.sum(slot_onehot * router_part[:, None, :], axis=2)
-    routed_input = scaled_input[:, None, None, :] * slot_onehot[:, :, :, None].astype(jnp.bfloat16)
-    query_part = jnp.einsum(
-        "tsed,edhk->tshk", routed_input, expert_query_weight, preferred_element_type=jnp.float32
-    )
-    keyval_part = jnp.einsum(
-        "td,dhk->thk", scaled_input, key_value_weight, preferred_element_type=jnp.float32
+    assert heads_local == 1
+    packed = packed_partials(
+        inverse,
+        gathered,
+        gain,
+        w_router,
+        expert_query_weight.reshape(experts, local_width, head_dim),
+        key_value_weight.reshape(local_width, 2 * head_dim),
+        route,
     )
     query_cols = top_count * heads_local * head_dim
     keyval_cols = heads_local * 2 * head_dim
-    small_cols = top_count + 1
-    packed_cols = query_cols + keyval_cols + padded_width(small_cols)
-    packed = jnp.concatenate(
-        [
-            query_part.reshape(total_rows, query_cols),
-            keyval_part.reshape(total_rows, keyval_cols),
-            chosen_part,
-            squares[:, None],
-            jnp.zeros((total_rows, padded_width(small_cols) - small_cols), jnp.float32),
-        ],
-        axis=1,
-    )
     summed = scatter_sum(packed, "gx")
     query_totals = summed[:, :query_cols].reshape(new_len, top_count, heads_local, head_dim)
     keyval_sums = summed[:, query_cols : query_cols + keyval_cols].reshape(
@@ -168,20 +211,27 @@
     attended_output = jnp.transpose(
         attended_output.reshape(heads_local, new_len, top_count, head_dim), (1, 2, 0, 3)
     ).reshape(new_len, query_cols)
+    gate_row = jnp.transpose(gate_weights).reshape(1, top_count * new_len)
+    assert gate_row.shape[1] <= query_cols
+    extra_rows = 8
     shipped = jnp.concatenate(
         [
             attended_output,
-            gate_weights,
-            jnp.zeros((new_len, padded_width(top_count) - top_count), jnp.bfloat16),
+            jnp.pad(gate_row, ((0, extra_rows - 1), (0, query_cols - gate_row.shape[1]))),
         ],
-        axis=1,
-    )
-    all_shipped = gather_rows(shipped, "gx")
-    by_request = jnp.take(
-        all_shipped.reshape(requests, new_len, all_shipped.shape[1]), deal, axis=0
-    ).reshape(total_rows, all_shipped.shape[1])
-    token_attended = by_request[:, :query_cols].reshape(total_rows, top_count, heads_local, head_dim)
-    token_gates = by_request[:, query_cols : query_cols + top_count].astype(jnp.float32)
+        axis=0,
+    )
+    all_shipped = gather_rows(shipped, "gx").reshape(requests, new_len + extra_rows, query_cols)
+    by_request = jnp.take(all_shipped, deal, axis=0)
+    token_attended = by_request[:, :new_len].reshape(total_rows, top_count, heads_local, head_dim)
+    token_gates = (
+        jnp.transpose(
+            by_request[:, new_len, : top_count * new_len].reshape(requests, top_count, new_len),
+            (0, 2, 1),
+        )
+        .reshape(total_rows, top_count)
+        .astype(jnp.float32)
+    )
     onehot = expert_onehot(route, experts)
     routed_attended = token_attended[:, :, None, :, :] * onehot[:, :, :, None, None].astype(
         jnp.bfloat16

time: 227 us -> 217 us (0.956); the launches traced: 223 us -> 215 us
  Pallas kernels: 0 us -> 14.9 us
  local copies, waits for them, and re-layouts: 21.8 us -> 8.12 us
  matrix products: 18.5 us -> 11.8 us
  waiting for transfers between devices: 91.7 us -> 87.1 us
  starting transfers between devices: 23.8 us -> 26.9 us
    pallas_call x0 -> x1, Pallas kernels: none -> 14.9 us  [packed_partials(): pl.pallas_call(pack_kernel, out_shape=jax.ShapeDtypeStruct((total_rows, p...]
    concatenate x4 -> x0, local copies, waits for them, and re-layouts: 11.1 us -> none  [the longest x3 11.1 us: per_device(): jnp.concatenate([query_part.reshape(total_rows, query_cols), keyval_part....]
    dot_general x3 -> x0, matrix products: 9.36 us -> none  [the longest x1 7.28 us: per_device(): jnp.einsum('tsed,edhk->tshk', routed_input, expert_query_weight, preferre...]
    all_to_all x1, waiting for transfers between devices: 20.6 us -> 15.9 us  [gather_rows(): gathered = lax.all_to_all(copies, axis_name, 0, 0, tiled=True)]
    all_to_all x1, starting transfers between devices: 16.9 us -> 20 us  [gather_rows(): gathered = lax.all_to_all(copies, axis_name, 0, 0, tiled=True)]
    unnamed x18, local copies, waits for them, and re-layouts: 0.63 us -> 2.93 us
where the time goes in v2:
time: 217 us; the launch traced here: 215 us
  waiting for transfers between devices  87.1 us (40%)
  blocking collectives  59.5 us (27%)
  starting transfers between devices  26.9 us (12%)
  Pallas kernels  14.9 us (7%)
  matrix products  11.8 us (5%)
  local copies, waits for them, and re-layouts  8.12 us (4%)
  other arithmetic  5.36 us (2%)
    all_to_all x1, waiting for transfers between devices, scatter_sum(): lax.all_to_all(part.reshape((members, part.shape[0] // members) + part.sh...  71.2 us
    all_to_all x1, blocking collectives, scatter_sum(): lax.all_to_all(part.reshape((members, part.shape[0] // members) + part.sh...  35.1 us
    all_gather x1, blocking collectives, per_device(): gathered = lax.all_gather(tokens, 'gy', axis=0, tiled=True)  24.4 us
    all_to_all x1, starting transfers between devices, gather_rows(): gathered = lax.all_to_all(copies, axis_name, 0, 0, tiled=True)  20 us
    all_to_all x1, waiting for transfers between devices, gather_rows(): gathered = lax.all_to_all(copies, axis_name, 0, 0, tiled=True)  15.9 us
    pallas_call x1, Pallas kernels, packed_partials(): pl.pallas_call(pack_kernel, out_shape=jax.ShapeDtypeStruct((total_rows, p...  14.9 us
    all_to_all x1, starting transfers between devices, scatter_sum(): lax.all_to_all(part.reshape((members, part.shape[0] // members) + part.sh...  6.95 us
    dot_general x1, matrix products, per_device(): jnp.einsum('tsehk,ehko->tso', routed_attended, expert_output_weight, pref...  6.08 us
  transfers between devices with their start and end apart: 2, of which 2 were waited for; matrix products, arithmetic and copies ran while one was open for 1% of the time, Pallas kernels for 0%

profile of v2, /device:TPU:1, one launch (start us, length us, event | category | flops | bytes accessed | tf_op | source)
XLA Modules:
  0.0 215.4 jit_solution(9238688267403717240)
XLA Ops:
  0.0 0.0 copy-start
  0.0 0.0 copy-start.3
  0.0 0.7 compare_select_fusion
  0.7 2.1 copy.44.route_ref
  2.8 24.4 %all_gather.3.tok_ref = bf16[2048,128]{1,0:T(8,128)(2,1)} all-gather(bf16[128,128]{1,0:T(8,128)(2,1)} %param.13), channel_id=1, replica_groups=mesh['gx'=16,'gy'=16] {'gy'}, dimensions={0}, use_global_device_ids=true | all-gather | bytes 557056 | tf_op jit(solution)/shard_map/all_gather | solution.py:134
  27.2 0.0 copy-done.3
  27.2 0.7 copy.43.router_ref
  27.9 1.2 scatter_custom_fusion.order_ref
  29.1 14.9 %shard_map.109 = f32[2048,640]{1,0:T(8,128)} custom-call(s32[16]{0:T(128)} %scatter_custom_fusion.order_ref, bf16[2048,128]{1,0:T(8,128)(2,1)} %all_gather.3.tok_ref, bf16[1,128]{1,0:T(2,128)(2,1)} %bitcast.114, bf16[128,8]{1,0:T(8,128)(2,1)} %copy.43.router_ref, bf16[8,128,128]{2,1,0:T(8,128)(2,1)} %bitcast.101, bf16[128,256]{1,0:T(8,128)(2,1)} %bitcast.105, ...), custom_call_target="tpu_custom_call" | custom-call | flops 675282944 | bytes 6029312 | tf_op jit(solution)/shard_map/pallas_call | solution.py:84
  44.0 0.0 copy-start.4
  44.0 0.0 copy-start.5
  44.0 6.9 %all-to-all-start = ((f32[16,128,640]{2,1,0:T(8,128)}), f32[16,128,640]{2,1,0:T(8,128)}, u32[]{:S(2)}, u32[]{:S(2)}) async-start(f32[16,128,640]{2,1,0:T(8,128)} %bitcast.95), calls=%async_computation | async-start | bytes 10485760 | tf_op jit(solution)/shard_map/all_to_all | solution.py:25
  51.0 0.0 copy-done.4
  51.0 0.7 dynamic-slice.4
  52.3 0.0 copy-done.5
  52.4 0.6 dynamic-slice.5
  53.5 71.2 %all-to-all-done = f32[16,128,640]{2,1,0:T(8,128)} async-done(((f32[16,128,640]{2,1,0:T(8,128)}), f32[16,128,640]{2,1,0:T(8,128)}, u32[]{:S(2)}, u32[]{:S(2)}) %all-to-all-start) | async-done | bytes 5242912 | tf_op jit(solution)/shard_map/all_to_all | solution.py:25
  124.7 2.8 %reduce_sum.49 = f32[128,640]{1,0:T(8,128)S(1)} reduce(f32[16,128,640]{2,1,0:T(8,128)} %all-to-all-done, f32[]{:T(128)} %constant.95.clone.1), dimensions={0}, to_apply=%region_1.0 | reduce | flops 1228800 | bytes 5570564 | tf_op jit(solution)/shard_map/reduce_sum | solution.py:32
  127.5 0.0 copy-start.1
  127.5 0.2 fusion.40
  127.7 0.1 fusion.37
  127.8 0.1 mul.107.clone
  127.9 0.1 mul.108
  128.0 0.1 multiply_convert_fusion.1
  128.2 0.0 copy-done.1
  128.2 5.9 %while.16 = (s32[]{:T(128)}, f32[1,256]{1,0:T(1,128)S(1)}, f32[1,256]{1,0:T(1,128)S(1)}, f32[1,256,128]{2,1,0:T(8,128)S(1)}, s32[]{:T(128)}, /*index=5*/s32[]{:T...) while((s32[]{:T(128)}, f32[1,256]{1,0:T(1,128)S(1)}, ...), condition=%wide.region_5.6_spmd, body=%wide.region_2.5_spmd.sunk | while | flops 136120832 | bytes 4016315 | solution.py:199
  128.2 1.3 fusion.54
  129.6 0.2 fusion.55
  129.8 1.3 fusion.56
  131.2 1.3 fusion.54
  132.5 0.2 fusion.55
  132.8 1.3 fusion.56
  134.2 0.0 slice-start
  134.2 0.2 fusion.45
  134.5 0.2 fusion.29
  134.7 0.3 slice-done
  135.0 0.1 copy.52
  135.1 1.1 broadcast_in_dim.75
  136.2 0.0 copy-start.6
  136.2 0.0 copy-start.2
  136.2 20.0 %all-to-all-start.1 = ((bf16[16,136,256]{2,1,0:T(8,128)(2,1)}), bf16[16,136,256]{2,1,0:T(8,128)(2,1)S(1)}, u32[]{:S(2)}, u32[]{:S(2)}) async-start(bf16[16,136,256]{2,1,0:T(8,128)(2,1)} %broadcast_in_dim.75), calls=%async_computation.1 | async-start | bytes 2228224 | tf_op jit(solution)/shard_map/all_to_all | solution.py:38
  156.2 0.0 copy-done.6
  156.3 0.0 copy-done.2
  156.3 15.9 %all-to-all-done.1 = bf16[16,136,256]{2,1,0:T(8,128)(2,1)S(1)} async-done(((bf16[16,136,256]{2,1,0:T(8,128)(2,1)}), bf16[16,136,256]{2,1,0:T(8,128)(2,1)S(1)}, u32[]{:S(2)}, u32[]{:S(2)}) %all-to-all-start.1) | async-done | bytes 1114144 | tf_op jit(solution)/shard_map/all_to_all | solution.py:38
  172.2 0.6 gather_fusion
  172.8 0.2 broadcast_select_fusion
  173.0 0.1 slice.59
  173.1 0.3 reshape.290
  173.4 0.1 copy.48
  173.6 0.0 copy-done
  173.6 6.1 %fusion.23 = f32[2048,128]{1,0:T(8,128)S(1)} fusion(bf16[2048,2,8]{0,2,1:T(8,128)(2,1)S(1)} %convert_convert_fusion, bf16[2048,2,128]{2,0,1:T(8,128)(2,1)S(1)} %copy.48, f32[2048,2]{0,1:T(2,128)S(1)} %bitcast.106, bf16[8,1,128,128]{3,2,1,0:T(8,128)(2,1)S(1)} %copy-done), kind=kOutput, calls=%fused_computation.26 | convolution fusion | flops 1078722560 | bytes 2441216 | tf_op jit(solution)/shard_map/tsehk,ehko->tso/dot_general | solution.py:239
  179.7 35.1 %all_to_all.15 = f32[16,128,128]{2,1,0:T(8,128)S(1)} all-to-all(f32[16,128,128]{2,1,0:T(8,128)S(1)} %bitcast.98), channel_id=1, replica_groups=mesh['gx'=16,'gy'=16] {'gy'}, dimensions={0} | all-to-all | bytes 2097152 | tf_op jit(solution)/shard_map/all_to_all | solution.py:25
  214.8 0.7 reduce_sum.53
  (28 shorter events, 0.3 us)
Async XLA Ops:
  0.0 173.6 %copy-start = (bf16[8,1,128,128]{3,2,1,0:T(8,128)(2,1)S(1)}, bf16[8,1,128,128]{3,2,1,0:T(8,128)(2,1)}, u32[]{:S(2)}) copy-start(bf16[8,1,128,128]{3,2,1,0:T(8,128)(2,1)} %param.18) | copy-start | bytes 786436
  0.0 27.2 %copy-start.3 = (bf16[128,8]{0,1:T(8,128)(2,1)S(1)}, bf16[128,8]{0,1:T(8,128)(2,1)}, u32[]{:S(2)}) copy-start(bf16[128,8]{0,1:T(8,128)(2,1)} %param.15) | copy-start | bytes 6148
  44.0 7.0 %copy-start.4 = (s32[16]{0:T(128)S(1)}, s32[16]{0:T(128)}, u32[]{:S(2)}) copy-start(s32[16]{0:T(128)} %scatter_custom_fusion.order_ref) | copy-start | bytes 196
  44.0 8.3 %copy-start.5 = (s32[16]{0:T(128)S(1)}, s32[16]{0:T(128)}, u32[]{:S(2)}) copy-start(s32[16]{0:T(128)} %param.21) | copy-start | bytes 196
  44.0 80.7 %all-to-all-start = ((f32[16,128,640]{2,1,0:T(8,128)}), f32[16,128,640]{2,1,0:T(8,128)}, u32[]{:S(2)}, u32[]{:S(2)}) async-start(f32[16,128,640]{2,1,0:T(8,128)} %bitcast.95), calls=%async_computation | async-start | bytes 10485760 | tf_op jit(solution)/shard_map/all_to_all | solution.py:25
  127.5 0.7 copy-start.1
  134.2 0.8 slice-start
  136.2 20.0 %copy-start.6 = (s32[16]{0:T(128)S(1)}, s32[16]{0:T(128)}, u32[]{:S(2)}) copy-start(s32[16]{0:T(128)} %param.22) | copy-start | bytes 196
  136.2 20.1 %copy-start.2 = (s32[2048,2]{0,1:T(2,128)S(1)}, s32[2048,2]{0,1:T(2,128)}, u32[]{:S(2)}) copy-start(s32[2048,2]{0,1:T(2,128)} %param.23) | copy-start | bytes 49156
  136.2 36.0 %all-to-all-start.1 = ((bf16[16,136,256]{2,1,0:T(8,128)(2,1)}), bf16[16,136,256]{2,1,0:T(8,128)(2,1)S(1)}, u32[]{:S(2)}, u32[]{:S(2)}) async-start(bf16[16,136,256]{2,1,0:T(8,128)(2,1)} %broadcast_in_dim.75), calls=%async_computation.1 | async-start | bytes 2228224 | tf_op jit(solution)/shard_map/all_to_all | solution.py:38

commit v3 on v2

--- a/solution.py
+++ b/solution.py
@@ -3,7 +3,7 @@
 from jax import lax
 from jax.experimental import pallas as pl
 from jax.experimental.pallas import tpu as pltpu
-from jax.sharding import PartitionSpec as P
+from jax.sharding import Mesh, PartitionSpec as P
 
 masked_score = -1e30
 norm_eps = 1e-06
@@ -39,20 +39,18 @@
     return gathered.reshape((members * piece.shape[0],) + piece.shape[1:])
 
 
-def pack_kernel(order_ref, tok_ref, gain_ref, router_ref, query_ref, keyval_ref, route_ref, out_ref):
-    rows, width = tok_ref.shape
+def pack_kernel(
+    order_ref, tok_ref, gain_ref, router_ref, query_ref, keyval_ref, route_ref, route_t_ref, out_ref
+):
+    width = tok_ref.shape[1]
+    rows = tok_ref.shape[0]
     experts = query_ref.shape[0]
     head_dim = query_ref.shape[2]
     keyval_cols = keyval_ref.shape[1]
     widened = tok_ref[...].astype(jnp.float32)
-    squares = jnp.sum(widened * widened, axis=1, keepdims=True)
     scaled = (widened * gain_ref[...].astype(jnp.float32)).astype(jnp.bfloat16)
-    logits = jnp.dot(scaled, router_ref[...], preferred_element_type=jnp.float32)
     first = route_ref[:, 0:1]
     second = route_ref[:, 1:2]
-    expert_lane = lax.broadcasted_iota(jnp.int32, logits.shape, 1)
-    chosen_first = jnp.sum(jnp.where(expert_lane == first, logits, 0.0), axis=1, keepdims=True)
-    chosen_second = jnp.sum(jnp.where(expert_lane == second, logits, 0.0), axis=1, keepdims=True)
     query_first = jnp.zeros((rows, head_dim), jnp.float32)
     query_second = jnp.zeros((rows, head_dim), jnp.float32)
     for expert in range(experts):
@@ -60,16 +58,26 @@
         query_first = query_first + jnp.where(first == expert, projected, 0.0)
         query_second = query_second + jnp.where(second == expert, projected, 0.0)
     keyval = jnp.dot(scaled, keyval_ref[...], preferred_element_type=jnp.float32)
-    lane = lax.broadcasted_iota(jnp.int32, (rows, LANES), 1)
-    small = jnp.where(
-        lane == 0,
-        chosen_first,
-        jnp.where(lane == 1, chosen_second, jnp.where(lane == 2, squares, 0.0)),
-    )
-    out_ref[:, 0:head_dim] = query_first
-    out_ref[:, head_dim : 2 * head_dim] = query_second
-    out_ref[:, 2 * head_dim : 2 * head_dim + keyval_cols] = keyval
-    out_ref[:, 2 * head_dim + keyval_cols :] = small
+    out_ref[0:rows, 0:head_dim] = query_first
+    out_ref[0:rows, head_dim : 2 * head_dim] = query_second
+    out_ref[0:rows, 2 * head_dim : 2 * head_dim + keyval_cols] = keyval
+    widened_t = jnp.transpose(widened)
+    squares_row = jnp.sum(widened_t * widened_t, axis=0, keepdims=True)
+    logits_t = lax.dot_general(
+        router_ref[...], scaled, (((1,), (1,)), ((), ())), preferred_element_type=jnp.float32
+    )
+    expert_row = lax.broadcasted_iota(jnp.int32, logits_t.shape, 0)
+    route_t = route_t_ref[...]
+    chosen_first = jnp.sum(jnp.where(expert_row == route_t[0:1, :], logits_t, 0.0), axis=0, keepdims=True)
+    chosen_second = jnp.sum(jnp.where(expert_row == route_t[1:2, :], logits_t, 0.0), axis=0, keepdims=True)
+    extra = out_ref.shape[0] - rows
+    out_ref[rows:, :] = jnp.zeros((extra, out_ref.shape[1]), jnp.float32)
+    out_ref[rows : rows + 1, 0:rows] = chosen_first
+    out_ref[rows : rows + 1, rows : 2 * rows] = chosen_second
+    out_ref[rows : rows + 1, 2 * rows : 3 * rows] = squares_row
+
+
+EXTRA_ROWS = 8
 
 
 def packed_partials(order, gathered, gain, w_router, query_weight, keyval_weight, route):
@@ -78,27 +86,30 @@
     rows = total_rows // requests
     experts, _, head_dim = query_weight.shape
     keyval_cols = keyval_weight.shape[1]
-    packed_cols = 2 * head_dim + keyval_cols + LANES
+    packed_cols = 2 * head_dim + keyval_cols
+    assert 3 * rows <= packed_cols
+    block_rows = rows + EXTRA_ROWS
     flops = 2 * total_rows * width * (experts * head_dim + keyval_cols + w_router.shape[1])
-    moved = 2 * total_rows * width + 4 * total_rows * packed_cols + 2 * query_weight.size
+    moved = 2 * total_rows * width + 4 * requests * block_rows * packed_cols + 2 * query_weight.size
     return pl.pallas_call(
         pack_kernel,
-        out_shape=jax.ShapeDtypeStruct((total_rows, packed_cols), jnp.float32),
+        out_shape=jax.ShapeDtypeStruct((requests * block_rows, packed_cols), jnp.float32),
         grid_spec=pltpu.PrefetchScalarGridSpec(
             num_scalar_prefetch=1,
             grid=(requests,),
             in_specs=[
                 pl.BlockSpec((rows, width), lambda s, order_ref: (order_ref[s], 0)),
                 pl.BlockSpec((1, width), lambda s, order_ref: (0, 0)),
-                pl.BlockSpec(w_router.shape, lambda s, order_ref: (0, 0)),
+                pl.BlockSpec((w_router.shape[1], width), lambda s, order_ref: (0, 0)),
                 pl.BlockSpec(query_weight.shape, lambda s, order_ref: (0, 0, 0)),
                 pl.BlockSpec(keyval_weight.shape, lambda s, order_ref: (0, 0)),
                 pl.BlockSpec((rows, route.shape[1]), lambda s, order_ref: (order_ref[s], 0)),
+                pl.BlockSpec((route.shape[1], rows), lambda s, order_ref: (0, order_ref[s])),
             ],
-            out_specs=pl.BlockSpec((rows, packed_cols), lambda s, order_ref: (s, 0)),
+            out_specs=pl.BlockSpec((block_rows, packed_cols), lambda s, order_ref: (s, 0)),
         ),
         cost_estimate=pl.CostEstimate(flops=flops, transcendentals=0, bytes_accessed=moved),
-    )(order, gathered, gain.reshape(1, width), w_router, query_weight, keyval_weight, route)
+    )(order, gathered, gain.reshape(1, width), jnp.transpose(w_router), query_weight, keyval_weight, route, jnp.transpose(route))
 
 
 def absorb(carry_state, scores, value_rows):
@@ -131,7 +142,7 @@
     heads_local = expert_query_weight.shape[2]
     head_dim = expert_query_weight.shape[3]
     top_count = route.shape[1]
-    gathered = lax.all_gather(tokens, "gy", axis=0, tiled=True)
+    gathered = lax.all_gather(tokens, TOKEN_AXES, axis=0, tiled=True)
     total_rows, local_width = gathered.shape
     new_len = total_rows // requests
     full_width = local_width * lax.axis_size("gx")
@@ -150,12 +161,12 @@
     query_cols = top_count * heads_local * head_dim
     keyval_cols = heads_local * 2 * head_dim
     summed = scatter_sum(packed, "gx")
-    query_totals = summed[:, :query_cols].reshape(new_len, top_count, heads_local, head_dim)
-    keyval_sums = summed[:, query_cols : query_cols + keyval_cols].reshape(
+    query_totals = summed[:new_len, :query_cols].reshape(new_len, top_count, heads_local, head_dim)
+    keyval_sums = summed[:new_len, query_cols : query_cols + keyval_cols].reshape(
         new_len, heads_local, 2 * head_dim
     )
-    chosen_sums = summed[:, query_cols + keyval_cols : query_cols + keyval_cols + top_count]
-    square_sums = summed[:, query_cols + keyval_cols + top_count]
+    chosen_sums = jnp.transpose(summed[new_len, : top_count * new_len].reshape(top_count, new_len))
+    square_sums = summed[new_len, top_count * new_len : (top_count + 1) * new_len]
     inverse_root_mean = lax.rsqrt(square_sums / full_width + norm_eps)
     chosen = chosen_sums * inverse_root_mean[:, None]
     gate_gap = chosen[:, 0] - chosen[:, 1]
@@ -222,7 +233,13 @@
         axis=0,
     )
     all_shipped = gather_rows(shipped, "gx").reshape(requests, new_len + extra_rows, query_cols)
-    by_request = jnp.take(all_shipped, deal, axis=0)
+    cores = lax.axis_size("cc")
+    chips = lax.axis_size("zz")
+    staged = jnp.arange(requests, dtype=jnp.int32).reshape(chips, cores).T.reshape(requests)
+    by_request = jnp.take(all_shipped, jnp.take(deal, staged), axis=0)
+    route = jnp.take(route.reshape(requests, new_len, top_count), staged, axis=0).reshape(
+        total_rows, top_count
+    )
     token_attended = by_request[:, :new_len].reshape(total_rows, top_count, heads_local, head_dim)
     token_gates = (
         jnp.transpose(
@@ -240,24 +257,30 @@
         "tsehk,ehko->tso", routed_attended, expert_output_weight, preferred_element_type=jnp.float32
     )
     mixed_part = jnp.sum(token_gates[:, :, None] * projected, axis=1)
-    output_sum = scatter_sum(mixed_part, "gy")
+    output_sum = scatter_sum(scatter_sum(mixed_part, "cc"), "zz")
     return output_sum.astype(jnp.bfloat16)
 
 
+TOKEN_AXES = ("zz", "cc")
+
+
 def solution(mesh):
+    gx_size, gy_size = mesh.devices.shape
+    staged_mesh = Mesh(mesh.devices.reshape(gx_size, gy_size // 2, 2), ("gx",) + TOKEN_AXES)
+    gy = TOKEN_AXES
     placed = (
-        P("gy", "gx"),
+        P(gy, "gx"),
         P("gx"),
         P("gx", None),
-        P(None, "gx", "gy", None),
-        P("gx", "gy", None),
-        P(None, "gy", None, "gx"),
-        P("gx", "gy", None, None),
-        P("gx", "gy", None, None),
+        P(None, "gx", gy, None),
+        P("gx", gy, None),
+        P(None, gy, None, "gx"),
+        P("gx", gy, None, None),
+        P("gx", gy, None, None),
         P(),
         P(),
         P(),
     )
     return jax.shard_map(
-        per_device, mesh=mesh, in_specs=placed, out_specs=P("gy", "gx"), check_vma=False
-    )
+        per_device, mesh=staged_mesh, in_specs=placed, out_specs=P(gy, "gx"), check_vma=False
+    )

time: 217 us -> 188 us (0.87)
  waiting for transfers between devices: 87.1 us -> 70.2 us
  blocking collectives: 59.5 us -> 51.7 us
  starting transfers between devices: 26.9 us -> 20.1 us
  matrix products: 11.8 us -> 14.5 us
    all_to_all x1, waiting for transfers between devices: 71.2 us -> 54.9 us  [scatter_sum(): lax.all_to_all(part.reshape((members, part.shape[0] // members) + part.sh...]
    all_to_all x1 -> x2, blocking collectives: 35.1 us -> 27.3 us  [scatter_sum(): lax.all_to_all(part.reshape((members, part.shape[0] // members) + part.sh...]
    all_to_all x1, starting transfers between devices: 20 us -> 13.1 us  [gather_rows(): gathered = lax.all_to_all(copies, axis_name, 0, 0, tiled=True)]
  transfers between devices with their start and end apart: 2 -> 2, of which waited for: 2 -> 2; matrix products, arithmetic and copies ran while one was open for 1% -> 2% of each run, Pallas kernels for 0% -> 0%
where the time goes in v3:
time: 188 us; the launch traced here: 185 us
  waiting for transfers between devices  70.2 us (37%)
  blocking collectives  51.7 us (28%)
  starting transfers between devices  20.1 us (11%)
  matrix products  14.5 us (8%)
  Pallas kernels  13.1 us (7%)
  local copies, waits for them, and re-layouts  8.46 us (5%)
  other arithmetic  5.49 us (3%)
    all_to_all x1, waiting for transfers between devices, scatter_sum(): lax.all_to_all(part.reshape((members, part.shape[0] // members) + part.sh...  54.9 us
    all_to_all x2, blocking collectives, scatter_sum(): lax.all_to_all(part.reshape((members, part.shape[0] // members) + part.sh...  27.3 us
    all_gather x1, blocking collectives, per_device(): gathered = lax.all_gather(tokens, TOKEN_AXES, axis=0, tiled=True)  24.4 us
    all_to_all x1, waiting for transfers between devices, gather_rows(): gathered = lax.all_to_all(copies, axis_name, 0, 0, tiled=True)  15.3 us
    all_to_all x1, starting transfers between devices, gather_rows(): gathered = lax.all_to_all(copies, axis_name, 0, 0, tiled=True)  13.1 us
    pallas_call x1, Pallas kernels, packed_partials(): pl.pallas_call(pack_kernel, out_shape=jax.ShapeDtypeStruct((requests * bl...  13.1 us
    all_to_all x1, starting transfers between devices, scatter_sum(): lax.all_to_all(part.reshape((members, part.shape[0] // members) + part.sh...  6.94 us
    dot_general x1, matrix products, per_device(): jnp.einsum('tsehk,ehko->tso', routed_attended, expert_output_weight, pref...  6.08 us
  transfers between devices with their start and end apart: 2, of which 2 were waited for; matrix products, arithmetic and copies ran while one was open for 2% of the time, Pallas kernels for 0%

profile of v3, /device:TPU:1, one launch (start us, length us, event | category | flops | bytes accessed | tf_op | source)
XLA Modules:
  0.0 185.2 jit_solution(10320801451480052113)
XLA Ops:
  0.0 0.0 copy-start
  0.0 0.7 compare_select_fusion.1
  0.7 2.1 %copy.19.route_ref = s32[2048,2]{1,0:T(8,128)} copy(s32[2048,2]{0,1:T(2,128)} %param.23) | data formatting | bytes 32768 | tf_op args[10]
  2.8 24.4 %all_gather.3.tok_ref = bf16[2048,128]{1,0:T(8,128)(2,1)} all-gather(bf16[128,128]{1,0:T(8,128)(2,1)} %param.13), channel_id=1, replica_groups=mesh['gx'=16,'zz'=8,'cc'=2] {'zz','cc'}, dimensions={0}, use_global_device_ids=true | all-gather | bytes 557056 | tf_op jit(solution)/shard_map/all_gather | solution.py:145
  27.1 1.1 scatter_custom_fusion.order_ref
  28.2 13.1 %shard_map.109 = f32[2176,512]{1,0:T(8,128)} custom-call(s32[16]{0:T(128)} %scatter_custom_fusion.order_ref, bf16[2048,128]{1,0:T(8,128)(2,1)} %all_gather.3.tok_ref, bf16[1,128]{1,0:T(2,128)(2,1)} %bitcast.140, bf16[8,128]{1,0:T(8,128)(2,1)} %bitcast.135, bf16[8,128,128]{2,1,0:T(8,128)(2,1)} %bitcast.125, bf16[128,256]{1,0:T(8,128)(2,1)} %bitcast.129, ...), custom_call_target="tpu_custom_call" | custom-call | flops 675282944 | bytes 5242880 | tf_op jit(solution)/shard_map/pallas_call | solution.py:94
  41.3 0.0 copy-start.3
  41.3 0.0 copy-start.4
  41.3 0.0 copy-start.1
  41.3 6.9 %all-to-all-start = ((f32[16,136,512]{2,1,0:T(8,128)}), f32[16,136,512]{2,1,0:T(8,128)}, u32[]{:S(2)}, u32[]{:S(2)}) async-start(f32[16,136,512]{2,1,0:T(8,128)} %bitcast.118), calls=%async_computation | async-start | bytes 8912896 | tf_op jit(solution)/shard_map/all_to_all | solution.py:25
  48.3 0.0 copy-done.3
  48.3 0.6 dynamic-slice.4
  49.5 0.0 copy-done.4
  49.6 0.6 dynamic-slice.5
  50.8 0.1 reshape.349
  50.9 0.1 reshape.348
  51.0 0.0 copy-done.1
  51.0 0.7 gather_fusion
  51.7 0.1 broadcast_bitcast_fusion
  51.8 54.9 %all-to-all-done = f32[16,136,512]{2,1,0:T(8,128)} async-done(((f32[16,136,512]{2,1,0:T(8,128)}), f32[16,136,512]{2,1,0:T(8,128)}, u32[]{:S(2)}, u32[]{:S(2)}) %all-to-all-start) | async-done | bytes 4456480 | tf_op jit(solution)/shard_map/all_to_all | solution.py:25
  106.7 2.7 %reduce_sum.58 = f32[136,512]{1,0:T(8,128)S(1)} reduce(f32[16,136,512]{2,1,0:T(8,128)} %all-to-all-done, f32[]{:T(128)} %constant.122.clone.1), dimensions={0}, to_apply=%region_1.0 | reduce | flops 1044480 | bytes 4734980 | tf_op jit(solution)/shard_map/reduce_sum | solution.py:32
  109.4 0.1 fusion.37
  109.6 0.1 mul.112
  109.6 0.1 mul.113
  109.8 0.1 multiply_convert_fusion.1
  109.9 8.9 %while.16 = (s32[]{:T(128)}, f32[1,256]{1,0:T(1,128)S(1)}, f32[1,256]{1,0:T(1,128)S(1)}, f32[1,256,128]{2,1,0:T(8,128)S(1)}, s32[]{:T(128)}, /*index=5*/s32[]{:T...) while((s32[]{:T(128)}, f32[1,256]{1,0:T(1,128)S(1)}, ...), condition=%wide.region_5.6_spmd, body=%wide.region_2.5_spmd.sunk | while | flops 136120832 | bytes 4016315 | solution.py:210
  110.0 1.3 fusion.56
  111.3 0.2 fusion.57
  111.5 1.3 fusion.58
  112.9 1.3 fusion.56
  114.3 0.2 fusion.57
  114.5 1.3 fusion.58
  115.9 1.3 fusion.56
  117.2 0.2 fusion.57
  117.5 1.3 fusion.58
  118.9 0.2 fusion.47
  119.1 0.2 fusion.29
  119.5 1.1 broadcast_in_dim.90
  120.5 0.0 copy-start.2
  120.5 13.1 %all-to-all-start.1 = ((bf16[16,136,256]{2,1,0:T(8,128)(2,1)}), bf16[16,136,256]{2,1,0:T(8,128)(2,1)S(1)}, u32[]{:S(2)}, u32[]{:S(2)}) async-start(bf16[16,136,256]{2,1,0:T(8,128)(2,1)} %broadcast_in_dim.90), calls=%async_computation.1 | async-start | bytes 2228224 | tf_op jit(solution)/shard_map/all_to_all | solution.py:38
  133.7 0.0 copy-done.2
  133.7 0.6 gather_fusion.2
  134.3 15.3 %all-to-all-done.1 = bf16[16,136,256]{2,1,0:T(8,128)(2,1)S(1)} async-done(((bf16[16,136,256]{2,1,0:T(8,128)(2,1)}), bf16[16,136,256]{2,1,0:T(8,128)(2,1)S(1)}, u32[]{:S(2)}, u32[]{:S(2)}) %all-to-all-start.1) | async-done | bytes 1114144 | tf_op jit(solution)/shard_map/all_to_all | solution.py:38
  149.7 0.6 gather_fusion.1
  150.3 0.2 broadcast_select_fusion
  150.5 0.1 slice.63
  150.6 0.3 reshape.457
  150.9 0.1 copy.21
  151.0 0.0 copy-done
  151.0 6.1 %fusion.23 = f32[2048,128]{1,0:T(8,128)S(1)} fusion(bf16[2048,2,8]{0,2,1:T(8,128)(2,1)S(1)} %convert_convert_fusion, bf16[2048,2,128]{2,0,1:T(8,128)(2,1)S(1)} %copy.21, f32[2048,2]{0,1:T(2,128)S(1)} %bitcast.130, bf16[8,1,128,128]{3,2,1,0:T(8,128)(2,1)S(1)} %copy-done), kind=kOutput, calls=%fused_computation.28 | convolution fusion | flops 1078722560 | bytes 2441216 | tf_op jit(solution)/shard_map/tsehk,ehko->tso/dot_general | solution.py:256
  157.1 7.4 %all_to_all.20 = f32[2,1024,128]{2,1,0:T(8,128)S(1)} all-to-all(f32[2,1024,128]{2,1,0:T(8,128)S(1)} %bitcast.122), channel_id=1, replica_groups=mesh['gx'=16,'zz'=8,'cc'=2] {'cc'}, dimensions={0} | all-to-all | bytes 2097152 | tf_op jit(solution)/shard_map/all_to_all | solution.py:25
  164.6 0.1 reduce_sum.62
  164.7 19.9 %all_to_all.21 = f32[8,128,128]{2,1,0:T(8,128)S(1)} all-to-all(f32[8,128,128]{2,1,0:T(8,128)S(1)} %bitcast.119), channel_id=1, replica_groups=mesh['gx'=16,'zz'=8,'cc'=2] {'zz'}, dimensions={0} | all-to-all | bytes 1048576 | tf_op jit(solution)/shard_map/all_to_all | solution.py:25
  184.5 0.6 reduce_sum.63
  (39 shorter events, 0.4 us)
Async XLA Ops:
  0.0 151.0 %copy-start = (bf16[8,1,128,128]{3,2,1,0:T(8,128)(2,1)S(1)}, bf16[8,1,128,128]{3,2,1,0:T(8,128)(2,1)}, u32[]{:S(2)}) copy-start(bf16[8,1,128,128]{3,2,1,0:T(8,128)(2,1)} %param.18) | copy-start | bytes 786436
  41.3 7.0 %copy-start.3 = (s32[16]{0:T(128)S(1)}, s32[16]{0:T(128)}, u32[]{:S(2)}) copy-start(s32[16]{0:T(128)} %scatter_custom_fusion.order_ref) | copy-start | bytes 196
  41.3 8.3 %copy-start.4 = (s32[16]{0:T(128)S(1)}, s32[16]{0:T(128)}, u32[]{:S(2)}) copy-start(s32[16]{0:T(128)} %param.21) | copy-start | bytes 196
  41.3 9.7 %copy-start.1 = (s32[16]{0:T(128)S(1)}, s32[16]{0:T(128)}, u32[]{:S(2)}) copy-start(s32[16]{0:T(128)} %param.22) | copy-start | bytes 196
  41.3 65.4 %all-to-all-start = ((f32[16,136,512]{2,1,0:T(8,128)}), f32[16,136,512]{2,1,0:T(8,128)}, u32[]{:S(2)}, u32[]{:S(2)}) async-start(f32[16,136,512]{2,1,0:T(8,128)} %bitcast.118), calls=%async_computation | async-start | bytes 8912896 | tf_op jit(solution)/shard_map/all_to_all | solution.py:25
  120.5 13.1 %copy-start.2 = (s32[2048,2]{0,1:T(2,128)S(1)}, s32[2048,2]{0,1:T(2,128)}, u32[]{:S(2)}) copy-start(s32[2048,2]{0,1:T(2,128)} %param.23) | copy-start | bytes 49156
  120.5 29.1 %all-to-all-start.1 = ((bf16[16,136,256]{2,1,0:T(8,128)(2,1)}), bf16[16,136,256]{2,1,0:T(8,128)(2,1)S(1)}, u32[]{:S(2)}, u32[]{:S(2)}) async-start(bf16[16,136,256]{2,1,0:T(8,128)(2,1)} %broadcast_in_dim.90), calls=%async_computation.1 | async-start | bytes 2228224 | tf_op jit(solution)/shard_map/all_to_all | solution.py:38

commit v4 on v3

--- a/solution.py
+++ b/solution.py
@@ -78,6 +78,60 @@
 
 
 EXTRA_ROWS = 8
+
+
+def attend_kernel(length_ref, query_ref, cache_k_ref, cache_v_ref, fresh_ref, out_ref):
+    rows, head_dim = query_ref.shape
+    fresh_len = fresh_ref.shape[0]
+    top_count = rows // fresh_len
+    score_scale = head_dim ** (-0.5)
+    contract_last = (((1,), (1,)), ((), ()))
+    query = query_ref[...]
+    cached = lax.dot_general(query, cache_k_ref[...], contract_last, preferred_element_type=jnp.float32)
+    cached = cached * score_scale
+    key_col = lax.broadcasted_iota(jnp.int32, cached.shape, 1)
+    cached = jnp.where(key_col < length_ref[0], cached, masked_score)
+    fresh_keys = fresh_ref[:, 0:head_dim]
+    fresh_values = fresh_ref[:, head_dim : 2 * head_dim]
+    fresh = lax.dot_general(query, fresh_keys, contract_last, preferred_element_type=jnp.float32)
+    fresh = fresh * score_scale
+    fresh_col = lax.broadcasted_iota(jnp.int32, fresh.shape, 1)
+    query_token = lax.broadcasted_iota(jnp.int32, fresh.shape, 0) // top_count
+    fresh = jnp.where(fresh_col <= query_token, fresh, masked_score)
+    top = jnp.maximum(
+        jnp.max(cached, axis=1, keepdims=True), jnp.max(fresh, axis=1, keepdims=True)
+    )
+    cached_weights = jnp.exp(cached - top)
+    fresh_weights = jnp.exp(fresh - top)
+    denominator = jnp.sum(cached_weights, axis=1, keepdims=True) + jnp.sum(
+        fresh_weights, axis=1, keepdims=True
+    )
+    summed = jnp.dot(
+        cached_weights.astype(jnp.bfloat16), cache_v_ref[...], preferred_element_type=jnp.float32
+    ) + jnp.dot(fresh_weights.astype(jnp.bfloat16), fresh_values, preferred_element_type=jnp.float32)
+    out_ref[...] = (summed / denominator).astype(jnp.bfloat16)
+
+
+def attend(length, query, cache_k, cache_v, fresh):
+    rows, head_dim = query.shape
+    span = cache_k.shape[0]
+    full = lambda shape: pl.BlockSpec(shape, lambda i, length_ref: (0,) * len(shape))
+    keys = span + fresh.shape[0]
+    return pl.pallas_call(
+        attend_kernel,
+        out_shape=jax.ShapeDtypeStruct((rows, head_dim), jnp.bfloat16),
+        grid_spec=pltpu.PrefetchScalarGridSpec(
+            num_scalar_prefetch=1,
+            grid=(1,),
+            in_specs=[full(query.shape), full(cache_k.shape), full(cache_v.shape), full(fresh.shape)],
+            out_specs=full((rows, head_dim)),
+        ),
+        cost_estimate=pl.CostEstimate(
+            flops=4 * rows * keys * head_dim,
+            transcendentals=rows * keys,
+            bytes_accessed=2 * (2 * span * head_dim + 2 * rows * head_dim + fresh.size),
+        ),
+    )(length.reshape(1), query, cache_k, cache_v, fresh)
 
 
 def packed_partials(order, gathered, gain, w_router, query_weight, keyval_weight, route):
@@ -110,18 +164,6 @@
         ),
         cost_estimate=pl.CostEstimate(flops=flops, transcendentals=0, bytes_accessed=moved),
     )(order, gathered, gain.reshape(1, width), jnp.transpose(w_router), query_weight, keyval_weight, route, jnp.transpose(route))
-
-
-def absorb(carry_state, scores, value_rows):
-    running_max, running_sum, accumulated = carry_state
-    new_max = jnp.maximum(running_max, jnp.max(scores, axis=2))
-    shrink = jnp.exp(running_max - new_max)
-    weights = jnp.exp(scores - new_max[:, :, None])
-    running_sum = running_sum * shrink + jnp.sum(weights, axis=2)
-    accumulated = accumulated * shrink[:, :, None] + jnp.einsum(
-        "hrk,hkd->hrd", weights.astype(jnp.bfloat16), value_rows, preferred_element_type=jnp.float32
-    )
-    return (new_max, running_sum, accumulated)
 
 
 def per_device(
@@ -176,51 +218,13 @@
     query_matrix = (query_totals * inverse_root_mean[:, None, None, None]).astype(jnp.bfloat16)
     key_value_rows = (keyval_sums * inverse_root_mean[:, None, None]).astype(jnp.bfloat16)
     query_rows = new_len * top_count
-    query_by_head = jnp.transpose(query_matrix, (2, 0, 1, 3)).reshape(
-        heads_local, query_rows, head_dim
-    )
-    fresh_keyval = jnp.transpose(key_value_rows, (1, 0, 2))
-    fresh_keys = fresh_keyval[:, :, :head_dim]
-    fresh_values = fresh_keyval[:, :, head_dim:]
     length = jnp.take(lengths, jnp.take(inverse, slot_index))
-    local_keys = cache_keys[0]
-    local_values = cached_value_slots[0]
-    cache_span = local_keys.shape[1]
-    key_block = min(1024, cache_span)
-    score_scale = head_dim ** (-0.5)
-    initial = (
-        jnp.full((heads_local, query_rows), masked_score, jnp.float32),
-        jnp.zeros((heads_local, query_rows), jnp.float32),
-        jnp.zeros((heads_local, query_rows, head_dim), jnp.float32),
-    )
-
-    def visit_block(block_index, carry_state):
-        first_key = block_index * key_block
-        key_rows = lax.dynamic_slice_in_dim(local_keys, first_key, key_block, 1)
-        value_rows = lax.dynamic_slice_in_dim(local_values, first_key, key_block, 1)
-        scores = (
-            jnp.einsum("hrd,hkd->hrk", query_by_head, key_rows, preferred_element_type=jnp.float32)
-            * score_scale
-        )
-        visible = first_key + jnp.arange(key_block, dtype=jnp.int32) < length
-        scores = jnp.where(visible[None, None, :], scores, masked_score)
-        return absorb(carry_state, scores, value_rows)
-
-    block_count = (length + key_block - 1) // key_block
-    carry_state = lax.fori_loop(0, block_count, visit_block, initial)
-    fresh_scores = (
-        jnp.einsum("hrd,hkd->hrk", query_by_head, fresh_keys, preferred_element_type=jnp.float32)
-        * score_scale
-    )
-    causal = (
-        jnp.arange(new_len, dtype=jnp.int32)[None, :]
-        <= (jnp.arange(query_rows, dtype=jnp.int32) // top_count)[:, None]
-    )
-    fresh_scores = jnp.where(causal[None], fresh_scores, masked_score)
-    running_max, running_sum, accumulated = absorb(carry_state, fresh_scores, fresh_values)
-    attended_output = (accumulated / running_sum[:, :, None]).astype(jnp.bfloat16)
-    attended_output = jnp.transpose(
-        attended_output.reshape(heads_local, new_len, top_count, head_dim), (1, 2, 0, 3)
+    attended_output = attend(
+        length,
+        query_matrix.reshape(query_rows, head_dim),
+        cache_keys[0, 0],
+        cached_value_slots[0, 0],
+        key_value_rows.reshape(new_len, 2 * head_dim),
     ).reshape(new_len, query_cols)
     gate_row = jnp.transpose(gate_weights).reshape(1, top_count * new_len)
     assert gate_row.shape[1] <= query_cols

time: 188 us -> 185 us (0.984)
  matrix products: 14.5 us -> 6.08 us
  Pallas kernels: 13.1 us -> 17.5 us
    dot_general x8 -> x0, matrix products: 8.39 us -> none  [the longest x4 4.25 us: absorb(): jnp.einsum('hrk,hkd->hrd', weights.astype(jnp.bfloat16), value_rows, pref...]
    pallas_call x0 -> x1, Pallas kernels: none -> 4.41 us  [attend(): pl.pallas_call(attend_kernel, out_shape=jax.ShapeDtypeStruct((rows, head_...]
where the time goes in v4:
time: 185 us; the launch traced here: 183 us
  waiting for transfers between devices  70.2 us (38%)
  blocking collectives  51.7 us (28%)
  starting transfers between devices  21.4 us (12%)
  Pallas kernels  17.5 us (9%)
  local copies, waits for them, and re-layouts  9.22 us (5%)
  matrix products  6.08 us (3%)
  other arithmetic  5.91 us (3%)
    all_to_all x1, waiting for transfers between devices, scatter_sum(): lax.all_to_all(part.reshape((members, part.shape[0] // members) + part.sh...  54.9 us
    all_to_all x2, blocking collectives, scatter_sum(): lax.all_to_all(part.reshape((members, part.shape[0] // members) + part.sh...  27.3 us
    all_gather x1, blocking collectives, per_device(): gathered = lax.all_gather(tokens, TOKEN_AXES, axis=0, tiled=True)  24.4 us
    all_to_all x1, waiting for transfers between devices, gather_rows(): gathered = lax.all_to_all(copies, axis_name, 0, 0, tiled=True)  15.3 us
    all_to_all x1, starting transfers between devices, gather_rows(): gathered = lax.all_to_all(copies, axis_name, 0, 0, tiled=True)  14.4 us
    pallas_call x1, Pallas kernels, packed_partials(): pl.pallas_call(pack_kernel, out_shape=jax.ShapeDtypeStruct((requests * bl...  13.1 us
    all_to_all x1, starting transfers between devices, scatter_sum(): lax.all_to_all(part.reshape((members, part.shape[0] // members) + part.sh...  6.94 us
    dot_general x1, matrix products, per_device(): jnp.einsum('tsehk,ehko->tso', routed_attended, expert_output_weight, pref...  6.08 us
  transfers between devices with their start and end apart: 2, of which 2 were waited for; matrix products, arithmetic and copies ran while one was open for 2% of the time, Pallas kernels for 0%

profile of v4, /device:TPU:1, one launch (start us, length us, event | category | flops | bytes accessed | tf_op | source)
XLA Modules:
  0.0 183.5 jit_solution(17748803944661671685)
XLA Ops:
  0.0 0.0 copy-start
  0.0 0.7 compare_select_fusion.1
  0.7 2.1 %copy.19.route_ref = s32[2048,2]{1,0:T(8,128)} copy(s32[2048,2]{0,1:T(2,128)} %param.21) | data formatting | bytes 32768 | tf_op args[10]
  2.8 24.4 %all_gather.3.tok_ref = bf16[2048,128]{1,0:T(8,128)(2,1)} all-gather(bf16[128,128]{1,0:T(8,128)(2,1)} %param.11), channel_id=1, replica_groups=mesh['gx'=16,'zz'=8,'cc'=2] {'zz','cc'}, dimensions={0}, use_global_device_ids=true | all-gather | bytes 557056 | tf_op jit(solution)/shard_map/all_gather | solution.py:187
  27.1 1.1 scatter_custom_fusion.order_ref
  28.2 13.1 %shard_map.109 = f32[2176,512]{1,0:T(8,128)} custom-call(s32[16]{0:T(128)} %scatter_custom_fusion.order_ref, bf16[2048,128]{1,0:T(8,128)(2,1)} %all_gather.3.tok_ref, bf16[1,128]{1,0:T(2,128)(2,1)} %bitcast.67, bf16[8,128]{1,0:T(8,128)(2,1)} %bitcast.65, bf16[8,128,128]{2,1,0:T(8,128)(2,1)} %bitcast.61, bf16[128,256]{1,0:T(8,128)(2,1)} %bitcast.62, ...), custom_call_target="tpu_custom_call" | custom-call | flops 675282944 | bytes 5242880 | tf_op jit(solution)/shard_map/pallas_call | solution.py:148
  41.3 0.0 copy-start.3
  41.3 0.0 copy-start.4
  41.3 0.0 copy-start.1
  41.3 6.9 %all-to-all-start = ((f32[16,136,512]{2,1,0:T(8,128)}), f32[16,136,512]{2,1,0:T(8,128)}, u32[]{:S(2)}, u32[]{:S(2)}) async-start(f32[16,136,512]{2,1,0:T(8,128)} %bitcast.56), calls=%async_computation | async-start | bytes 8912896 | tf_op jit(solution)/shard_map/all_to_all | solution.py:25
  48.3 0.0 copy-done.3
  48.3 0.6 dynamic-slice.4
  49.6 0.1 reshape.246
  49.6 0.1 reshape.245
  49.7 0.0 copy-done.4
  49.7 0.6 dynamic-slice.5
  50.4 0.0 copy-done.1
  50.4 0.7 gather_fusion
  51.7 0.1 broadcast_bitcast_fusion
  51.8 54.9 %all-to-all-done = f32[16,136,512]{2,1,0:T(8,128)} async-done(((f32[16,136,512]{2,1,0:T(8,128)}), f32[16,136,512]{2,1,0:T(8,128)}, u32[]{:S(2)}, u32[]{:S(2)}) %all-to-all-start) | async-done | bytes 4456480 | tf_op jit(solution)/shard_map/all_to_all | solution.py:25
  106.7 2.7 %reduce_sum.36 = f32[136,512]{1,0:T(8,128)S(1)} reduce(f32[16,136,512]{2,1,0:T(8,128)} %all-to-all-done, f32[]{:T(128)} %constant.76.clone.1), dimensions={0}, to_apply=%region_1.0 | reduce | flops 1044480 | bytes 4734980 | tf_op jit(solution)/shard_map/reduce_sum | solution.py:32
  109.4 0.7 fusion.15
  110.2 0.1 mul.61
  110.2 0.1 mul.62
  110.4 0.7 multiply_convert_fusion.query_ref
  111.1 4.4 %shard_map.110 = bf16[256,128]{1,0:T(8,128)(2,1)} custom-call(s32[1]{0:T(128)S(6)} %select_n.104.length_ref, bf16[256,128]{1,0:T(8,128)(2,1)} %multiply_convert_fusion.query_ref, bf16[4096,128]{1,0:T(8,128)(2,1)} %bitcast.58, bf16[4096,128]{1,0:T(8,128)(2,1)} %bitcast.59, bf16[128,256]{1,0:T(8,128)(2,1)} %get-tuple-element.29.fresh_ref), custom_call_target="tpu_custom_call" | custom-call | flops 553648128 | bytes 2293760 | tf_op jit(solution)/shard_map/pallas_call | solution.py:120
  115.5 0.9 reshape.253
  116.5 1.1 broadcast_in_dim.52
  117.5 0.0 copy-start.2
  117.5 14.4 %all-to-all-start.1 = ((bf16[16,136,256]{2,1,0:T(8,128)(2,1)}), bf16[16,136,256]{2,1,0:T(8,128)(2,1)S(1)}, u32[]{:S(2)}, u32[]{:S(2)}) async-start(bf16[16,136,256]{2,1,0:T(8,128)(2,1)} %broadcast_in_dim.52), calls=%async_computation.1 | async-start | bytes 2228224 | tf_op jit(solution)/shard_map/all_to_all | solution.py:38
  132.0 0.0 copy-done.2
  132.0 0.6 gather_fusion.2
  132.6 15.3 %all-to-all-done.1 = bf16[16,136,256]{2,1,0:T(8,128)(2,1)S(1)} async-done(((bf16[16,136,256]{2,1,0:T(8,128)(2,1)}), bf16[16,136,256]{2,1,0:T(8,128)(2,1)S(1)}, u32[]{:S(2)}, u32[]{:S(2)}) %all-to-all-start.1) | async-done | bytes 1114144 | tf_op jit(solution)/shard_map/all_to_all | solution.py:38
  147.9 0.6 gather_fusion.1
  148.6 0.2 broadcast_select_fusion
  148.7 0.1 slice.53
  148.9 0.3 reshape.355
  149.2 0.1 copy.21
  149.3 0.0 copy-done
  149.3 6.1 %fusion.10 = f32[2048,128]{1,0:T(8,128)S(1)} fusion(bf16[2048,2,8]{0,2,1:T(8,128)(2,1)S(1)} %convert_convert_fusion, bf16[2048,2,128]{2,0,1:T(8,128)(2,1)S(1)} %copy.21, f32[2048,2]{0,1:T(2,128)S(1)} %bitcast.63, bf16[8,1,128,128]{3,2,1,0:T(8,128)(2,1)S(1)} %copy-done), kind=kOutput, calls=%fused_computation.10 | convolution fusion | flops 1078722560 | bytes 2441216 | tf_op jit(solution)/shard_map/tsehk,ehko->tso/dot_general | solution.py:260
  155.4 7.4 %all_to_all.20 = f32[2,1024,128]{2,1,0:T(8,128)S(1)} all-to-all(f32[2,1024,128]{2,1,0:T(8,128)S(1)} %bitcast.60), channel_id=1, replica_groups=mesh['gx'=16,'zz'=8,'cc'=2] {'cc'}, dimensions={0} | all-to-all | bytes 2097152 | tf_op jit(solution)/shard_map/all_to_all | solution.py:25
  162.8 0.1 reduce_sum.38
  163.0 19.9 %all_to_all.21 = f32[8,128,128]{2,1,0:T(8,128)S(1)} all-to-all(f32[8,128,128]{2,1,0:T(8,128)S(1)} %bitcast.57), channel_id=1, replica_groups=mesh['gx'=16,'zz'=8,'cc'=2] {'zz'}, dimensions={0} | all-to-all | bytes 1048576 | tf_op jit(solution)/shard_map/all_to_all | solution.py:25
  182.8 0.6 reduce_sum.39
  (18 shorter events, 0.1 us)
Async XLA Ops:
  0.0 149.3 %copy-start = (bf16[8,1,128,128]{3,2,1,0:T(8,128)(2,1)S(1)}, bf16[8,1,128,128]{3,2,1,0:T(8,128)(2,1)}, u32[]{:S(2)}) copy-start(bf16[8,1,128,128]{3,2,1,0:T(8,128)(2,1)} %param.16) | copy-start | bytes 786436
  41.3 7.0 %copy-start.3 = (s32[16]{0:T(128)S(1)}, s32[16]{0:T(128)}, u32[]{:S(2)}) copy-start(s32[16]{0:T(128)} %scatter_custom_fusion.order_ref) | copy-start | bytes 196
  41.3 8.4 %copy-start.4 = (s32[16]{0:T(128)S(1)}, s32[16]{0:T(128)}, u32[]{:S(2)}) copy-start(s32[16]{0:T(128)} %param.19) | copy-start | bytes 196
  41.3 9.1 %copy-start.1 = (s32[16]{0:T(128)S(1)}, s32[16]{0:T(128)}, u32[]{:S(2)}) copy-start(s32[16]{0:T(128)} %param.20) | copy-start | bytes 196
  41.3 65.4 %all-to-all-start = ((f32[16,136,512]{2,1,0:T(8,128)}), f32[16,136,512]{2,1,0:T(8,128)}, u32[]{:S(2)}, u32[]{:S(2)}) async-start(f32[16,136,512]{2,1,0:T(8,128)} %bitcast.56), calls=%async_computation | async-start | bytes 8912896 | tf_op jit(solution)/shard_map/all_to_all | solution.py:25
  117.5 14.5 %copy-start.2 = (s32[2048,2]{0,1:T(2,128)S(1)}, s32[2048,2]{0,1:T(2,128)}, u32[]{:S(2)}) copy-start(s32[2048,2]{0,1:T(2,128)} %param.21) | copy-start | bytes 49156
  117.5 30.4 %all-to-all-start.1 = ((bf16[16,136,256]{2,1,0:T(8,128)(2,1)}), bf16[16,136,256]{2,1,0:T(8,128)(2,1)S(1)}, u32[]{:S(2)}, u32[]{:S(2)}) async-start(bf16[16,136,256]{2,1,0:T(8,128)(2,1)} %broadcast_in_dim.52), calls=%async_computation.1 | async-start | bytes 2228224 | tf_op jit(solution)/shard_map/all_to_all | solution.py:38

commit v5 on v4

--- a/solution.py
+++ b/solution.py
@@ -39,45 +39,85 @@
     return gathered.reshape((members * piece.shape[0],) + piece.shape[1:])
 
 
-def pack_kernel(
-    order_ref, tok_ref, gain_ref, router_ref, query_ref, keyval_ref, route_ref, route_t_ref, out_ref
-):
-    width = tok_ref.shape[1]
-    rows = tok_ref.shape[0]
-    experts = query_ref.shape[0]
-    head_dim = query_ref.shape[2]
-    keyval_cols = keyval_ref.shape[1]
+def pack_kernel(tok_ref, gain_ref, router_ref, weight_ref, route_ref, route_t_ref, out_ref):
+    rows = route_t_ref.shape[2]
+    block_rows = rows + EXTRA_ROWS
+    per_step = tok_ref.shape[0] // rows
+    head_dim = out_ref.shape[1] // 4
+    experts = (weight_ref.shape[1] - 2 * head_dim) // head_dim
     widened = tok_ref[...].astype(jnp.float32)
     scaled = (widened * gain_ref[...].astype(jnp.float32)).astype(jnp.bfloat16)
+    projected = jnp.dot(scaled, weight_ref[...], preferred_element_type=jnp.float32)
     first = route_ref[:, 0:1]
     second = route_ref[:, 1:2]
-    query_first = jnp.zeros((rows, head_dim), jnp.float32)
-    query_second = jnp.zeros((rows, head_dim), jnp.float32)
+    query_first = jnp.zeros((tok_ref.shape[0], head_dim), jnp.float32)
+    query_second = jnp.zeros((tok_ref.shape[0], head_dim), jnp.float32)
     for expert in range(experts):
-        projected = jnp.dot(scaled, query_ref[expert], preferred_element_type=jnp.float32)
-        query_first = query_first + jnp.where(first == expert, projected, 0.0)
-        query_second = query_second + jnp.where(second == expert, projected, 0.0)
-    keyval = jnp.dot(scaled, keyval_ref[...], preferred_element_type=jnp.float32)
-    out_ref[0:rows, 0:head_dim] = query_first
-    out_ref[0:rows, head_dim : 2 * head_dim] = query_second
-    out_ref[0:rows, 2 * head_dim : 2 * head_dim + keyval_cols] = keyval
-    widened_t = jnp.transpose(widened)
-    squares_row = jnp.sum(widened_t * widened_t, axis=0, keepdims=True)
-    logits_t = lax.dot_general(
-        router_ref[...], scaled, (((1,), (1,)), ((), ())), preferred_element_type=jnp.float32
-    )
-    expert_row = lax.broadcasted_iota(jnp.int32, logits_t.shape, 0)
-    route_t = route_t_ref[...]
-    chosen_first = jnp.sum(jnp.where(expert_row == route_t[0:1, :], logits_t, 0.0), axis=0, keepdims=True)
-    chosen_second = jnp.sum(jnp.where(expert_row == route_t[1:2, :], logits_t, 0.0), axis=0, keepdims=True)
-    extra = out_ref.shape[0] - rows
-    out_ref[rows:, :] = jnp.zeros((extra, out_ref.shape[1]), jnp.float32)
-    out_ref[rows : rows + 1, 0:rows] = chosen_first
-    out_ref[rows : rows + 1, rows : 2 * rows] = chosen_second
-    out_ref[rows : rows + 1, 2 * rows : 3 * rows] = squares_row
+        part = projected[:, expert * head_dim : (expert + 1) * head_dim]
+        query_first = query_first + jnp.where(first == expert, part, 0.0)
+        query_second = query_second + jnp.where(second == expert, part, 0.0)
+    keyval = projected[:, experts * head_dim :]
+    contract_last = (((1,), (1,)), ((), ()))
+    for block in range(per_step):
+        low = block * rows
+        top = block * block_rows
+        out_ref[top : top + rows, 0:head_dim] = query_first[low : low + rows]
+        out_ref[top : top + rows, head_dim : 2 * head_dim] = query_second[low : low + rows]
+        out_ref[top : top + rows, 2 * head_dim :] = keyval[low : low + rows]
+        widened_t = jnp.transpose(widened[low : low + rows])
+        squares_row = jnp.sum(widened_t * widened_t, axis=0, keepdims=True)
+        logits_t = lax.dot_general(
+            router_ref[...], scaled[low : low + rows], contract_last, preferred_element_type=jnp.float32
+        )
+        expert_row = lax.broadcasted_iota(jnp.int32, logits_t.shape, 0)
+        route_t = route_t_ref[block]
+        chosen_first = jnp.sum(
+            jnp.where(expert_row == route_t[0:1, :], logits_t, 0.0), axis=0, keepdims=True
+        )
+        chosen_second = jnp.sum(
+            jnp.where(expert_row == route_t[1:2, :], logits_t, 0.0), axis=0, keepdims=True
+        )
+        out_ref[top + rows : top + block_rows, :] = jnp.zeros((EXTRA_ROWS, out_ref.shape[1]), jnp.float32)
+        out_ref[top + rows : top + rows + 1, 0:rows] = chosen_first
+        out_ref[top + rows : top + rows + 1, rows : 2 * rows] = chosen_second
+        out_ref[top + rows : top + rows + 1, 2 * rows : 3 * rows] = squares_row
 
 
 EXTRA_ROWS = 8
+REQUESTS_PER_STEP = 4
+
+
+def packed_partials(ordered, gain, w_router, query_weight, keyval_weight, route, requests):
+    total_rows, width = ordered.shape
+    rows = total_rows // requests
+    experts, _, head_dim = query_weight.shape
+    keyval_cols = keyval_weight.shape[1]
+    packed_cols = 2 * head_dim + keyval_cols
+    assert 3 * rows <= packed_cols and keyval_cols == 2 * head_dim
+    block_rows = rows + EXTRA_ROWS
+    step_rows = REQUESTS_PER_STEP * rows
+    weight = jnp.concatenate(
+        [jnp.transpose(query_weight, (1, 0, 2)).reshape(width, experts * head_dim), keyval_weight],
+        axis=1,
+    )
+    route_t = jnp.transpose(route.reshape(requests, rows, route.shape[1]), (0, 2, 1))
+    flops = 2 * total_rows * width * (weight.shape[1] + w_router.shape[1])
+    moved = 2 * total_rows * width + 4 * requests * block_rows * packed_cols + 2 * weight.size
+    return pl.pallas_call(
+        pack_kernel,
+        out_shape=jax.ShapeDtypeStruct((requests * block_rows, packed_cols), jnp.float32),
+        grid=(requests // REQUESTS_PER_STEP,),
+        in_specs=[
+            pl.BlockSpec((step_rows, width), lambda s: (s, 0)),
+            pl.BlockSpec((1, width), lambda s: (0, 0)),
+            pl.BlockSpec((w_router.shape[1], width), lambda s: (0, 0)),
+            pl.BlockSpec(weight.shape, lambda s: (0, 0)),
+            pl.BlockSpec((step_rows, route.shape[1]), lambda s: (s, 0)),
+            pl.BlockSpec((REQUESTS_PER_STEP, route.shape[1], rows), lambda s: (s, 0, 0)),
+        ],
+        out_specs=pl.BlockSpec((REQUESTS_PER_STEP * block_rows, packed_cols), lambda s: (s, 0)),
+        cost_estimate=pl.CostEstimate(flops=flops, transcendentals=0, bytes_accessed=moved),
+    )(ordered, gain.reshape(1, width), jnp.transpose(w_router), weight, route, route_t)
 
 
 def attend_kernel(length_ref, query_ref, cache_k_ref, cache_v_ref, fresh_ref, out_ref):
@@ -132,38 +172,6 @@
             bytes_accessed=2 * (2 * span * head_dim + 2 * rows * head_dim + fresh.size),
         ),
     )(length.reshape(1), query, cache_k, cache_v, fresh)
-
-
-def packed_partials(order, gathered, gain, w_router, query_weight, keyval_weight, route):
-    total_rows, width = gathered.shape
-    requests = order.shape[0]
-    rows = total_rows // requests
-    experts, _, head_dim = query_weight.shape
-    keyval_cols = keyval_weight.shape[1]
-    packed_cols = 2 * head_dim + keyval_cols
-    assert 3 * rows <= packed_cols
-    block_rows = rows + EXTRA_ROWS
-    flops = 2 * total_rows * width * (experts * head_dim + keyval_cols + w_router.shape[1])
-    moved = 2 * total_rows * width + 4 * requests * block_rows * packed_cols + 2 * query_weight.size
-    return pl.pallas_call(
-        pack_kernel,
-        out_shape=jax.ShapeDtypeStruct((requests * block_rows, packed_cols), jnp.float32),
-        grid_spec=pltpu.PrefetchScalarGridSpec(
-            num_scalar_prefetch=1,
-            grid=(requests,),
-            in_specs=[
-                pl.BlockSpec((rows, width), lambda s, order_ref: (order_ref[s], 0)),
-                pl.BlockSpec((1, width), lambda s, order_ref: (0, 0)),
-                pl.BlockSpec((w_router.shape[1], width), lambda s, order_ref: (0, 0)),
-                pl.BlockSpec(query_weight.shape, lambda s, order_ref: (0, 0, 0)),
-                pl.BlockSpec(keyval_weight.shape, lambda s, order_ref: (0, 0)),
-                pl.BlockSpec((rows, route.shape[1]), lambda s, order_ref: (order_ref[s], 0)),
-                pl.BlockSpec((route.shape[1], rows), lambda s, order_ref: (0, order_ref[s])),
-            ],
-            out_specs=pl.BlockSpec((block_rows, packed_cols), lambda s, order_ref: (s, 0)),
-        ),
-        cost_estimate=pl.CostEstimate(flops=flops, transcendentals=0, bytes_accessed=moved),
-    )(order, gathered, gain.reshape(1, width), jnp.transpose(w_router), query_weight, keyval_weight, route, jnp.transpose(route))
 
 
 def per_device(
@@ -191,14 +199,20 @@
     slot_index = lax.axis_index("gx")
     inverse = jnp.zeros((requests,), jnp.int32).at[deal].set(jnp.arange(requests, dtype=jnp.int32))
     assert heads_local == 1
+    ordered = jnp.take(gathered.reshape(requests, new_len, local_width), inverse, axis=0).reshape(
+        total_rows, local_width
+    )
+    slot_route = jnp.take(route.reshape(requests, new_len, top_count), inverse, axis=0).reshape(
+        total_rows, top_count
+    )
     packed = packed_partials(
-        inverse,
-        gathered,
+        ordered,
         gain,
         w_router,
         expert_query_weight.reshape(experts, local_width, head_dim),
         key_value_weight.reshape(local_width, 2 * head_dim),
-        route,
+        slot_route,
+        requests,
     )
     query_cols = top_count * heads_local * head_dim
     keyval_cols = heads_local * 2 * head_dim

time: 185 us -> 180 us (0.973)
  Pallas kernels: 17.5 us -> 11.9 us
  other arithmetic: 5.91 us -> 8.6 us
    pallas_call x1, Pallas kernels: 13.1 us -> 7.45 us  [packed_partials(): pl.pallas_call(pack_kernel, out_shape=jax.ShapeDtypeStruct((requests * bl...]
    unnamed x12 -> x15, local copies, waits for them, and re-layouts: 2.08 us -> 0.03 us
    gather x0 -> x2, local copies, waits for them, and re-layouts: none -> 1.96 us  [the longest x1 1.31 us: per_device(): jnp.take(route.reshape(requests, new_len, top_count), inverse, axis=0)]
where the time goes in v5:
time: 180 us
  waiting for transfers between devices  70.4 us (39%)
  blocking collectives  50 us (28%)
  starting transfers between devices  21.4 us (12%)
  Pallas kernels  11.9 us (7%)
  local copies, waits for them, and re-layouts  9.97 us (6%)
  other arithmetic  8.6 us (5%)
  matrix products  6.08 us (3%)
    all_to_all x1, waiting for transfers between devices, scatter_sum(): lax.all_to_all(part.reshape((members, part.shape[0] // members) + part.sh...  55.2 us
    all_to_all x2, blocking collectives, scatter_sum(): lax.all_to_all(part.reshape((members, part.shape[0] // members) + part.sh...  27.3 us
    all_gather x1, blocking collectives, per_device(): gathered = lax.all_gather(tokens, TOKEN_AXES, axis=0, tiled=True)  22.7 us
    all_to_all x1, waiting for transfers between devices, gather_rows(): gathered = lax.all_to_all(copies, axis_name, 0, 0, tiled=True)  15.2 us
    all_to_all x1, starting transfers between devices, gather_rows(): gathered = lax.all_to_all(copies, axis_name, 0, 0, tiled=True)  14.4 us
    pallas_call x1, Pallas kernels, packed_partials(): pl.pallas_call(pack_kernel, out_shape=jax.ShapeDtypeStruct((requests * bl...  7.45 us
    all_to_all x1, starting transfers between devices, scatter_sum(): lax.all_to_all(part.reshape((members, part.shape[0] // members) + part.sh...  6.94 us
    dot_general x1, matrix products, per_device(): jnp.einsum('tsehk,ehko->tso', routed_attended, expert_output_weight, pref...  6.08 us
  transfers between devices with their start and end apart: 2, of which 2 were waited for; matrix products, arithmetic and copies ran while one was open for 2% of the time, Pallas kernels for 0%

profile of v5, /device:TPU:1, one launch (start us, length us, event | category | flops | bytes accessed | tf_op | source)
XLA Modules:
  0.0 179.8 jit_solution(8336381573313879287)
XLA Ops:
  0.0 0.0 copy-start
  0.0 0.7 compare_select_fusion.2
  0.7 0.6 scatter_custom_fusion
  1.4 0.1 broadcast_bitcast_fusion
  1.4 0.0 copy-start.5
  1.5 1.3 gather_fusion.3
  2.8 0.7 fusion.24
  3.5 0.0 copy-start.3
  3.5 1.4 copy.22.route_ref
  4.8 0.0 copy-done.5
  4.8 22.7 %all_gather.3 = bf16[2048,128]{1,0:T(8,128)(2,1)S(1)} all-gather(bf16[128,128]{1,0:T(8,128)(2,1)S(1)} %copy-done.5), channel_id=1, replica_groups=mesh['gx'=16,'zz'=8,'cc'=2] {'zz','cc'}, dimensions={0}, use_global_device_ids=true | all-gather | bytes 557056 | tf_op jit(solution)/shard_map/all_gather | solution.py:195
  27.5 0.0 copy-start.4
  27.5 0.6 gather_fusion.1
  28.2 0.0 copy-done.3
  28.2 1.2 bitcast_select_fusion.tok_ref
  29.4 0.0 copy-done.4
  29.4 0.7 pad_maximum_fusion.weight_ref
  30.2 7.4 %shard_map.109 = f32[2176,512]{1,0:T(8,128)} custom-call(bf16[2048,128]{1,0:T(8,128)(2,1)} %bitcast_select_fusion.tok_ref, bf16[1,128]{1,0:T(2,128)(2,1)} %bitcast.80, bf16[8,128]{1,0:T(8,128)(2,1)} %bitcast.78, bf16[128,1280]{1,0:T(8,128)(2,1)} %pad_maximum_fusion.weight_ref, s32[2048,2]{1,0:T(8,128)} %copy.22.route_ref, ...), custom_call_target="tpu_custom_call" | custom-call | flops 675282944 | bytes 5308416 | tf_op jit(solution)/shard_map/pallas_call | solution.py:106
  37.6 0.0 copy-start.6
  37.6 0.0 copy-start.1
  37.6 6.9 %all-to-all-start = ((f32[16,136,512]{2,1,0:T(8,128)}), f32[16,136,512]{2,1,0:T(8,128)}, u32[]{:S(2)}, u32[]{:S(2)}) async-start(f32[16,136,512]{2,1,0:T(8,128)} %bitcast.69), calls=%async_computation | async-start | bytes 8912896 | tf_op jit(solution)/shard_map/all_to_all | solution.py:25
  44.6 0.6 dynamic-slice.4
  45.8 0.1 reshape.247
  45.8 0.1 reshape.246
  45.9 0.0 copy-done.6
  45.9 0.6 dynamic-slice.5
  46.5 0.0 copy-done.1
  46.5 0.7 gather_fusion
  47.8 55.2 %all-to-all-done = f32[16,136,512]{2,1,0:T(8,128)} async-done(((f32[16,136,512]{2,1,0:T(8,128)}), f32[16,136,512]{2,1,0:T(8,128)}, u32[]{:S(2)}, u32[]{:S(2)}) %all-to-all-start) | async-done | bytes 4456480 | tf_op jit(solution)/shard_map/all_to_all | solution.py:25
  103.0 2.7 %reduce_sum.36 = f32[136,512]{1,0:T(8,128)S(1)} reduce(f32[16,136,512]{2,1,0:T(8,128)} %all-to-all-done, f32[]{:T(128)} %constant.87.clone.1), dimensions={0}, to_apply=%region_1.0 | reduce | flops 1044480 | bytes 4734980 | tf_op jit(solution)/shard_map/reduce_sum | solution.py:32
  105.7 0.7 fusion.15
  106.5 0.1 mul.61
  106.5 0.1 mul.62
  106.7 0.7 multiply_convert_fusion.query_ref
  107.4 4.4 %shard_map.110 = bf16[256,128]{1,0:T(8,128)(2,1)} custom-call(s32[1]{0:T(128)S(6)} %select_n.108.length_ref, bf16[256,128]{1,0:T(8,128)(2,1)} %multiply_convert_fusion.query_ref, bf16[4096,128]{1,0:T(8,128)(2,1)} %bitcast.72, bf16[4096,128]{1,0:T(8,128)(2,1)} %bitcast.73, bf16[128,256]{1,0:T(8,128)(2,1)} %get-tuple-element.30.fresh_ref), custom_call_target="tpu_custom_call" | custom-call | flops 553648128 | bytes 2293760 | tf_op jit(solution)/shard_map/pallas_call | solution.py:160
  111.8 0.9 reshape.258
  112.8 1.1 broadcast_in_dim.68
  113.8 0.0 copy-start.2
  113.8 14.4 %all-to-all-start.1 = ((bf16[16,136,256]{2,1,0:T(8,128)(2,1)}), bf16[16,136,256]{2,1,0:T(8,128)(2,1)S(1)}, u32[]{:S(2)}, u32[]{:S(2)}) async-start(bf16[16,136,256]{2,1,0:T(8,128)(2,1)} %broadcast_in_dim.68), calls=%async_computation.1 | async-start | bytes 2228224 | tf_op jit(solution)/shard_map/all_to_all | solution.py:38
  128.3 0.0 copy-done.2
  128.3 0.6 gather_fusion.4
  128.9 0.1 select_bitcast_fusion
  129.0 15.2 %all-to-all-done.1 = bf16[16,136,256]{2,1,0:T(8,128)(2,1)S(1)} async-done(((bf16[16,136,256]{2,1,0:T(8,128)(2,1)}), bf16[16,136,256]{2,1,0:T(8,128)(2,1)S(1)}, u32[]{:S(2)}, u32[]{:S(2)}) %all-to-all-start.1) | async-done | bytes 1114144 | tf_op jit(solution)/shard_map/all_to_all | solution.py:38
  144.2 0.6 gather_fusion.2
  144.9 0.2 broadcast_select_fusion
  145.0 0.1 slice.57
  145.2 0.3 reshape.382
  145.5 0.1 copy.24
  145.6 0.0 copy-done
  145.6 6.1 %fusion.10 = f32[2048,128]{1,0:T(8,128)S(1)} fusion(bf16[2048,2,8]{0,2,1:T(8,128)(2,1)S(1)} %convert_convert_fusion, bf16[2048,2,128]{2,0,1:T(8,128)(2,1)S(1)} %copy.24, f32[2048,2]{0,1:T(2,128)S(1)} %bitcast.76, bf16[8,1,128,128]{3,2,1,0:T(8,128)(2,1)S(1)} %copy-done), kind=kOutput, calls=%fused_computation.12 | convolution fusion | flops 1078722560 | bytes 2441216 | tf_op jit(solution)/shard_map/tsehk,ehko->tso/dot_general | solution.py:274
  151.7 7.4 %all_to_all.20 = f32[2,1024,128]{2,1,0:T(8,128)S(1)} all-to-all(f32[2,1024,128]{2,1,0:T(8,128)S(1)} %bitcast.74), channel_id=1, replica_groups=mesh['gx'=16,'zz'=8,'cc'=2] {'cc'}, dimensions={0} | all-to-all | bytes 2097152 | tf_op jit(solution)/shard_map/all_to_all | solution.py:25
  159.1 0.1 reduce_sum.38
  159.2 19.9 %all_to_all.21 = f32[8,128,128]{2,1,0:T(8,128)S(1)} all-to-all(f32[8,128,128]{2,1,0:T(8,128)S(1)} %bitcast.71), channel_id=1, replica_groups=mesh['gx'=16,'zz'=8,'cc'=2] {'zz'}, dimensions={0} | all-to-all | bytes 1048576 | tf_op jit(solution)/shard_map/all_to_all | solution.py:25
  179.1 0.6 reduce_sum.39
  (23 shorter events, 0.2 us)
Async XLA Ops:
  0.0 145.6 %copy-start = (bf16[8,1,128,128]{3,2,1,0:T(8,128)(2,1)S(1)}, bf16[8,1,128,128]{3,2,1,0:T(8,128)(2,1)}, u32[]{:S(2)}) copy-start(bf16[8,1,128,128]{3,2,1,0:T(8,128)(2,1)} %param.18) | copy-start | bytes 786436
  1.4 3.4 %copy-start.5 = (bf16[128,128]{1,0:T(8,128)(2,1)S(1)}, bf16[128,128]{1,0:T(8,128)(2,1)}, u32[]{:S(2)}) copy-start(bf16[128,128]{1,0:T(8,128)(2,1)} %param.13) | copy-start | bytes 98308
  3.5 24.7 %copy-start.3 = (bf16[8,128,1,128]{3,1,2,0:T(8,128)(2,1)S(1)}, bf16[8,128,1,128]{3,1,2,0:T(8,128)(2,1)}, u32[]{:S(2)}) copy-start(bf16[8,128,1,128]{3,1,2,0:T(8,128)(2,1)} %param.16) | copy-start | bytes 786436
  27.5 1.9 %copy-start.4 = (bf16[128,1,256]{2,0,1:T(8,128)(2,1)S(1)}, bf16[128,1,256]{2,0,1:T(8,128)(2,1)}, u32[]{:S(2)}) copy-start(bf16[128,1,256]{2,0,1:T(8,128)(2,1)} %param.17) | copy-start | bytes 196612
  37.6 8.3 %copy-start.6 = (s32[16]{0:T(128)S(1)}, s32[16]{0:T(128)}, u32[]{:S(2)}) copy-start(s32[16]{0:T(128)} %param.21) | copy-start | bytes 196
  37.6 8.9 %copy-start.1 = (s32[16]{0:T(128)S(1)}, s32[16]{0:T(128)}, u32[]{:S(2)}) copy-start(s32[16]{0:T(128)} %param.22) | copy-start | bytes 196
  37.6 65.4 %all-to-all-start = ((f32[16,136,512]{2,1,0:T(8,128)}), f32[16,136,512]{2,1,0:T(8,128)}, u32[]{:S(2)}, u32[]{:S(2)}) async-start(f32[16,136,512]{2,1,0:T(8,128)} %bitcast.69), calls=%async_computation | async-start | bytes 8912896 | tf_op jit(solution)/shard_map/all_to_all | solution.py:25
  113.8 14.5 %copy-start.2 = (s32[2048,2]{0,1:T(2,128)S(1)}, s32[2048,2]{0,1:T(2,128)}, u32[]{:S(2)}) copy-start(s32[2048,2]{0,1:T(2,128)} %param.23) | copy-start | bytes 49156
  113.8 30.4 %all-to-all-start.1 = ((bf16[16,136,256]{2,1,0:T(8,128)(2,1)}), bf16[16,136,256]{2,1,0:T(8,128)(2,1)S(1)}, u32[]{:S(2)}, u32[]{:S(2)}) async-start(bf16[16,136,256]{2,1,0:T(8,128)(2,1)} %broadcast_in_dim.68), calls=%async_computation.1 | async-start | bytes 2228224 | tf_op jit(solution)/shard_map/all_to_all | solution.py:38

commit v6 on v5

--- a/solution.py
+++ b/solution.py
@@ -174,6 +174,55 @@
     )(length.reshape(1), query, cache_k, cache_v, fresh)
 
 
+def mix_kernel(shipped_ref, route_ref, weight_ref, out_ref):
+    block_rows = shipped_ref.shape[0] // REQUESTS_PER_STEP
+    rows = block_rows - EXTRA_ROWS
+    head_dim = weight_ref.shape[0]
+    experts = weight_ref.shape[1] // out_ref.shape[1]
+    width = out_ref.shape[1]
+    top_count = shipped_ref.shape[1] // head_dim
+    for block in range(REQUESTS_PER_STEP):
+        top = block * block_rows
+        low = block * rows
+        gates = jnp.transpose(shipped_ref[top + rows : top + block_rows, :].astype(jnp.float32))
+        mixed = jnp.zeros((rows, width), jnp.float32)
+        for slot in range(top_count):
+            attended = shipped_ref[top : top + rows, slot * head_dim : (slot + 1) * head_dim]
+            projected = jnp.dot(attended, weight_ref[...], preferred_element_type=jnp.float32)
+            chosen = route_ref[low : low + rows, slot : slot + 1]
+            picked = jnp.zeros((rows, width), jnp.float32)
+            for expert in range(experts):
+                picked = picked + jnp.where(
+                    chosen == expert, projected[:, expert * width : (expert + 1) * width], 0.0
+                )
+            mixed = mixed + gates[slot * rows : (slot + 1) * rows, 0:1] * picked
+        out_ref[low : low + rows, :] = mixed
+
+
+def mixed_partials(shipped, route, output_weight, requests):
+    block_rows = shipped.shape[0] // requests
+    rows = block_rows - EXTRA_ROWS
+    experts, head_dim, width = output_weight.shape
+    weight = jnp.transpose(output_weight, (1, 0, 2)).reshape(head_dim, experts * width)
+    total_rows = requests * rows
+    return pl.pallas_call(
+        mix_kernel,
+        out_shape=jax.ShapeDtypeStruct((total_rows, width), jnp.float32),
+        grid=(requests // REQUESTS_PER_STEP,),
+        in_specs=[
+            pl.BlockSpec((REQUESTS_PER_STEP * block_rows, shipped.shape[1]), lambda s: (s, 0)),
+            pl.BlockSpec((REQUESTS_PER_STEP * rows, route.shape[1]), lambda s: (s, 0)),
+            pl.BlockSpec(weight.shape, lambda s: (0, 0)),
+        ],
+        out_specs=pl.BlockSpec((REQUESTS_PER_STEP * rows, width), lambda s: (s, 0)),
+        cost_estimate=pl.CostEstimate(
+            flops=2 * total_rows * route.shape[1] * head_dim * experts * width,
+            transcendentals=0,
+            bytes_accessed=2 * shipped.size + 2 * weight.size + 4 * total_rows * width,
+        ),
+    )(shipped, route, weight)
+
+
 def per_device(
     tokens,
     gain,
@@ -258,23 +307,13 @@
     route = jnp.take(route.reshape(requests, new_len, top_count), staged, axis=0).reshape(
         total_rows, top_count
     )
-    token_attended = by_request[:, :new_len].reshape(total_rows, top_count, heads_local, head_dim)
-    token_gates = (
-        jnp.transpose(
-            by_request[:, new_len, : top_count * new_len].reshape(requests, top_count, new_len),
-            (0, 2, 1),
-        )
-        .reshape(total_rows, top_count)
-        .astype(jnp.float32)
-    )
-    onehot = expert_onehot(route, experts)
-    routed_attended = token_attended[:, :, None, :, :] * onehot[:, :, :, None, None].astype(
-        jnp.bfloat16
-    )
-    projected = jnp.einsum(
-        "tsehk,ehko->tso", routed_attended, expert_output_weight, preferred_element_type=jnp.float32
-    )
-    mixed_part = jnp.sum(token_gates[:, :, None] * projected, axis=1)
+    assert heads_local == 1
+    mixed_part = mixed_partials(
+        by_request.reshape(requests * (new_len + extra_rows), query_cols),
+        route,
+        expert_output_weight.reshape(experts, head_dim, expert_output_weight.shape[3]),
+        requests,
+    )
     output_sum = scatter_sum(scatter_sum(mixed_part, "cc"), "zz")
     return output_sum.astype(jnp.bfloat16)
 

time: 180 us -> 184 us (1.022)
  Pallas kernels: 11.9 us -> 19.6 us
  matrix products: 6.08 us -> 0 us
  waiting for transfers between devices: 70.4 us -> 68.1 us
    pallas_call x0 -> x1, Pallas kernels: none -> 7.7 us  [mixed_partials(): pl.pallas_call(mix_kernel, out_shape=jax.ShapeDtypeStruct((total_rows, wi...]
    dot_general x1 -> x0, matrix products: 6.08 us -> none  [per_device(): jnp.einsum('tsehk,ehko->tso', routed_attended, expert_output_weight, pref...]
    all_to_all x1, waiting for transfers between devices: 15.2 us -> 13.1 us  [gather_rows(): gathered = lax.all_to_all(copies, axis_name, 0, 0, tiled=True)]
  transfers between devices with their start and end apart: 2 -> 2, of which waited for: 2 -> 2; matrix products, arithmetic and copies ran while one was open for 2% -> 3% of each run, Pallas kernels for 0% -> 0%
where the time goes in v6:
time: 184 us
  waiting for transfers between devices  68.1 us (37%)
  blocking collectives  51 us (28%)
  starting transfers between devices  21.5 us (12%)
  Pallas kernels  19.6 us (11%)
  local copies, waits for them, and re-layouts  11.7 us (6%)
  other arithmetic  10.4 us (6%)
    all_to_all x1, waiting for transfers between devices, scatter_sum(): lax.all_to_all(part.reshape((members, part.shape[0] // members) + part.sh...  55.1 us
    all_to_all x2, blocking collectives, scatter_sum(): lax.all_to_all(part.reshape((members, part.shape[0] // members) + part.sh...  28.3 us
    all_gather x1, blocking collectives, per_device(): gathered = lax.all_gather(tokens, TOKEN_AXES, axis=0, tiled=True)  22.7 us
    all_to_all x1, starting transfers between devices, gather_rows(): gathered = lax.all_to_all(copies, axis_name, 0, 0, tiled=True)  14.6 us
    all_to_all x1, waiting for transfers between devices, gather_rows(): gathered = lax.all_to_all(copies, axis_name, 0, 0, tiled=True)  13.1 us
    pallas_call x1, Pallas kernels, mixed_partials(): pl.pallas_call(mix_kernel, out_shape=jax.ShapeDtypeStruct((total_rows, wi...  7.7 us
    pallas_call x1, Pallas kernels, packed_partials(): pl.pallas_call(pack_kernel, out_shape=jax.ShapeDtypeStruct((requests * bl...  7.43 us
    all_to_all x1, starting transfers between devices, scatter_sum(): lax.all_to_all(part.reshape((members, part.shape[0] // members) + part.sh...  6.94 us
  transfers between devices with their start and end apart: 2, of which 2 were waited for; matrix products, arithmetic and copies ran while one was open for 3% of the time, Pallas kernels for 0%

profile of v6, /device:TPU:1, one launch (start us, length us, event | category | flops | bytes accessed | tf_op | source)
XLA Modules:
  0.0 183.7 jit_solution(16415230054430454741)
XLA Ops:
  0.0 0.0 copy-start
  0.0 0.7 compare_select_fusion.2
  0.7 0.6 scatter_custom_fusion
  1.4 0.1 broadcast_bitcast_fusion
  1.4 0.0 copy-start.5
  1.5 1.3 gather_fusion.3
  2.8 0.7 fusion.10
  3.5 1.4 copy.19.route_ref
  4.8 0.0 copy-done.5
  4.8 22.7 %all_gather.3 = bf16[2048,128]{1,0:T(8,128)(2,1)S(1)} all-gather(bf16[128,128]{1,0:T(8,128)(2,1)S(1)} %copy-done.5), channel_id=1, replica_groups=mesh['gx'=16,'zz'=8,'cc'=2] {'zz','cc'}, dimensions={0}, use_global_device_ids=true | all-gather | bytes 557056 | tf_op jit(solution)/shard_map/all_gather | solution.py:244
  27.5 0.0 copy-start.4
  27.5 0.6 gather_fusion.1
  28.2 0.0 copy-done
  28.2 1.2 bitcast_select_fusion.1.tok_ref
  29.4 0.0 copy-done.4
  29.4 0.7 pad_maximum_fusion.weight_ref
  30.1 7.4 %shard_map.109 = f32[2176,512]{1,0:T(8,128)} custom-call(bf16[2048,128]{1,0:T(8,128)(2,1)} %bitcast_select_fusion.1.tok_ref, bf16[1,128]{1,0:T(2,128)(2,1)} %bitcast.73, bf16[8,128]{1,0:T(8,128)(2,1)} %bitcast.71, bf16[128,1280]{1,0:T(8,128)(2,1)} %pad_maximum_fusion.weight_ref, s32[2048,2]{1,0:T(8,128)} %copy.19.route_ref, ...), custom_call_target="tpu_custom_call" | custom-call | flops 675282944 | bytes 5308416 | tf_op jit(solution)/shard_map/pallas_call | solution.py:106
  37.6 0.0 copy-start.6
  37.6 0.0 copy-start.1
  37.6 6.9 %all-to-all-start = ((f32[16,136,512]{2,1,0:T(8,128)}), f32[16,136,512]{2,1,0:T(8,128)}, u32[]{:S(2)}, u32[]{:S(2)}) async-start(f32[16,136,512]{2,1,0:T(8,128)} %bitcast.62), calls=%async_computation | async-start | bytes 8912896 | tf_op jit(solution)/shard_map/all_to_all | solution.py:25
  44.5 0.6 dynamic-slice.4
  45.7 0.1 reshape.232
  45.7 0.1 reshape.231
  45.8 0.0 copy-done.6
  45.8 0.6 dynamic-slice.5
  46.4 0.0 copy-done.1
  46.4 0.7 gather_fusion
  47.1 0.1 broadcast_in_dim.60
  47.2 0.1 broadcast_in_dim.61
  47.8 55.1 %all-to-all-done = f32[16,136,512]{2,1,0:T(8,128)} async-done(((f32[16,136,512]{2,1,0:T(8,128)}), f32[16,136,512]{2,1,0:T(8,128)}, u32[]{:S(2)}, u32[]{:S(2)}) %all-to-all-start) | async-done | bytes 4456480 | tf_op jit(solution)/shard_map/all_to_all | solution.py:25
  102.9 2.7 %reduce_sum.27 = f32[136,512]{1,0:T(8,128)S(1)} reduce(f32[16,136,512]{2,1,0:T(8,128)} %all-to-all-done, f32[]{:T(128)} %constant.87.clone.1), dimensions={0}, to_apply=%region_1.0 | reduce | flops 1044480 | bytes 4734980 | tf_op jit(solution)/shard_map/reduce_sum | solution.py:32
  105.7 0.7 fusion.1
  106.4 0.1 mul.35
  106.5 0.1 mul.36
  106.6 0.7 multiply_convert_fusion.query_ref
  107.4 4.4 %shard_map.110 = bf16[256,128]{1,0:T(8,128)(2,1)} custom-call(s32[1]{0:T(128)S(6)} %select_n.109.length_ref, bf16[256,128]{1,0:T(8,128)(2,1)} %multiply_convert_fusion.query_ref, bf16[4096,128]{1,0:T(8,128)(2,1)} %bitcast.65, bf16[4096,128]{1,0:T(8,128)(2,1)} %bitcast.66, bf16[128,256]{1,0:T(8,128)(2,1)} %get-tuple-element.30.fresh_ref), custom_call_target="tpu_custom_call" | custom-call | flops 553648128 | bytes 2293760 | tf_op jit(solution)/shard_map/pallas_call | solution.py:160
  111.8 0.9 reshape.243
  112.7 1.1 broadcast_in_dim.71
  113.8 0.0 copy-start.2
  113.8 14.6 %all-to-all-start.1 = ((bf16[16,136,256]{2,1,0:T(8,128)(2,1)}), bf16[16,136,256]{2,1,0:T(8,128)(2,1)S(1)}, u32[]{:S(2)}, u32[]{:S(2)}) async-start(bf16[16,136,256]{2,1,0:T(8,128)(2,1)} %broadcast_in_dim.71), calls=%async_computation.1 | async-start | bytes 2228224 | tf_op jit(solution)/shard_map/all_to_all | solution.py:38
  128.4 0.0 copy-done.2
  128.4 0.0 copy-start.3
  128.4 0.6 gather_fusion.4
  129.0 0.1 broadcast_select_fusion
  129.1 1.4 copy.20
  130.5 0.0 copy-done.3
  130.5 0.7 copy_bitcast_fusion.weight_ref
  131.3 13.1 %all-to-all-done.1 = bf16[16,136,256]{2,1,0:T(8,128)(2,1)S(1)} async-done(((bf16[16,136,256]{2,1,0:T(8,128)(2,1)}), bf16[16,136,256]{2,1,0:T(8,128)(2,1)S(1)}, u32[]{:S(2)}, u32[]{:S(2)}) %all-to-all-start.1) | async-done | bytes 1114144 | tf_op jit(solution)/shard_map/all_to_all | solution.py:38
  144.3 0.6 gather_fusion.2
  145.0 2.0 %bitcast_select_fusion.shipped_ref = bf16[2176,256]{1,0:T(8,128)(2,1)} fusion(bf16[16,136,256]{2,1,0:T(8,128)(2,1)S(1)} %gather_fusion.2, pred[2176]{0:T(1024)(128)(4,1)S(1)} %broadcast_in_dim.61), kind=kLoop, calls=%fused_computation.6 | loop fusion | flops 557056 | bytes 2230400 | tf_op jit(solution)/shard_map/jit(_take)/select_n | solution.py:306
  147.0 7.7 %shard_map.111 = f32[2048,128]{1,0:T(8,128)} custom-call(bf16[2176,256]{1,0:T(8,128)(2,1)} %bitcast_select_fusion.shipped_ref, s32[2048,2]{1,0:T(8,128)} %bitcast.67, bf16[128,1024]{1,0:T(8,128)(2,1)} %copy_bitcast_fusion.weight_ref), custom_call_target="tpu_custom_call" | custom-call | flops 1073741824 | bytes 2424832 | tf_op jit(solution)/shard_map/pallas_call | solution.py:208
  154.7 8.6 %all_to_all.20 = f32[2,1024,128]{2,1,0:T(8,128)S(1)} all-to-all(f32[2,1024,128]{2,1,0:T(8,128)} %bitcast.68), channel_id=1, replica_groups=mesh['gx'=16,'zz'=8,'cc'=2] {'cc'}, dimensions={0} | all-to-all | bytes 2097152 | tf_op jit(solution)/shard_map/all_to_all | solution.py:25
  163.2 0.1 reduce_sum.28
  163.3 19.7 %all_to_all.21 = f32[8,128,128]{2,1,0:T(8,128)S(1)} all-to-all(f32[8,128,128]{2,1,0:T(8,128)S(1)} %bitcast.64), channel_id=1, replica_groups=mesh['gx'=16,'zz'=8,'cc'=2] {'zz'}, dimensions={0} | all-to-all | bytes 1048576 | tf_op jit(solution)/shard_map/all_to_all | solution.py:25
  183.0 0.6 reduce_sum.29
  (21 shorter events, 0.2 us)
Async XLA Ops:
  0.0 28.2 %copy-start = (bf16[8,128,1,128]{3,1,2,0:T(8,128)(2,1)S(1)}, bf16[8,128,1,128]{3,1,2,0:T(8,128)(2,1)}, u32[]{:S(2)}) copy-start(bf16[8,128,1,128]{3,1,2,0:T(8,128)(2,1)} %param.16) | copy-start | bytes 786436
  1.4 3.4 %copy-start.5 = (bf16[128,128]{1,0:T(8,128)(2,1)S(1)}, bf16[128,128]{1,0:T(8,128)(2,1)}, u32[]{:S(2)}) copy-start(bf16[128,128]{1,0:T(8,128)(2,1)} %param.13) | copy-start | bytes 98308
  27.5 1.9 %copy-start.4 = (bf16[128,1,256]{2,0,1:T(8,128)(2,1)S(1)}, bf16[128,1,256]{2,0,1:T(8,128)(2,1)}, u32[]{:S(2)}) copy-start(bf16[128,1,256]{2,0,1:T(8,128)(2,1)} %param.17) | copy-start | bytes 196612
  37.6 8.3 %copy-start.6 = (s32[16]{0:T(128)S(1)}, s32[16]{0:T(128)}, u32[]{:S(2)}) copy-start(s32[16]{0:T(128)} %param.21) | copy-start | bytes 196
  37.6 8.8 %copy-start.1 = (s32[16]{0:T(128)S(1)}, s32[16]{0:T(128)}, u32[]{:S(2)}) copy-start(s32[16]{0:T(128)} %param.22) | copy-start | bytes 196
  37.6 65.3 %all-to-all-start = ((f32[16,136,512]{2,1,0:T(8,128)}), f32[16,136,512]{2,1,0:T(8,128)}, u32[]{:S(2)}, u32[]{:S(2)}) async-start(f32[16,136,512]{2,1,0:T(8,128)} %bitcast.62), calls=%async_computation | async-start | bytes 8912896 | tf_op jit(solution)/shard_map/all_to_all | solution.py:25
  113.8 14.6 %copy-start.2 = (s32[2048,2]{0,1:T(2,128)S(1)}, s32[2048,2]{0,1:T(2,128)}, u32[]{:S(2)}) copy-start(s32[2048,2]{0,1:T(2,128)} %param.23) | copy-start | bytes 49156
  113.8 30.6 %all-to-all-start.1 = ((bf16[16,136,256]{2,1,0:T(8,128)(2,1)}), bf16[16,136,256]{2,1,0:T(8,128)(2,1)S(1)}, u32[]{:S(2)}, u32[]{:S(2)}) async-start(bf16[16,136,256]{2,1,0:T(8,128)(2,1)} %broadcast_in_dim.71), calls=%async_computation.1 | async-start | bytes 2228224 | tf_op jit(solution)/shard_map/all_to_all | solution.py:38
  128.4 2.1 %copy-start.3 = (bf16[8,1,128,128]{3,2,1,0:T(8,128)(2,1)S(1)}, bf16[8,1,128,128]{3,2,1,0:T(8,128)(2,1)}, u32[]{:S(2)}) copy-start(bf16[8,1,128,128]{3,2,1,0:T(8,128)(2,1)} %param.18) | copy-start | bytes 786436

commit v7 on v4

--- a/solution.py
+++ b/solution.py
@@ -5,6 +5,7 @@
 from jax.experimental.pallas import tpu as pltpu
 from jax.sharding import Mesh, PartitionSpec as P
 
+
 masked_score = -1e30
 norm_eps = 1e-06
 LANES = 128
@@ -14,10 +15,6 @@
     return (route_rows[:, :, None] == jnp.arange(experts, dtype=jnp.int32)[None, None, :]).astype(
         jnp.float32
     )
-
-
-def padded_width(width):
-    return -(-width // LANES) * LANES
 
 
 def scatter_sum(part, axis_name):
@@ -37,47 +34,6 @@
     copies = jnp.broadcast_to(piece[None], (members,) + piece.shape)
     gathered = lax.all_to_all(copies, axis_name, 0, 0, tiled=True)
     return gathered.reshape((members * piece.shape[0],) + piece.shape[1:])
-
-
-def pack_kernel(
-    order_ref, tok_ref, gain_ref, router_ref, query_ref, keyval_ref, route_ref, route_t_ref, out_ref
-):
-    width = tok_ref.shape[1]
-    rows = tok_ref.shape[0]
-    experts = query_ref.shape[0]
-    head_dim = query_ref.shape[2]
-    keyval_cols = keyval_ref.shape[1]
-    widened = tok_ref[...].astype(jnp.float32)
-    scaled = (widened * gain_ref[...].astype(jnp.float32)).astype(jnp.bfloat16)
-    first = route_ref[:, 0:1]
-    second = route_ref[:, 1:2]
-    query_first = jnp.zeros((rows, head_dim), jnp.float32)
-    query_second = jnp.zeros((rows, head_dim), jnp.float32)
-    for expert in range(experts):
-        projected = jnp.dot(scaled, query_ref[expert], preferred_element_type=jnp.float32)
-        query_first = query_first + jnp.where(first == expert, projected, 0.0)
-        query_second = query_second + jnp.where(second == expert, projected, 0.0)
-    keyval = jnp.dot(scaled, keyval_ref[...], preferred_element_type=jnp.float32)
-    out_ref[0:rows, 0:head_dim] = query_first
-    out_ref[0:rows, head_dim : 2 * head_dim] = query_second
-    out_ref[0:rows, 2 * head_dim : 2 * head_dim + keyval_cols] = keyval
-    widened_t = jnp.transpose(widened)
-    squares_row = jnp.sum(widened_t * widened_t, axis=0, keepdims=True)
-    logits_t = lax.dot_general(
-        router_ref[...], scaled, (((1,), (1,)), ((), ())), preferred_element_type=jnp.float32
-    )
-    expert_row = lax.broadcasted_iota(jnp.int32, logits_t.shape, 0)
-    route_t = route_t_ref[...]
-    chosen_first = jnp.sum(jnp.where(expert_row == route_t[0:1, :], logits_t, 0.0), axis=0, keepdims=True)
-    chosen_second = jnp.sum(jnp.where(expert_row == route_t[1:2, :], logits_t, 0.0), axis=0, keepdims=True)
-    extra = out_ref.shape[0] - rows
-    out_ref[rows:, :] = jnp.zeros((extra, out_ref.shape[1]), jnp.float32)
-    out_ref[rows : rows + 1, 0:rows] = chosen_first
-    out_ref[rows : rows + 1, rows : 2 * rows] = chosen_second
-    out_ref[rows : rows + 1, 2 * rows : 3 * rows] = squares_row
-
-
-EXTRA_ROWS = 8
 
 
 def attend_kernel(length_ref, query_ref, cache_k_ref, cache_v_ref, fresh_ref, out_ref):
@@ -134,39 +90,7 @@
     )(length.reshape(1), query, cache_k, cache_v, fresh)
 
 
-def packed_partials(order, gathered, gain, w_router, query_weight, keyval_weight, route):
-    total_rows, width = gathered.shape
-    requests = order.shape[0]
-    rows = total_rows // requests
-    experts, _, head_dim = query_weight.shape
-    keyval_cols = keyval_weight.shape[1]
-    packed_cols = 2 * head_dim + keyval_cols
-    assert 3 * rows <= packed_cols
-    block_rows = rows + EXTRA_ROWS
-    flops = 2 * total_rows * width * (experts * head_dim + keyval_cols + w_router.shape[1])
-    moved = 2 * total_rows * width + 4 * requests * block_rows * packed_cols + 2 * query_weight.size
-    return pl.pallas_call(
-        pack_kernel,
-        out_shape=jax.ShapeDtypeStruct((requests * block_rows, packed_cols), jnp.float32),
-        grid_spec=pltpu.PrefetchScalarGridSpec(
-            num_scalar_prefetch=1,
-            grid=(requests,),
-            in_specs=[
-                pl.BlockSpec((rows, width), lambda s, order_ref: (order_ref[s], 0)),
-                pl.BlockSpec((1, width), lambda s, order_ref: (0, 0)),
-                pl.BlockSpec((w_router.shape[1], width), lambda s, order_ref: (0, 0)),
-                pl.BlockSpec(query_weight.shape, lambda s, order_ref: (0, 0, 0)),
-                pl.BlockSpec(keyval_weight.shape, lambda s, order_ref: (0, 0)),
-                pl.BlockSpec((rows, route.shape[1]), lambda s, order_ref: (order_ref[s], 0)),
-                pl.BlockSpec((route.shape[1], rows), lambda s, order_ref: (0, order_ref[s])),
-            ],
-            out_specs=pl.BlockSpec((block_rows, packed_cols), lambda s, order_ref: (s, 0)),
-        ),
-        cost_estimate=pl.CostEstimate(flops=flops, transcendentals=0, bytes_accessed=moved),
-    )(order, gathered, gain.reshape(1, width), jnp.transpose(w_router), query_weight, keyval_weight, route, jnp.transpose(route))
-
-
-def per_device(
+def per_device_body(
     tokens,
     gain,
     w_router,
@@ -184,31 +108,70 @@
     heads_local = expert_query_weight.shape[2]
     head_dim = expert_query_weight.shape[3]
     top_count = route.shape[1]
+    assert heads_local == 1
+    local_width = tokens.shape[1]
+    members = lax.axis_size("gx")
+    full_width = local_width * members
+    slot_index = lax.axis_index("gx")
+    new_len = tokens.shape[0]
+    total_rows = new_len * requests
+    query_cols = experts * head_dim
+    keyval_cols = 2 * head_dim
+    small_piece = jnp.concatenate(
+        [
+            w_router,
+            gain[:, None],
+            jnp.zeros((local_width, LANES - w_router.shape[1] - 1), jnp.bfloat16),
+        ],
+        axis=1,
+    )
+    weight_piece = jnp.concatenate(
+        [
+            jnp.transpose(expert_query_weight.reshape(experts, local_width, head_dim), (1, 0, 2)).reshape(
+                local_width, query_cols
+            ),
+            key_value_weight.reshape(local_width, keyval_cols),
+            small_piece,
+        ],
+        axis=1,
+    )
+    pieces = [None] * members
+    pieces[0] = weight_piece
+    for offset in range(1, members):
+        pieces[offset] = lax.ppermute(
+            weight_piece, "gx", [(source, (source + offset) % members) for source in range(members)]
+        )
+    received = jnp.stack(pieces)
+    sources = (slot_index - jnp.arange(members, dtype=jnp.int32)) % members
+    head_weights = jnp.zeros_like(received).at[sources].set(received)
     gathered = lax.all_gather(tokens, TOKEN_AXES, axis=0, tiled=True)
-    total_rows, local_width = gathered.shape
-    new_len = total_rows // requests
-    full_width = local_width * lax.axis_size("gx")
-    slot_index = lax.axis_index("gx")
     inverse = jnp.zeros((requests,), jnp.int32).at[deal].set(jnp.arange(requests, dtype=jnp.int32))
-    assert heads_local == 1
-    packed = packed_partials(
-        inverse,
-        gathered,
-        gain,
-        w_router,
-        expert_query_weight.reshape(experts, local_width, head_dim),
-        key_value_weight.reshape(local_width, 2 * head_dim),
-        route,
-    )
+    by_slot = jnp.take(gathered.reshape(requests, new_len, local_width), inverse, axis=0)
+    own_tokens = lax.all_to_all(by_slot, "gx", 0, 0, tiled=True)
+    my_request = jnp.take(inverse, slot_index)
+    my_route = jnp.take(route.reshape(requests, new_len, top_count), my_request, axis=0)
+    widened = own_tokens.astype(jnp.float32)
+    square_sums = jnp.sum(widened * widened, axis=(0, 2))
+    gain_full = head_weights[:, :, query_cols + keyval_cols + w_router.shape[1]]
+    scaled_input = (widened * gain_full.astype(jnp.float32)[:, None, :]).astype(jnp.bfloat16)
+    router_cols = slice(query_cols + keyval_cols, query_cols + keyval_cols + w_router.shape[1])
+    logits_raw = jnp.einsum(
+        "itd,ide->te", scaled_input, head_weights[:, :, router_cols], preferred_element_type=jnp.float32
+    )
+    projected = jnp.einsum(
+        "itd,idk->tk",
+        scaled_input,
+        head_weights[:, :, : query_cols + keyval_cols],
+        preferred_element_type=jnp.float32,
+    )
+    my_onehot = expert_onehot(my_route, experts)
+    query_totals = jnp.sum(
+        my_onehot[:, :, :, None] * projected[:, None, :query_cols].reshape(new_len, 1, experts, head_dim),
+        axis=2,
+    ).reshape(new_len, top_count, heads_local, head_dim)
+    keyval_sums = projected[:, query_cols:].reshape(new_len, heads_local, keyval_cols)
+    chosen_sums = jnp.sum(my_onehot * logits_raw[:, None, :], axis=2)
     query_cols = top_count * heads_local * head_dim
-    keyval_cols = heads_local * 2 * head_dim
-    summed = scatter_sum(packed, "gx")
-    query_totals = summed[:new_len, :query_cols].reshape(new_len, top_count, heads_local, head_dim)
-    keyval_sums = summed[:new_len, query_cols : query_cols + keyval_cols].reshape(
-        new_len, heads_local, 2 * head_dim
-    )
-    chosen_sums = jnp.transpose(summed[new_len, : top_count * new_len].reshape(top_count, new_len))
-    square_sums = summed[new_len, top_count * new_len : (top_count + 1) * new_len]
     inverse_root_mean = lax.rsqrt(square_sums / full_width + norm_eps)
     chosen = chosen_sums * inverse_root_mean[:, None]
     gate_gap = chosen[:, 0] - chosen[:, 1]
@@ -285,6 +248,4 @@
         P(),
         P(),
     )
-    return jax.shard_map(
-        per_device, mesh=staged_mesh, in_specs=placed, out_specs=P(gy, "gx"), check_vma=False
-    )
+    return jax.shard_map(per_device_body, mesh=staged_mesh, in_specs=placed, out_specs=P(gy, "gx"), check_vma=False)

time: 185 us -> 232 us (1.25)
  starting transfers between devices: 21.4 us -> 61.3 us
  local copies, waits for them, and re-layouts: 9.22 us -> 47.3 us
  waiting for transfers between devices: 70.2 us -> 48.5 us
  Pallas kernels: 17.5 us -> 4.4 us
  matrix products: 6.08 us -> 10.7 us
    all_to_all x1, waiting for transfers between devices: 54.9 us -> 0.01 us  [per_device_body(): own_tokens = lax.all_to_all(by_slot, 'gx', 0, 0, tiled=True)]
    ppermute x0 -> x15, starting transfers between devices: none -> 38.1 us  [per_device_body(): lax.ppermute(weight_piece, 'gx', [(source, (source + offset) % members) f...]
    ppermute x0 -> x15, waiting for transfers between devices: none -> 33.7 us  [per_device_body(): lax.ppermute(weight_piece, 'gx', [(source, (source + offset) % members) f...]
    scatter x1 -> x2, local copies, waits for them, and re-layouts: 1.11 us -> 19 us  [the longest x1 18.4 us: per_device_body(): head_weights = jnp.zeros_like(received).at[sources].set(received)]
    pallas_call x1 -> x0, Pallas kernels: 13.1 us -> none  [packed_partials(): pl.pallas_call(pack_kernel, out_shape=jax.ShapeDtypeStruct((requests * bl...]
    unnamed x12 -> x23, local copies, waits for them, and re-layouts: 2.08 us -> 13.5 us
    dot_general x1 -> x3, matrix products: 6.08 us -> 10.7 us  [the longest x1 6.08 us: per_device_body(): jnp.einsum('tsehk,ehko->tso', routed_attended, expert_output_weight, pref...]
    broadcast_in_dim x1 -> x4, local copies, waits for them, and re-layouts: 0.07 us -> 3.95 us  [the longest x1 3.09 us: per_device_body(): head_weights = jnp.zeros_like(received).at[sources].set(received)]
  transfers between devices with their start and end apart: 2 -> 17, of which waited for: 2 -> 9; matrix products, arithmetic and copies ran while one was open for 2% -> 19% of each run, Pallas kernels for 0% -> 0%
where the time goes in v7:
time: 232 us; the launch traced here: 231 us
  starting transfers between devices  61.3 us (26%)
  blocking collectives  50.8 us (22%)
  waiting for transfers between devices  48.5 us (21%)
  local copies, waits for them, and re-layouts  47.3 us (20%)
  matrix products  10.7 us (5%)
  other arithmetic  6.84 us (3%)
  Pallas kernels  4.4 us (2%)
    ppermute x15, starting transfers between devices, per_device_body(): lax.ppermute(weight_piece, 'gx', [(source, (source + offset) % members) f...  38.1 us
    ppermute x15, waiting for transfers between devices, per_device_body(): lax.ppermute(weight_piece, 'gx', [(source, (source + offset) % members) f...  33.7 us
    all_to_all x2, blocking collectives, scatter_sum(): lax.all_to_all(part.reshape((members, part.shape[0] // members) + part.sh...  27.2 us
    all_gather x1, blocking collectives, per_device_body(): gathered = lax.all_gather(tokens, TOKEN_AXES, axis=0, tiled=True)  23.6 us
    scatter x1, local copies, waits for them, and re-layouts, per_device_body(): head_weights = jnp.zeros_like(received).at[sources].set(received)  18.4 us
    all_to_all x1, starting transfers between devices, gather_rows(): gathered = lax.all_to_all(copies, axis_name, 0, 0, tiled=True)  17.4 us
    all_to_all x1, waiting for transfers between devices, gather_rows(): gathered = lax.all_to_all(copies, axis_name, 0, 0, tiled=True)  14.8 us
    unnamed x23, local copies, waits for them, and re-layouts  13.5 us
  transfers between devices with their start and end apart: 17, of which 9 were waited for; matrix products, arithmetic and copies ran while one was open for 19% of the time, Pallas kernels for 0%

profile of v7, /device:TPU:1, one launch (start us, length us, event | category | flops | bytes accessed | tf_op | source)
XLA Modules:
  0.0 231.4 jit_solution(10550967534189660424)
XLA Ops:
  0.0 1.0 copy_bitcast_fusion
  1.0 0.8 copy.37
  1.8 0.8 copy.38
  2.6 1.0 concatenate.6
  3.6 2.2 collective-permute-start
  5.8 2.6 %collective-permute-start.1 = (bf16[128,1408]{1,0:T(8,128)(2,1)S(1)}, bf16[128,1408]{1,0:T(8,128)(2,1)S(1)}, u32[]{:S(2)}, u32[]{:S(2)}) collective-permute-start(bf16[128,1408]{1,0:T(8,128)(2,1)S(1)} %concatenate.6), channel_id=1, source_target_pairs={{0,32},{16,48},{32,64},{48,80},{64,96},{80,112},{96,128},{112,144}... | collective-permute-start | bytes 1081352 | tf_op jit(solution)/shard_map/ppermute | solution.py:141
  8.4 2.0 collective-permute-start.2
  10.4 1.2 collective-permute-start.3
  11.6 1.0 collective-permute-start.4
  12.6 0.7 compare_select_fusion.3
  14.0 23.6 %all_gather.3 = bf16[2048,128]{1,0:T(8,128)(2,1)S(1)} all-gather(bf16[128,128]{1,0:T(8,128)(2,1)} %param.11), channel_id=1, replica_groups=mesh['gx'=16,'zz'=8,'cc'=2] {'zz','cc'}, dimensions={0}, use_global_device_ids=true | all-gather | bytes 557056 | tf_op jit(solution)/shard_map/all_gather | solution.py:147
  37.5 0.6 gather_fusion.1
  38.2 0.9 broadcast_select_fusion.1
  39.1 5.8 %all-to-all-start = ((bf16[16,128,128]{2,1,0:T(8,128)(2,1)}), bf16[16,128,128]{2,1,0:T(8,128)(2,1)S(1)}, u32[]{:S(2)}, u32[]{:S(2)}) async-start(bf16[16,128,128]{2,1,0:T(8,128)(2,1)} %broadcast_select_fusion.1), calls=%async_computation | async-start | bytes 1048576 | tf_op jit(solution)/shard_map/all_to_all | solution.py:150
  46.3 0.7 select_bitcast_fusion
  47.2 1.2 dynamic-slice.8
  48.4 1.3 gather_fusion
  50.5 0.8 bitcast_dynamic-update-slice_fusion.15
  51.2 3.8 %collective-permute-start.5 = (bf16[128,1408]{1,0:T(8,128)(2,1)S(1)}, bf16[128,1408]{1,0:T(8,128)(2,1)S(1)}, u32[]{:S(2)}, u32[]{:S(2)}) collective-permute-start(bf16[128,1408]{1,0:T(8,128)(2,1)S(1)} %concatenate.6), channel_id=1, source_target_pairs={{0,96},{16,112},{32,128},{48,144},{64,160},{80,176},{96,192},{112,... | collective-permute-start | bytes 1081352 | tf_op jit(solution)/shard_map/ppermute | solution.py:141
  55.0 1.7 bitcast_dynamic-update-slice_fusion.14
  56.8 2.4 %collective-permute-start.6 = (bf16[128,1408]{1,0:T(8,128)(2,1)S(1)}, bf16[128,1408]{1,0:T(8,128)(2,1)S(1)}, u32[]{:S(2)}, u32[]{:S(2)}) collective-permute-start(bf16[128,1408]{1,0:T(8,128)(2,1)S(1)} %concatenate.6), channel_id=1, source_target_pairs={{0,112},{16,128},{32,144},{48,160},{64,176},{80,192},{96,208},{112... | collective-permute-start | bytes 1081352 | tf_op jit(solution)/shard_map/ppermute | solution.py:141
  59.1 0.8 bitcast_dynamic-update-slice_fusion.13
  59.9 1.8 collective-permute-start.7
  61.7 0.8 bitcast_dynamic-update-slice_fusion.12
  62.5 2.1 collective-permute-start.8
  64.6 0.8 bitcast_dynamic-update-slice_fusion.11
  65.3 2.1 collective-permute-start.9
  67.4 0.8 bitcast_dynamic-update-slice_fusion.10
  68.2 1.8 collective-permute-done.5
  69.9 5.4 %collective-permute-start.10 = (bf16[128,1408]{1,0:T(8,128)(2,1)S(1)}, bf16[128,1408]{1,0:T(8,128)(2,1)S(1)}, u32[]{:S(2)}, u32[]{:S(2)}) collective-permute-start(bf16[128,1408]{1,0:T(8,128)(2,1)S(1)} %concatenate.6), channel_id=1, source_target_pairs={{0,176},{16,192},{32,208},{48,224},{64,240},{80,0},{96,16},{112,32... | collective-permute-start | bytes 1081352 | tf_op jit(solution)/shard_map/ppermute | solution.py:141
  75.4 0.8 bitcast_dynamic-update-slice_fusion.9
  76.1 0.8 bitcast_dynamic-update-slice_fusion.8
  77.0 5.0 %collective-permute-done.7 = bf16[128,1408]{1,0:T(8,128)(2,1)S(1)} collective-permute-done((bf16[128,1408]{1,0:T(8,128)(2,1)S(1)}, bf16[128,1408]{1,0:T(8,128)(2,1)S(1)}, u32[]{:S(2)}, u32[]{:S(2)}) %collective-permute-start.7) | collective-permute-done | bytes 360480 | tf_op jit(solution)/shard_map/ppermute | solution.py:141
  82.0 2.4 %collective-permute-start.12 = (bf16[128,1408]{1,0:T(8,128)(2,1)S(1)}, bf16[128,1408]{1,0:T(8,128)(2,1)S(1)}, u32[]{:S(2)}, u32[]{:S(2)}) collective-permute-start(bf16[128,1408]{1,0:T(8,128)(2,1)S(1)} %concatenate.6), channel_id=1, source_target_pairs={{0,208},{16,224},{32,240},{48,0},{64,16},{80,32},{96,48},{112,64},... | collective-permute-start | bytes 1081352 | tf_op jit(solution)/shard_map/ppermute | solution.py:141
  84.4 0.8 bitcast_dynamic-update-slice_fusion.7
  85.1 4.8 %collective-permute-done.8 = bf16[128,1408]{1,0:T(8,128)(2,1)S(1)} collective-permute-done((bf16[128,1408]{1,0:T(8,128)(2,1)S(1)}, bf16[128,1408]{1,0:T(8,128)(2,1)S(1)}, u32[]{:S(2)}, u32[]{:S(2)}) %collective-permute-start.8) | collective-permute-done | bytes 360480 | tf_op jit(solution)/shard_map/ppermute | solution.py:141
  89.9 9.0 %collective-permute-start.13 = (bf16[128,1408]{1,0:T(8,128)(2,1)S(1)}, bf16[128,1408]{1,0:T(8,128)(2,1)S(1)}, u32[]{:S(2)}, u32[]{:S(2)}) collective-permute-start(bf16[128,1408]{1,0:T(8,128)(2,1)S(1)} %concatenate.6), channel_id=1, source_target_pairs={{0,224},{16,240},{32,0},{48,16},{64,32},{80,48},{96,64},{112,80},{... | collective-permute-start | bytes 1081352 | tf_op jit(solution)/shard_map/ppermute | solution.py:141
  98.9 0.8 bitcast_dynamic-update-slice_fusion.6
  99.7 3.6 %collective-permute-done.9 = bf16[128,1408]{1,0:T(8,128)(2,1)S(1)} collective-permute-done((bf16[128,1408]{1,0:T(8,128)(2,1)S(1)}, bf16[128,1408]{1,0:T(8,128)(2,1)S(1)}, u32[]{:S(2)}, u32[]{:S(2)}) %collective-permute-start.9) | collective-permute-done | bytes 360480 | tf_op jit(solution)/shard_map/ppermute | solution.py:141
  103.4 0.8 bitcast_dynamic-update-slice_fusion.5
  104.2 1.4 collective-permute-done.10
  105.7 0.8 bitcast_dynamic-update-slice_fusion.4
  106.4 0.8 bitcast_dynamic-update-slice_fusion.3
  107.2 9.2 %collective-permute-done.12 = bf16[128,1408]{1,0:T(8,128)(2,1)S(1)} collective-permute-done((bf16[128,1408]{1,0:T(8,128)(2,1)S(1)}, bf16[128,1408]{1,0:T(8,128)(2,1)S(1)}, u32[]{:S(2)}, u32[]{:S(2)}) %collective-permute-start.12) | collective-permute-done | bytes 360480 | tf_op jit(solution)/shard_map/ppermute | solution.py:141
  116.4 0.8 bitcast_dynamic-update-slice_fusion.2
  117.1 0.9 collective-permute-done.13
  118.0 0.8 bitcast_dynamic-update-slice_fusion.1
  118.8 7.0 %collective-permute-done.14 = bf16[128,1408]{1,0:T(8,128)(2,1)S(1)} collective-permute-done((bf16[128,1408]{1,0:T(8,128)(2,1)S(1)}, bf16[128,1408]{1,0:T(8,128)(2,1)S(1)}, u32[]{:S(2)}, u32[]{:S(2)}) %collective-permute-start.14) | collective-permute-done | bytes 360480 | tf_op jit(solution)/shard_map/ppermute | solution.py:141
  125.8 0.8 bitcast_dynamic-update-slice_fusion
  126.5 3.1 %broadcast_in_dim.95 = bf16[16,128,1408]{2,1,0:T(8,128)(2,1)} broadcast(bf16[]{:T(256)} %constant.122.clone.1), dimensions={} | broadcast | bytes 5767170 | tf_op jit(solution)/shard_map/broadcast_in_dim | solution.py:146
  129.6 18.4 %scatter_fusion = bf16[16,128,1408]{2,1,0:T(8,128)(2,1)} fusion(bf16[16,128,1408]{2,1,0:T(8,128)(2,1)} %broadcast_in_dim.95, s32[16]{0:T(128)S(1)} %fusion.29, bf16[16,128,1408]{2,1,0:T(8,128)(2,1)} %bitcast_dynamic-update-slice_fusion), kind=kCustom, calls=%fused_computation.5 | custom fusion | bytes 17301568 | tf_op jit(solution)/shard_map/scatter | solution.py:146
  148.1 1.4 convert_reduce_fusion
  149.7 3.3 %fusion.12 = f32[128,1280]{1,0:T(8,128)S(1)} fusion(bf16[16,128,1408]{2,1,0:T(8,128)(2,1)} %scatter_fusion, bf16[16,128,128]{2,1,0:T(8,128)(2,1)S(1)} %all-to-all-done, f32[16,128]{1,0:T(8,128)S(1)} %convert_reduce_fusion), kind=kOutput, calls=%fused_computation.14 | convolution fusion | flops 671875072 | bytes 6430720 | tf_op jit(solution)/shard_map/itd,idk->tk/dot_general | solution.py:161
  153.1 0.7 fusion.25.fresh_ref
  154.6 0.7 multiply_convert_fusion.query_ref
  155.3 4.4 %shard_map.109 = bf16[256,128]{1,0:T(8,128)(2,1)} custom-call(s32[1]{0:T(128)} %bitcast.4.length_ref, bf16[256,128]{1,0:T(8,128)(2,1)} %multiply_convert_fusion.query_ref, bf16[4096,128]{1,0:T(8,128)(2,1)} %bitcast.104, bf16[4096,128]{1,0:T(8,128)(2,1)} %bitcast.105, bf16[128,256]{1,0:T(8,128)(2,1)} %fusion.25.fresh_ref), custom_call_target="tpu_custom_call" | custom-call | flops 553648128 | bytes 2293760 | tf_op jit(solution)/shard_map/pallas_call | solution.py:76
  159.7 0.9 reshape.310
  160.6 1.3 convolution_bitcast_fusion
  162.0 1.1 broadcast_in_dim.98
  163.1 17.4 %all-to-all-start.1 = ((bf16[16,136,256]{2,1,0:T(8,128)(2,1)}), bf16[16,136,256]{2,1,0:T(8,128)(2,1)S(1)}, u32[]{:S(2)}, u32[]{:S(2)}) async-start(bf16[16,136,256]{2,1,0:T(8,128)(2,1)} %broadcast_in_dim.98), calls=%async_computation.1 | async-start | bytes 2228224 | tf_op jit(solution)/shard_map/all_to_all | solution.py:35
  181.2 14.8 %all-to-all-done.1 = bf16[16,136,256]{2,1,0:T(8,128)(2,1)S(1)} async-done(((bf16[16,136,256]{2,1,0:T(8,128)(2,1)}), bf16[16,136,256]{2,1,0:T(8,128)(2,1)S(1)}, u32[]{:S(2)}, u32[]{:S(2)}) %all-to-all-start.1) | async-done | bytes 1114144 | tf_op jit(solution)/shard_map/all_to_all | solution.py:35
  197.3 6.1 %fusion.15 = f32[2048,128]{1,0:T(8,128)S(1)} fusion(bf16[2048,2,8]{0,2,1:T(8,128)(2,1)S(1)} %convert_convert_fusion, bf16[2048,2,128]{2,0,1:T(8,128)(2,1)S(1)} %copy.42, f32[2048,2]{0,1:T(2,128)S(1)} %bitcast.109, bf16[8,1,128,128]{3,2,1,0:T(8,128)(2,1)S(1)} %copy-done), kind=kOutput, calls=%fused_computation.15 | convolution fusion | flops 1078722560 | bytes 2441216 | tf_op jit(solution)/shard_map/tsehk,ehko->tso/dot_general | solution.py:223
  203.4 7.5 %all_to_all.20 = f32[2,1024,128]{2,1,0:T(8,128)S(1)} all-to-all(f32[2,1024,128]{2,1,0:T(8,128)S(1)} %bitcast.106), channel_id=1, replica_groups=mesh['gx'=16,'zz'=8,'cc'=2] {'cc'}, dimensions={0} | all-to-all | bytes 2097152 | tf_op jit(solution)/shard_map/all_to_all | solution.py:22
  211.1 19.7 %all_to_all.21 = f32[8,128,128]{2,1,0:T(8,128)S(1)} all-to-all(f32[8,128,128]{2,1,0:T(8,128)S(1)} %bitcast.103), channel_id=1, replica_groups=mesh['gx'=16,'zz'=8,'cc'=2] {'zz'}, dimensions={0} | all-to-all | bytes 1048576 | tf_op jit(solution)/shard_map/all_to_all | solution.py:22
  (57 shorter events, 5.6 us)
Async XLA Ops:
  0.0 197.3 %copy-start = (bf16[8,1,128,128]{3,2,1,0:T(8,128)(2,1)S(1)}, bf16[8,1,128,128]{3,2,1,0:T(8,128)(2,1)}, u32[]{:S(2)}) copy-start(bf16[8,1,128,128]{3,2,1,0:T(8,128)(2,1)} %param.16) | copy-start | bytes 786436
  3.6 47.7 %collective-permute-start = (bf16[128,1408]{1,0:T(8,128)(2,1)S(1)}, bf16[128,1408]{1,0:T(8,128)(2,1)}, u32[]{:S(2)}, u32[]{:S(2)}) collective-permute-start(bf16[128,1408]{1,0:T(8,128)(2,1)S(1)} %concatenate.6), channel_id=1, source_target_pairs={{0,16},{16,32},{32,48},{48,64},{64,80},{80,96},{96,112},{112,128},... | collective-permute-start | bytes 1081352 | tf_op jit(solution)/shard_map/ppermute | solution.py:141
  5.8 51.0 %collective-permute-start.1 = (bf16[128,1408]{1,0:T(8,128)(2,1)S(1)}, bf16[128,1408]{1,0:T(8,128)(2,1)S(1)}, u32[]{:S(2)}, u32[]{:S(2)}) collective-permute-start(bf16[128,1408]{1,0:T(8,128)(2,1)S(1)} %concatenate.6), channel_id=1, source_target_pairs={{0,32},{16,48},{32,64},{48,80},{64,96},{80,112},{96,128},{112,144}... | collective-permute-start | bytes 1081352 | tf_op jit(solution)/shard_map/ppermute | solution.py:141
  8.4 51.5 %collective-permute-start.2 = (bf16[128,1408]{1,0:T(8,128)(2,1)S(1)}, bf16[128,1408]{1,0:T(8,128)(2,1)S(1)}, u32[]{:S(2)}, u32[]{:S(2)}) collective-permute-start(bf16[128,1408]{1,0:T(8,128)(2,1)S(1)} %concatenate.6), channel_id=1, source_target_pairs={{0,48},{16,64},{32,80},{48,96},{64,112},{80,128},{96,144},{112,160... | collective-permute-start | bytes 1081352 | tf_op jit(solution)/shard_map/ppermute | solution.py:141
  10.4 52.1 %collective-permute-start.3 = (bf16[128,1408]{1,0:T(8,128)(2,1)S(1)}, bf16[128,1408]{1,0:T(8,128)(2,1)S(1)}, u32[]{:S(2)}, u32[]{:S(2)}) collective-permute-start(bf16[128,1408]{1,0:T(8,128)(2,1)S(1)} %concatenate.6), channel_id=1, source_target_pairs={{0,64},{16,80},{32,96},{48,112},{64,128},{80,144},{96,160},{112,17... | collective-permute-start | bytes 1081352 | tf_op jit(solution)/shard_map/ppermute | solution.py:141
  11.6 53.7 %collective-permute-start.4 = (bf16[128,1408]{1,0:T(8,128)(2,1)S(1)}, bf16[128,1408]{1,0:T(8,128)(2,1)S(1)}, u32[]{:S(2)}, u32[]{:S(2)}) collective-permute-start(bf16[128,1408]{1,0:T(8,128)(2,1)S(1)} %concatenate.6), channel_id=1, source_target_pairs={{0,80},{16,96},{32,112},{48,128},{64,144},{80,160},{96,176},{112,1... | collective-permute-start | bytes 1081352 | tf_op jit(solution)/shard_map/ppermute | solution.py:141
  39.1 110.4 %all-to-all-start = ((bf16[16,128,128]{2,1,0:T(8,128)(2,1)}), bf16[16,128,128]{2,1,0:T(8,128)(2,1)S(1)}, u32[]{:S(2)}, u32[]{:S(2)}) async-start(bf16[16,128,128]{2,1,0:T(8,128)(2,1)} %broadcast_select_fusion.1), calls=%async_computation | async-start | bytes 1048576 | tf_op jit(solution)/shard_map/all_to_all | solution.py:150
  51.2 18.7 %collective-permute-start.5 = (bf16[128,1408]{1,0:T(8,128)(2,1)S(1)}, bf16[128,1408]{1,0:T(8,128)(2,1)S(1)}, u32[]{:S(2)}, u32[]{:S(2)}) collective-permute-start(bf16[128,1408]{1,0:T(8,128)(2,1)S(1)} %concatenate.6), channel_id=1, source_target_pairs={{0,96},{16,112},{32,128},{48,144},{64,160},{80,176},{96,192},{112,... | collective-permute-start | bytes 1081352 | tf_op jit(solution)/shard_map/ppermute | solution.py:141
  56.8 19.4 %collective-permute-start.6 = (bf16[128,1408]{1,0:T(8,128)(2,1)S(1)}, bf16[128,1408]{1,0:T(8,128)(2,1)S(1)}, u32[]{:S(2)}, u32[]{:S(2)}) collective-permute-start(bf16[128,1408]{1,0:T(8,128)(2,1)S(1)} %concatenate.6), channel_id=1, source_target_pairs={{0,112},{16,128},{32,144},{48,160},{64,176},{80,192},{96,208},{112... | collective-permute-start | bytes 1081352 | tf_op jit(solution)/shard_map/ppermute | solution.py:141
  59.9 22.1 %collective-permute-start.7 = (bf16[128,1408]{1,0:T(8,128)(2,1)S(1)}, bf16[128,1408]{1,0:T(8,128)(2,1)S(1)}, u32[]{:S(2)}, u32[]{:S(2)}) collective-permute-start(bf16[128,1408]{1,0:T(8,128)(2,1)S(1)} %concatenate.6), channel_id=1, source_target_pairs={{0,128},{16,144},{32,160},{48,176},{64,192},{80,208},{96,224},{112... | collective-permute-start | bytes 1081352 | tf_op jit(solution)/shard_map/ppermute | solution.py:141
  62.5 27.5 %collective-permute-start.8 = (bf16[128,1408]{1,0:T(8,128)(2,1)S(1)}, bf16[128,1408]{1,0:T(8,128)(2,1)S(1)}, u32[]{:S(2)}, u32[]{:S(2)}) collective-permute-start(bf16[128,1408]{1,0:T(8,128)(2,1)S(1)} %concatenate.6), channel_id=1, source_target_pairs={{0,144},{16,160},{32,176},{48,192},{64,208},{80,224},{96,240},{112... | collective-permute-start | bytes 1081352 | tf_op jit(solution)/shard_map/ppermute | solution.py:141
  65.3 38.0 %collective-permute-start.9 = (bf16[128,1408]{1,0:T(8,128)(2,1)S(1)}, bf16[128,1408]{1,0:T(8,128)(2,1)S(1)}, u32[]{:S(2)}, u32[]{:S(2)}) collective-permute-start(bf16[128,1408]{1,0:T(8,128)(2,1)S(1)} %concatenate.6), channel_id=1, source_target_pairs={{0,160},{16,176},{32,192},{48,208},{64,224},{80,240},{96,0},{112,1... | collective-permute-start | bytes 1081352 | tf_op jit(solution)/shard_map/ppermute | solution.py:141
  69.9 35.7 %collective-permute-start.10 = (bf16[128,1408]{1,0:T(8,128)(2,1)S(1)}, bf16[128,1408]{1,0:T(8,128)(2,1)S(1)}, u32[]{:S(2)}, u32[]{:S(2)}) collective-permute-start(bf16[128,1408]{1,0:T(8,128)(2,1)S(1)} %concatenate.6), channel_id=1, source_target_pairs={{0,176},{16,192},{32,208},{48,224},{64,240},{80,0},{96,16},{112,32... | collective-permute-start | bytes 1081352 | tf_op jit(solution)/shard_map/ppermute | solution.py:141
  76.1 30.3 %collective-permute-start.11 = (bf16[128,1408]{1,0:T(8,128)(2,1)S(1)}, bf16[128,1408]{1,0:T(8,128)(2,1)S(1)}, u32[]{:S(2)}, u32[]{:S(2)}) collective-permute-start(bf16[128,1408]{1,0:T(8,128)(2,1)S(1)} %concatenate.6), channel_id=1, source_target_pairs={{0,192},{16,208},{32,224},{48,240},{64,0},{80,16},{96,32},{112,48}... | collective-permute-start | bytes 1081352 | tf_op jit(solution)/shard_map/ppermute | solution.py:141
  82.0 34.4 %collective-permute-start.12 = (bf16[128,1408]{1,0:T(8,128)(2,1)S(1)}, bf16[128,1408]{1,0:T(8,128)(2,1)S(1)}, u32[]{:S(2)}, u32[]{:S(2)}) collective-permute-start(bf16[128,1408]{1,0:T(8,128)(2,1)S(1)} %concatenate.6), channel_id=1, source_target_pairs={{0,208},{16,224},{32,240},{48,0},{64,16},{80,32},{96,48},{112,64},... | collective-permute-start | bytes 1081352 | tf_op jit(solution)/shard_map/ppermute | solution.py:141
  89.9 28.1 %collective-permute-start.13 = (bf16[128,1408]{1,0:T(8,128)(2,1)S(1)}, bf16[128,1408]{1,0:T(8,128)(2,1)S(1)}, u32[]{:S(2)}, u32[]{:S(2)}) collective-permute-start(bf16[128,1408]{1,0:T(8,128)(2,1)S(1)} %concatenate.6), channel_id=1, source_target_pairs={{0,224},{16,240},{32,0},{48,16},{64,32},{80,48},{96,64},{112,80},{... | collective-permute-start | bytes 1081352 | tf_op jit(solution)/shard_map/ppermute | solution.py:141
  103.3 22.4 %collective-permute-start.14 = (bf16[128,1408]{1,0:T(8,128)(2,1)S(1)}, bf16[128,1408]{1,0:T(8,128)(2,1)S(1)}, u32[]{:S(2)}, u32[]{:S(2)}) collective-permute-start(bf16[128,1408]{1,0:T(8,128)(2,1)S(1)} %concatenate.6), channel_id=1, source_target_pairs={{0,240},{16,0},{32,16},{48,32},{64,48},{80,64},{96,80},{112,96},{1... | collective-permute-start | bytes 1081352 | tf_op jit(solution)/shard_map/ppermute | solution.py:141
  153.0 27.5 %copy-start.1 = (s32[2048,2]{0,1:T(2,128)S(1)}, s32[2048,2]{0,1:T(2,128)}, u32[]{:S(2)}) copy-start(s32[2048,2]{0,1:T(2,128)} %param.21) | copy-start | bytes 49156
  163.1 32.9 %all-to-all-start.1 = ((bf16[16,136,256]{2,1,0:T(8,128)(2,1)}), bf16[16,136,256]{2,1,0:T(8,128)(2,1)S(1)}, u32[]{:S(2)}, u32[]{:S(2)}) async-start(bf16[16,136,256]{2,1,0:T(8,128)(2,1)} %broadcast_in_dim.98), calls=%async_computation.1 | async-start | bytes 2228224 | tf_op jit(solution)/shard_map/all_to_all | solution.py:35

commit v8 on v7

--- a/solution.py
+++ b/solution.py
@@ -135,15 +135,8 @@
         ],
         axis=1,
     )
-    pieces = [None] * members
-    pieces[0] = weight_piece
-    for offset in range(1, members):
-        pieces[offset] = lax.ppermute(
-            weight_piece, "gx", [(source, (source + offset) % members) for source in range(members)]
-        )
-    received = jnp.stack(pieces)
-    sources = (slot_index - jnp.arange(members, dtype=jnp.int32)) % members
-    head_weights = jnp.zeros_like(received).at[sources].set(received)
+    head_weights = gather_rows(weight_piece, "gx")
+    head_weights = head_weights.reshape(members, local_width, weight_piece.shape[1])
     gathered = lax.all_gather(tokens, TOKEN_AXES, axis=0, tiled=True)
     inverse = jnp.zeros((requests,), jnp.int32).at[deal].set(jnp.arange(requests, dtype=jnp.int32))
     by_slot = jnp.take(gathered.reshape(requests, new_len, local_width), inverse, axis=0)

time: 232 us -> 207 us (0.89)
  waiting for transfers between devices: 48.5 us -> 98.8 us
  starting transfers between devices: 61.3 us -> 20 us
  local copies, waits for them, and re-layouts: 47.3 us -> 11.7 us
  blocking collectives: 50.8 us -> 53.2 us
    all_to_all x1 -> x2, waiting for transfers between devices: 14.8 us -> 89.6 us  [gather_rows(): gathered = lax.all_to_all(copies, axis_name, 0, 0, tiled=True)]
    ppermute x15 -> x0, starting transfers between devices: 38.1 us -> none  [per_device_body(): lax.ppermute(weight_piece, 'gx', [(source, (source + offset) % members) f...]
    ppermute x15 -> x0, waiting for transfers between devices: 33.7 us -> none  [per_device_body(): lax.ppermute(weight_piece, 'gx', [(source, (source + offset) % members) f...]
    scatter x1 -> x0, local copies, waits for them, and re-layouts: 18.4 us -> none  [per_device_body(): head_weights = jnp.zeros_like(received).at[sources].set(received)]
    unnamed x23 -> x21, local copies, waits for them, and re-layouts: 13.5 us -> 0.47 us
    all_to_all x1, waiting for transfers between devices: 0.01 us -> 9.2 us  [per_device_body(): own_tokens = lax.all_to_all(by_slot, 'gx', 0, 0, tiled=True)]
    all_to_all x1 -> x2, starting transfers between devices: 17.4 us -> 13.2 us  [gather_rows(): gathered = lax.all_to_all(copies, axis_name, 0, 0, tiled=True)]
    broadcast_in_dim x2 -> x0, local copies, waits for them, and re-layouts: 3.87 us -> none  [the longest x1 3.09 us: per_device_body(): head_weights = jnp.zeros_like(received).at[sources].set(received)]
  transfers between devices with their start and end apart: 17 -> 3, of which waited for: 9 -> 3; matrix products, arithmetic and copies ran while one was open for 19% -> 2% of each run, Pallas kernels for 0% -> 0%
where the time goes in v8:
time: 207 us
  waiting for transfers between devices  98.8 us (48%)
  blocking collectives  53.2 us (26%)
  starting transfers between devices  20 us (10%)
  local copies, waits for them, and re-layouts  11.7 us (6%)
  matrix products  10.7 us (5%)
  other arithmetic  6.2 us (3%)
  Pallas kernels  4.4 us (2%)
    all_to_all x2, waiting for transfers between devices, gather_rows(): gathered = lax.all_to_all(copies, axis_name, 0, 0, tiled=True)  89.6 us
    all_to_all x2, blocking collectives, scatter_sum(): lax.all_to_all(part.reshape((members, part.shape[0] // members) + part.sh...  30.1 us
    all_gather x1, blocking collectives, per_device_body(): gathered = lax.all_gather(tokens, TOKEN_AXES, axis=0, tiled=True)  23.1 us
    all_to_all x2, starting transfers between devices, gather_rows(): gathered = lax.all_to_all(copies, axis_name, 0, 0, tiled=True)  13.2 us
    all_to_all x1, waiting for transfers between devices, per_device_body(): own_tokens = lax.all_to_all(by_slot, 'gx', 0, 0, tiled=True)  9.2 us
    all_to_all x1, starting transfers between devices, per_device_body(): own_tokens = lax.all_to_all(by_slot, 'gx', 0, 0, tiled=True)  6.75 us
    dot_general x1, matrix products, per_device_body(): jnp.einsum('tsehk,ehko->tso', routed_attended, expert_output_weight, pref...  6.08 us
    pallas_call x1, Pallas kernels, attend(): pl.pallas_call(attend_kernel, out_shape=jax.ShapeDtypeStruct((rows, head_...  4.4 us
  transfers between devices with their start and end apart: 3, of which 3 were waited for; matrix products, arithmetic and copies ran while one was open for 2% of the time, Pallas kernels for 0%

profile of v8, /device:TPU:1, one launch (start us, length us, event | category | flops | bytes accessed | tf_op | source)
XLA Modules:
  0.0 206.7 jit_solution(17805365917484439229)
XLA Ops:
  0.0 0.0 copy-start
  0.0 0.0 copy-start.3
  0.0 0.7 compare_select_fusion.2
  0.7 0.6 scatter_custom_fusion
  1.4 0.0 copy-start.4
  1.4 0.0 copy-start.5
  1.4 0.0 copy-start.6
  1.4 23.1 %all_gather.3 = bf16[2048,128]{1,0:T(8,128)(2,1)S(1)} all-gather(bf16[128,128]{1,0:T(8,128)(2,1)} %param.11), channel_id=1, replica_groups=mesh['gx'=16,'zz'=8,'cc'=2] {'zz','cc'}, dimensions={0}, use_global_device_ids=true | all-gather | bytes 557056 | tf_op jit(solution)/shard_map/all_gather | solution.py:140
  24.5 0.6 gather_fusion.1
  25.2 0.9 broadcast_select_fusion.1
  26.1 6.8 %all-to-all-start = ((bf16[16,128,128]{2,1,0:T(8,128)(2,1)}), bf16[16,128,128]{2,1,0:T(8,128)(2,1)S(1)}, u32[]{:S(2)}, u32[]{:S(2)}) async-start(bf16[16,128,128]{2,1,0:T(8,128)(2,1)} %broadcast_select_fusion.1), calls=%async_computation | async-start | bytes 1048576 | tf_op jit(solution)/shard_map/all_to_all | solution.py:143
  32.9 0.0 copy-done.3
  32.9 0.2 copy.35
  33.1 0.0 copy-done.4
  33.1 0.1 copy.36
  33.2 0.0 copy-done.5
  33.2 0.0 copy-done.6
  33.2 0.4 concatenate.6
  33.6 0.2 copy.37
  33.8 9.2 %all-to-all-done = bf16[16,128,128]{2,1,0:T(8,128)(2,1)S(1)} async-done(((bf16[16,128,128]{2,1,0:T(8,128)(2,1)}), bf16[16,128,128]{2,1,0:T(8,128)(2,1)S(1)}, u32[]{:S(2)}, u32[]{:S(2)}) %all-to-all-start) | async-done | bytes 524320 | tf_op jit(solution)/shard_map/all_to_all | solution.py:143
  43.0 3.2 %broadcast_in_dim.99 = bf16[16,128,1408]{2,1,0:T(8,128)(2,1)} broadcast(bf16[128,1408]{1,0:T(8,128)(2,1)S(1)} %copy.37), dimensions={1,2} | broadcast | bytes 6127616 | tf_op jit(solution)/shard_map/broadcast_in_dim | solution.py:34
  46.2 0.0 copy-start.1
  46.2 0.0 copy-start.7
  46.2 0.0 copy-start.2
  46.2 4.7 %all-to-all-start.1 = ((bf16[16,128,1408]{2,1,0:T(8,128)(2,1)}), bf16[16,128,1408]{2,1,0:T(8,128)(2,1)}, u32[]{:S(2)}, u32[]{:S(2)}) async-start(bf16[16,128,1408]{2,1,0:T(8,128)(2,1)} %broadcast_in_dim.99), calls=%async_computation.1 | async-start | bytes 11534336 | tf_op jit(solution)/shard_map/all_to_all | solution.py:35
  51.0 0.1 reshape.255
  51.1 0.1 reshape.254
  51.1 0.6 dynamic-slice.7
  52.4 0.0 copy-done.1
  52.4 0.7 gather_fusion
  53.1 0.0 copy-done.7
  53.1 0.6 dynamic-slice.8
  53.7 0.0 copy-done.2
  53.7 0.1 copy.34
  54.5 0.1 broadcast_bitcast_fusion
  54.6 0.2 fusion.19
  54.8 0.1 mul.97.clone
  54.8 0.2 mul.98
  55.0 77.4 %all-to-all-done.1 = bf16[16,128,1408]{2,1,0:T(8,128)(2,1)} async-done(((bf16[16,128,1408]{2,1,0:T(8,128)(2,1)}), bf16[16,128,1408]{2,1,0:T(8,128)(2,1)}, u32[]{:S(2)}, u32[]{:S(2)}) %all-to-all-start.1) | async-done | bytes 5767200 | tf_op jit(solution)/shard_map/all_to_all | solution.py:35
  132.4 1.4 convert_reduce_fusion
  133.8 3.3 %fusion.12 = f32[128,1280]{1,0:T(8,128)S(1)} fusion(bf16[16,128,1408]{2,1,0:T(8,128)(2,1)} %all-to-all-done.1, bf16[16,128,128]{2,1,0:T(8,128)(2,1)S(1)} %all-to-all-done, f32[16,128]{1,0:T(8,128)S(1)} %convert_reduce_fusion), kind=kOutput, calls=%fused_computation.13 | convolution fusion | flops 671875072 | bytes 6430720 | tf_op jit(solution)/shard_map/itd,idk->tk/dot_general | solution.py:154
  137.2 0.7 fusion.25.fresh_ref
  138.0 1.3 convolution_bitcast_fusion
  139.3 0.1 select_reduce_fusion
  139.4 0.1 copy.47
  139.5 0.4 multiply_reduce_fusion
  139.9 0.7 multiply_convert_fusion.query_ref
  140.6 4.4 %shard_map.109 = bf16[256,128]{1,0:T(8,128)(2,1)} custom-call(s32[1]{0:T(128)} %bitcast.4.length_ref, bf16[256,128]{1,0:T(8,128)(2,1)} %multiply_convert_fusion.query_ref, bf16[4096,128]{1,0:T(8,128)(2,1)} %bitcast.67, bf16[4096,128]{1,0:T(8,128)(2,1)} %bitcast.68, bf16[128,256]{1,0:T(8,128)(2,1)} %fusion.25.fresh_ref), custom_call_target="tpu_custom_call" | custom-call | flops 553648128 | bytes 2293760 | tf_op jit(solution)/shard_map/pallas_call | solution.py:76
  145.0 0.9 reshape.262
  145.9 1.1 broadcast_in_dim.100
  147.0 8.5 %all-to-all-start.2 = ((bf16[16,136,256]{2,1,0:T(8,128)(2,1)}), bf16[16,136,256]{2,1,0:T(8,128)(2,1)S(1)}, u32[]{:S(2)}, u32[]{:S(2)}) async-start(bf16[16,136,256]{2,1,0:T(8,128)(2,1)} %broadcast_in_dim.100), calls=%async_computation.2 | async-start | bytes 2228224 | tf_op jit(solution)/shard_map/all_to_all | solution.py:35
  155.5 0.6 gather_fusion.3
  156.2 12.2 %all-to-all-done.2 = bf16[16,136,256]{2,1,0:T(8,128)(2,1)S(1)} async-done(((bf16[16,136,256]{2,1,0:T(8,128)(2,1)}), bf16[16,136,256]{2,1,0:T(8,128)(2,1)S(1)}, u32[]{:S(2)}, u32[]{:S(2)}) %all-to-all-start.2) | async-done | bytes 1114144 | tf_op jit(solution)/shard_map/all_to_all | solution.py:35
  168.4 0.6 gather_fusion.2
  169.0 0.2 broadcast_select_fusion
  169.2 0.1 slice.69
  169.3 0.3 reshape.398
  169.6 0.1 copy.41
  169.7 0.0 copy-done
  169.7 6.1 %fusion.15 = f32[2048,128]{1,0:T(8,128)S(1)} fusion(bf16[2048,2,8]{0,2,1:T(8,128)(2,1)S(1)} %convert_convert_fusion, bf16[2048,2,128]{2,0,1:T(8,128)(2,1)S(1)} %copy.41, f32[2048,2]{0,1:T(2,128)S(1)} %bitcast.73, bf16[8,1,128,128]{3,2,1,0:T(8,128)(2,1)S(1)} %copy-done), kind=kOutput, calls=%fused_computation.14 | convolution fusion | flops 1078722560 | bytes 2441216 | tf_op jit(solution)/shard_map/tsehk,ehko->tso/dot_general | solution.py:216
  175.8 10.2 %all_to_all.25 = f32[2,1024,128]{2,1,0:T(8,128)S(1)} all-to-all(f32[2,1024,128]{2,1,0:T(8,128)S(1)} %bitcast.69), channel_id=1, replica_groups=mesh['gx'=16,'zz'=8,'cc'=2] {'cc'}, dimensions={0} | all-to-all | bytes 2097152 | tf_op jit(solution)/shard_map/all_to_all | solution.py:22
  186.1 0.1 reduce_sum.61
  186.2 19.9 %all_to_all.26 = f32[8,128,128]{2,1,0:T(8,128)S(1)} all-to-all(f32[8,128,128]{2,1,0:T(8,128)S(1)} %bitcast.66), channel_id=1, replica_groups=mesh['gx'=16,'zz'=8,'cc'=2] {'zz'}, dimensions={0} | all-to-all | bytes 1048576 | tf_op jit(solution)/shard_map/all_to_all | solution.py:22
  206.0 0.6 reduce_sum.62
  (23 shorter events, 0.2 us)
Async XLA Ops:
  0.0 169.7 %copy-start = (bf16[8,1,128,128]{3,2,1,0:T(8,128)(2,1)S(1)}, bf16[8,1,128,128]{3,2,1,0:T(8,128)(2,1)}, u32[]{:S(2)}) copy-start(bf16[8,1,128,128]{3,2,1,0:T(8,128)(2,1)} %param.16) | copy-start | bytes 786436
  0.0 32.9 %copy-start.3 = (bf16[8,128,1,128]{3,1,2,0:T(8,128)(2,1)S(1)}, bf16[8,128,1,128]{3,1,2,0:T(8,128)(2,1)}, u32[]{:S(2)}) copy-start(bf16[8,128,1,128]{3,1,2,0:T(8,128)(2,1)} %param.14) | copy-start | bytes 786436
  1.4 31.7 %copy-start.4 = (bf16[128,1,256]{2,0,1:T(8,128)(2,1)S(1)}, bf16[128,1,256]{2,0,1:T(8,128)(2,1)}, u32[]{:S(2)}) copy-start(bf16[128,1,256]{2,0,1:T(8,128)(2,1)} %param.15) | copy-start | bytes 196612
  1.4 31.8 %copy-start.5 = (bf16[128,8]{0,1:T(8,128)(2,1)S(1)}, bf16[128,8]{0,1:T(8,128)(2,1)}, u32[]{:S(2)}) copy-start(bf16[128,8]{0,1:T(8,128)(2,1)} %param.13) | copy-start | bytes 6148
  1.4 31.8 %copy-start.6 = (bf16[128]{0:T(256)(128)(2,1)S(1)}, bf16[128]{0:T(256)(128)(2,1)}, u32[]{:S(2)}) copy-start(bf16[128]{0:T(256)(128)(2,1)} %param.12) | copy-start | bytes 772
  26.1 16.9 %all-to-all-start = ((bf16[16,128,128]{2,1,0:T(8,128)(2,1)}), bf16[16,128,128]{2,1,0:T(8,128)(2,1)S(1)}, u32[]{:S(2)}, u32[]{:S(2)}) async-start(bf16[16,128,128]{2,1,0:T(8,128)(2,1)} %broadcast_select_fusion.1), calls=%async_computation | async-start | bytes 1048576 | tf_op jit(solution)/shard_map/all_to_all | solution.py:143
  46.2 6.2 %copy-start.1 = (s32[16]{0:T(128)S(1)}, s32[16]{0:T(128)}, u32[]{:S(2)}) copy-start(s32[16]{0:T(128)} %param.20) | copy-start | bytes 196
  46.2 6.9 %copy-start.7 = (s32[16]{0:T(128)S(1)}, s32[16]{0:T(128)}, u32[]{:S(2)}) copy-start(s32[16]{0:T(128)} %param.19) | copy-start | bytes 196
  46.2 7.4 %copy-start.2 = (s32[2048,2]{0,1:T(2,128)S(1)}, s32[2048,2]{0,1:T(2,128)}, u32[]{:S(2)}) copy-start(s32[2048,2]{0,1:T(2,128)} %param.21) | copy-start | bytes 49156
  46.2 86.2 %all-to-all-start.1 = ((bf16[16,128,1408]{2,1,0:T(8,128)(2,1)}), bf16[16,128,1408]{2,1,0:T(8,128)(2,1)}, u32[]{:S(2)}, u32[]{:S(2)}) async-start(bf16[16,128,1408]{2,1,0:T(8,128)(2,1)} %broadcast_in_dim.99), calls=%async_computation.1 | async-start | bytes 11534336 | tf_op jit(solution)/shard_map/all_to_all | solution.py:35
  147.0 21.4 %all-to-all-start.2 = ((bf16[16,136,256]{2,1,0:T(8,128)(2,1)}), bf16[16,136,256]{2,1,0:T(8,128)(2,1)S(1)}, u32[]{:S(2)}, u32[]{:S(2)}) async-start(bf16[16,136,256]{2,1,0:T(8,128)(2,1)} %broadcast_in_dim.100), calls=%async_computation.2 | async-start | bytes 2228224 | tf_op jit(solution)/shard_map/all_to_all | solution.py:35

commit v9 on v5

--- a/solution.py
+++ b/solution.py
@@ -120,23 +120,38 @@
     )(ordered, gain.reshape(1, width), jnp.transpose(w_router), weight, route, route_t)
 
 
-def attend_kernel(length_ref, query_ref, cache_k_ref, cache_v_ref, fresh_ref, out_ref):
-    rows, head_dim = query_ref.shape
-    fresh_len = fresh_ref.shape[0]
-    top_count = rows // fresh_len
+def attend_kernel(length_ref, blocks_ref, cache_k_ref, cache_v_ref, out_ref):
+    members, block_rows, packed_cols = blocks_ref.shape
+    rows = block_rows - EXTRA_ROWS
+    head_dim = cache_k_ref.shape[1]
+    full_width = members * LANES
+    summed = blocks_ref[0]
+    for member in range(1, members):
+        summed = summed + blocks_ref[member]
+    partials = summed[0:rows]
+    extra = summed[rows:block_rows]
+    extra_t = jnp.transpose(extra)
+    inverse_col = lax.rsqrt(extra_t[2 * rows : 3 * rows, 0:1] / full_width + norm_eps)
+    inverse_row = lax.rsqrt(extra[0:1, 2 * rows : 3 * rows] / full_width + norm_eps)
+    gate_gap = extra[0:1, 0:rows] * inverse_row - extra[0:1, rows : 2 * rows] * inverse_row
+    gate_row = jnp.concatenate([jax.nn.sigmoid(gate_gap), jax.nn.sigmoid(-gate_gap)], axis=1)
+    gate_row = gate_row.astype(jnp.bfloat16).astype(jnp.float32)
+    scaled = partials * inverse_col
+    query = jnp.concatenate(
+        [scaled[:, 0:head_dim], scaled[:, head_dim : 2 * head_dim]], axis=0
+    ).astype(jnp.bfloat16)
+    fresh_keys = scaled[:, 2 * head_dim : 3 * head_dim].astype(jnp.bfloat16)
+    fresh_values = scaled[:, 3 * head_dim : 4 * head_dim].astype(jnp.bfloat16)
     score_scale = head_dim ** (-0.5)
     contract_last = (((1,), (1,)), ((), ()))
-    query = query_ref[...]
     cached = lax.dot_general(query, cache_k_ref[...], contract_last, preferred_element_type=jnp.float32)
     cached = cached * score_scale
     key_col = lax.broadcasted_iota(jnp.int32, cached.shape, 1)
     cached = jnp.where(key_col < length_ref[0], cached, masked_score)
-    fresh_keys = fresh_ref[:, 0:head_dim]
-    fresh_values = fresh_ref[:, head_dim : 2 * head_dim]
     fresh = lax.dot_general(query, fresh_keys, contract_last, preferred_element_type=jnp.float32)
     fresh = fresh * score_scale
     fresh_col = lax.broadcasted_iota(jnp.int32, fresh.shape, 1)
-    query_token = lax.broadcasted_iota(jnp.int32, fresh.shape, 0) // top_count
+    query_token = lax.broadcasted_iota(jnp.int32, fresh.shape, 0) % rows
     fresh = jnp.where(fresh_col <= query_token, fresh, masked_score)
     top = jnp.maximum(
         jnp.max(cached, axis=1, keepdims=True), jnp.max(fresh, axis=1, keepdims=True)
@@ -146,32 +161,45 @@
     denominator = jnp.sum(cached_weights, axis=1, keepdims=True) + jnp.sum(
         fresh_weights, axis=1, keepdims=True
     )
-    summed = jnp.dot(
+    attended = jnp.dot(
         cached_weights.astype(jnp.bfloat16), cache_v_ref[...], preferred_element_type=jnp.float32
     ) + jnp.dot(fresh_weights.astype(jnp.bfloat16), fresh_values, preferred_element_type=jnp.float32)
-    out_ref[...] = (summed / denominator).astype(jnp.bfloat16)
-
-
-def attend(length, query, cache_k, cache_v, fresh):
-    rows, head_dim = query.shape
-    span = cache_k.shape[0]
+    attended = (attended / denominator).astype(jnp.bfloat16)
+    first_slot = attended[0:rows]
+    second_slot = attended[rows : 2 * rows]
+    extra_row = lax.broadcasted_iota(jnp.int32, (EXTRA_ROWS, 2 * rows), 0)
+    gate_block = jnp.where(
+        extra_row == 0, jnp.broadcast_to(gate_row, (EXTRA_ROWS, 2 * rows)), 0.0
+    ).astype(jnp.bfloat16)
+    for member in range(out_ref.shape[0]):
+        out_ref[member, 0:rows, 0:head_dim] = first_slot
+        out_ref[member, 0:rows, head_dim : 2 * head_dim] = second_slot
+        out_ref[member, rows:block_rows, :] = gate_block
+
+
+def attend(length, blocks, cache_k, cache_v):
+    members, block_rows, packed_cols = blocks.shape
+    rows = block_rows - EXTRA_ROWS
+    span, head_dim = cache_k.shape
     full = lambda shape: pl.BlockSpec(shape, lambda i, length_ref: (0,) * len(shape))
-    keys = span + fresh.shape[0]
+    out_shape = (members, block_rows, 2 * head_dim)
+    keys = span + rows
+    query_rows = 2 * rows
     return pl.pallas_call(
         attend_kernel,
-        out_shape=jax.ShapeDtypeStruct((rows, head_dim), jnp.bfloat16),
+        out_shape=jax.ShapeDtypeStruct(out_shape, jnp.bfloat16),
         grid_spec=pltpu.PrefetchScalarGridSpec(
             num_scalar_prefetch=1,
             grid=(1,),
-            in_specs=[full(query.shape), full(cache_k.shape), full(cache_v.shape), full(fresh.shape)],
-            out_specs=full((rows, head_dim)),
+            in_specs=[full(blocks.shape), full(cache_k.shape), full(cache_v.shape)],
+            out_specs=full(out_shape),
         ),
         cost_estimate=pl.CostEstimate(
-            flops=4 * rows * keys * head_dim,
-            transcendentals=rows * keys,
-            bytes_accessed=2 * (2 * span * head_dim + 2 * rows * head_dim + fresh.size),
+            flops=4 * query_rows * keys * head_dim,
+            transcendentals=query_rows * keys,
+            bytes_accessed=4 * blocks.size + 4 * span * head_dim + 2 * members * block_rows * 2 * head_dim,
         ),
-    )(length.reshape(1), query, cache_k, cache_v, fresh)
+    )(length.reshape(1), blocks, cache_k, cache_v)
 
 
 def per_device(
@@ -216,41 +244,16 @@
     )
     query_cols = top_count * heads_local * head_dim
     keyval_cols = heads_local * 2 * head_dim
-    summed = scatter_sum(packed, "gx")
-    query_totals = summed[:new_len, :query_cols].reshape(new_len, top_count, heads_local, head_dim)
-    keyval_sums = summed[:new_len, query_cols : query_cols + keyval_cols].reshape(
-        new_len, heads_local, 2 * head_dim
-    )
-    chosen_sums = jnp.transpose(summed[new_len, : top_count * new_len].reshape(top_count, new_len))
-    square_sums = summed[new_len, top_count * new_len : (top_count + 1) * new_len]
-    inverse_root_mean = lax.rsqrt(square_sums / full_width + norm_eps)
-    chosen = chosen_sums * inverse_root_mean[:, None]
-    gate_gap = chosen[:, 0] - chosen[:, 1]
-    gate_weights = jnp.stack([jax.nn.sigmoid(gate_gap), jax.nn.sigmoid(-gate_gap)], axis=1).astype(
-        jnp.bfloat16
-    )
-    query_matrix = (query_totals * inverse_root_mean[:, None, None, None]).astype(jnp.bfloat16)
-    key_value_rows = (keyval_sums * inverse_root_mean[:, None, None]).astype(jnp.bfloat16)
-    query_rows = new_len * top_count
+    members = lax.axis_size("gx")
+    blocks = lax.all_to_all(
+        packed.reshape(members, packed.shape[0] // members, packed.shape[1]), "gx", 0, 0, tiled=True
+    )
     length = jnp.take(lengths, jnp.take(inverse, slot_index))
-    attended_output = attend(
-        length,
-        query_matrix.reshape(query_rows, head_dim),
-        cache_keys[0, 0],
-        cached_value_slots[0, 0],
-        key_value_rows.reshape(new_len, 2 * head_dim),
-    ).reshape(new_len, query_cols)
-    gate_row = jnp.transpose(gate_weights).reshape(1, top_count * new_len)
-    assert gate_row.shape[1] <= query_cols
-    extra_rows = 8
-    shipped = jnp.concatenate(
-        [
-            attended_output,
-            jnp.pad(gate_row, ((0, extra_rows - 1), (0, query_cols - gate_row.shape[1]))),
-        ],
-        axis=0,
-    )
-    all_shipped = gather_rows(shipped, "gx").reshape(requests, new_len + extra_rows, query_cols)
+    copies = attend(length, blocks, cache_keys[0, 0], cached_value_slots[0, 0])
+    extra_rows = EXTRA_ROWS
+    all_shipped = lax.all_to_all(copies, "gx", 0, 0, tiled=True).reshape(
+        requests, new_len + extra_rows, query_cols
+    )
     cores = lax.axis_size("cc")
     chips = lax.axis_size("zz")
     staged = jnp.arange(requests, dtype=jnp.int32).reshape(chips, cores).T.reshape(requests)

time: 180 us -> 176 us (0.978)
  other arithmetic: 8.6 us -> 4.41 us
  local copies, waits for them, and re-layouts: 9.97 us -> 7.84 us
  Pallas kernels: 11.9 us -> 13.9 us
    reduce_sum x3 -> x2, other arithmetic: 3.49 us -> 0.75 us  [scatter_sum(): return jnp.sum(blocks, axis=0)]
    pallas_call x1, Pallas kernels: 4.4 us -> 6.41 us  [attend(): pl.pallas_call(attend_kernel, out_shape=jax.ShapeDtypeStruct(out_shape, j...]
where the time goes in v9:
time: 176 us; the launch traced here: 175 us
  waiting for transfers between devices  70.2 us (40%)
  blocking collectives  49.9 us (28%)
  starting transfers between devices  21.4 us (12%)
  Pallas kernels  13.9 us (8%)
  local copies, waits for them, and re-layouts  7.84 us (4%)
  matrix products  6.08 us (3%)
  other arithmetic  4.41 us (3%)
    all_to_all x1, waiting for transfers between devices, per_device(): lax.all_to_all(packed.reshape(members, packed.shape[0] // members, packed...  55 us
    all_to_all x2, blocking collectives, scatter_sum(): lax.all_to_all(part.reshape((members, part.shape[0] // members) + part.sh...  27.2 us
    all_gather x1, blocking collectives, per_device(): gathered = lax.all_gather(tokens, TOKEN_AXES, axis=0, tiled=True)  22.7 us
    all_to_all x1, waiting for transfers between devices, per_device(): lax.all_to_all(copies, 'gx', 0, 0, tiled=True)  15.2 us
    all_to_all x1, starting transfers between devices, per_device(): lax.all_to_all(copies, 'gx', 0, 0, tiled=True)  14.4 us
    pallas_call x1, Pallas kernels, packed_partials(): pl.pallas_call(pack_kernel, out_shape=jax.ShapeDtypeStruct((requests * bl...  7.44 us
    all_to_all x1, starting transfers between devices, per_device(): lax.all_to_all(packed.reshape(members, packed.shape[0] // members, packed...  6.94 us
    pallas_call x1, Pallas kernels, attend(): pl.pallas_call(attend_kernel, out_shape=jax.ShapeDtypeStruct(out_shape, j...  6.41 us
  transfers between devices with their start and end apart: 2, of which 2 were waited for; matrix products, arithmetic and copies ran while one was open for 2% of the time, Pallas kernels for 0%

profile of v9, /device:TPU:1, one launch (start us, length us, event | category | flops | bytes accessed | tf_op | source)
XLA Modules:
  0.0 175.2 jit_solution(9582414058728846890)
XLA Ops:
  0.0 0.0 copy-start
  0.0 0.7 compare_select_fusion.2
  0.7 0.6 scatter_custom_fusion
  1.4 0.1 broadcast_bitcast_fusion
  1.4 0.0 copy-start.5
  1.5 1.3 gather_fusion.3
  2.8 0.7 fusion.18
  3.5 0.0 copy-start.3
  3.5 1.4 copy.18.route_ref
  4.8 0.0 copy-done.5
  4.8 22.7 %all_gather.3 = bf16[2048,128]{1,0:T(8,128)(2,1)S(1)} all-gather(bf16[128,128]{1,0:T(8,128)(2,1)S(1)} %copy-done.5), channel_id=1, replica_groups=mesh['gx'=16,'zz'=8,'cc'=2] {'zz','cc'}, dimensions={0}, use_global_device_ids=true | all-gather | bytes 557056 | tf_op jit(solution)/shard_map/all_gather | solution.py:223
  27.5 0.0 copy-start.4
  27.5 0.6 gather_fusion.1
  28.2 0.0 copy-done.3
  28.2 1.2 bitcast_select_fusion.tok_ref
  29.4 0.0 copy-done.4
  29.4 0.8 pad_maximum_fusion.weight_ref
  30.2 7.4 %shard_map.109 = f32[2176,512]{1,0:T(8,128)} custom-call(bf16[2048,128]{1,0:T(8,128)(2,1)} %bitcast_select_fusion.tok_ref, bf16[1,128]{1,0:T(2,128)(2,1)} %bitcast.66, bf16[8,128]{1,0:T(8,128)(2,1)} %bitcast.65, bf16[128,1280]{1,0:T(8,128)(2,1)} %pad_maximum_fusion.weight_ref, s32[2048,2]{1,0:T(8,128)} %copy.18.route_ref, ...), custom_call_target="tpu_custom_call" | custom-call | flops 675282944 | bytes 5308416 | tf_op jit(solution)/shard_map/pallas_call | solution.py:106
  37.6 0.0 copy-start.6
  37.6 0.0 copy-start.1
  37.6 6.9 %all-to-all-start = ((f32[16,136,512]{2,1,0:T(8,128)}), f32[16,136,512]{2,1,0:T(8,128)}, u32[]{:S(2)}, u32[]{:S(2)}) async-start(f32[16,136,512]{2,1,0:T(8,128)} %bitcast.57), calls=%async_computation | async-start | bytes 8912896 | tf_op jit(solution)/shard_map/all_to_all | solution.py:248
  44.6 0.6 dynamic-slice.4
  45.8 0.1 reshape.195
  45.9 0.1 reshape.194
  46.0 0.0 copy-done.6
  46.0 0.6 dynamic-slice.5
  46.6 0.0 copy-done.1
  46.6 0.7 gather_fusion
  48.0 55.0 %all-to-all-done.blocks_ref = f32[16,136,512]{2,1,0:T(8,128)} async-done(((f32[16,136,512]{2,1,0:T(8,128)}), f32[16,136,512]{2,1,0:T(8,128)}, u32[]{:S(2)}, u32[]{:S(2)}) %all-to-all-start) | async-done | bytes 4456480 | tf_op jit(solution)/shard_map/all_to_all | solution.py:248
  103.0 6.4 %shard_map.110 = bf16[16,136,256]{2,1,0:T(8,128)(2,1)} custom-call(s32[1]{0:T(128)S(6)} %select_n.108.length_ref, f32[16,136,512]{2,1,0:T(8,128)} %all-to-all-done.blocks_ref, bf16[4096,128]{1,0:T(8,128)(2,1)} %bitcast.61, bf16[4096,128]{1,0:T(8,128)(2,1)} %bitcast.62), custom_call_target="tpu_custom_call" | custom-call | flops 553648128 | bytes 7667712 | tf_op jit(solution)/shard_map/pallas_call | solution.py:188
  109.4 0.0 copy-start.2
  109.4 14.4 %all-to-all-start.1 = ((bf16[16,136,256]{2,1,0:T(8,128)(2,1)}), bf16[16,136,256]{2,1,0:T(8,128)(2,1)S(1)}, u32[]{:S(2)}, u32[]{:S(2)}) async-start(bf16[16,136,256]{2,1,0:T(8,128)(2,1)} %shard_map.110), calls=%async_computation.1 | async-start | bytes 2228224 | tf_op jit(solution)/shard_map/all_to_all | solution.py:254
  123.9 0.0 copy-done.2
  123.9 0.6 gather_fusion.4
  124.5 0.1 select_bitcast_fusion
  124.6 15.2 %all-to-all-done.1 = bf16[16,136,256]{2,1,0:T(8,128)(2,1)S(1)} async-done(((bf16[16,136,256]{2,1,0:T(8,128)(2,1)}), bf16[16,136,256]{2,1,0:T(8,128)(2,1)S(1)}, u32[]{:S(2)}, u32[]{:S(2)}) %all-to-all-start.1) | async-done | bytes 1114144 | tf_op jit(solution)/shard_map/all_to_all | solution.py:254
  139.8 0.6 gather_fusion.2
  140.4 0.2 broadcast_select_fusion
  140.6 0.1 slice.29
  140.7 0.3 mul.27
  141.0 0.1 copy.19
  141.2 0.0 copy-done
  141.2 6.1 %fusion.10 = f32[2048,128]{1,0:T(8,128)S(1)} fusion(bf16[2048,2,8]{0,2,1:T(8,128)(2,1)S(1)} %convert_convert_fusion, bf16[2048,2,128]{2,0,1:T(8,128)(2,1)S(1)} %copy.19, f32[2048,2]{0,1:T(2,128)S(1)} %bitcast.64, bf16[8,1,128,128]{3,2,1,0:T(8,128)(2,1)S(1)} %copy-done), kind=kOutput, calls=%fused_computation.12 | convolution fusion | flops 1078722560 | bytes 2441216 | tf_op jit(solution)/shard_map/tsehk,ehko->tso/dot_general | solution.py:277
  147.3 7.4 %all_to_all.20 = f32[2,1024,128]{2,1,0:T(8,128)S(1)} all-to-all(f32[2,1024,128]{2,1,0:T(8,128)S(1)} %bitcast.60), channel_id=1, replica_groups=mesh['gx'=16,'zz'=8,'cc'=2] {'cc'}, dimensions={0} | all-to-all | bytes 2097152 | tf_op jit(solution)/shard_map/all_to_all | solution.py:25
  154.7 0.1 reduce_sum.28
  154.8 19.8 %all_to_all.21 = f32[8,128,128]{2,1,0:T(8,128)S(1)} all-to-all(f32[8,128,128]{2,1,0:T(8,128)S(1)} %bitcast.59), channel_id=1, replica_groups=mesh['gx'=16,'zz'=8,'cc'=2] {'zz'}, dimensions={0} | all-to-all | bytes 1048576 | tf_op jit(solution)/shard_map/all_to_all | solution.py:25
  174.6 0.6 reduce_sum.29
  (15 shorter events, 0.1 us)
Async XLA Ops:
  0.0 141.2 %copy-start = (bf16[8,1,128,128]{3,2,1,0:T(8,128)(2,1)S(1)}, bf16[8,1,128,128]{3,2,1,0:T(8,128)(2,1)}, u32[]{:S(2)}) copy-start(bf16[8,1,128,128]{3,2,1,0:T(8,128)(2,1)} %param.18) | copy-start | bytes 786436
  1.4 3.4 %copy-start.5 = (bf16[128,128]{1,0:T(8,128)(2,1)S(1)}, bf16[128,128]{1,0:T(8,128)(2,1)}, u32[]{:S(2)}) copy-start(bf16[128,128]{1,0:T(8,128)(2,1)} %param.13) | copy-start | bytes 98308
  3.5 24.7 %copy-start.3 = (bf16[8,128,1,128]{3,1,2,0:T(8,128)(2,1)S(1)}, bf16[8,128,1,128]{3,1,2,0:T(8,128)(2,1)}, u32[]{:S(2)}) copy-start(bf16[8,128,1,128]{3,1,2,0:T(8,128)(2,1)} %param.16) | copy-start | bytes 786436
  27.5 1.9 %copy-start.4 = (bf16[128,1,256]{2,0,1:T(8,128)(2,1)S(1)}, bf16[128,1,256]{2,0,1:T(8,128)(2,1)}, u32[]{:S(2)}) copy-start(bf16[128,1,256]{2,0,1:T(8,128)(2,1)} %param.17) | copy-start | bytes 196612
  37.6 8.4 %copy-start.6 = (s32[16]{0:T(128)S(1)}, s32[16]{0:T(128)}, u32[]{:S(2)}) copy-start(s32[16]{0:T(128)} %param.21) | copy-start | bytes 196
  37.6 9.0 %copy-start.1 = (s32[16]{0:T(128)S(1)}, s32[16]{0:T(128)}, u32[]{:S(2)}) copy-start(s32[16]{0:T(128)} %param.22) | copy-start | bytes 196
  37.6 65.4 %all-to-all-start = ((f32[16,136,512]{2,1,0:T(8,128)}), f32[16,136,512]{2,1,0:T(8,128)}, u32[]{:S(2)}, u32[]{:S(2)}) async-start(f32[16,136,512]{2,1,0:T(8,128)} %bitcast.57), calls=%async_computation | async-start | bytes 8912896 | tf_op jit(solution)/shard_map/all_to_all | solution.py:248
  109.4 14.5 %copy-start.2 = (s32[2048,2]{0,1:T(2,128)S(1)}, s32[2048,2]{0,1:T(2,128)}, u32[]{:S(2)}) copy-start(s32[2048,2]{0,1:T(2,128)} %param.23) | copy-start | bytes 49156
  109.4 30.4 %all-to-all-start.1 = ((bf16[16,136,256]{2,1,0:T(8,128)(2,1)}), bf16[16,136,256]{2,1,0:T(8,128)(2,1)S(1)}, u32[]{:S(2)}, u32[]{:S(2)}) async-start(bf16[16,136,256]{2,1,0:T(8,128)(2,1)} %shard_map.110), calls=%async_computation.1 | async-start | bytes 2228224 | tf_op jit(solution)/shard_map/all_to_all | solution.py:254

commit v10 on v9

--- a/solution.py
+++ b/solution.py
@@ -39,38 +39,38 @@
     return gathered.reshape((members * piece.shape[0],) + piece.shape[1:])
 
 
-def pack_kernel(tok_ref, gain_ref, router_ref, weight_ref, route_ref, route_t_ref, out_ref):
-    rows = route_t_ref.shape[2]
+def pack_kernel(order_ref, tok_ref, gain_ref, router_ref, weight_ref, route_ref, route_t_ref, out_ref):
+    rows = tok_ref.shape[0] // order_ref.shape[0]
     block_rows = rows + EXTRA_ROWS
-    per_step = tok_ref.shape[0] // rows
     head_dim = out_ref.shape[1] // 4
     experts = (weight_ref.shape[1] - 2 * head_dim) // head_dim
-    widened = tok_ref[...].astype(jnp.float32)
-    scaled = (widened * gain_ref[...].astype(jnp.float32)).astype(jnp.bfloat16)
-    projected = jnp.dot(scaled, weight_ref[...], preferred_element_type=jnp.float32)
-    first = route_ref[:, 0:1]
-    second = route_ref[:, 1:2]
-    query_first = jnp.zeros((tok_ref.shape[0], head_dim), jnp.float32)
-    query_second = jnp.zeros((tok_ref.shape[0], head_dim), jnp.float32)
-    for expert in range(experts):
-        part = projected[:, expert * head_dim : (expert + 1) * head_dim]
-        query_first = query_first + jnp.where(first == expert, part, 0.0)
-        query_second = query_second + jnp.where(second == expert, part, 0.0)
-    keyval = projected[:, experts * head_dim :]
     contract_last = (((1,), (1,)), ((), ()))
-    for block in range(per_step):
-        low = block * rows
+    step = pl.program_id(0)
+    for block in range(REQUESTS_PER_STEP):
+        first_row = pl.multiple_of(order_ref[step * REQUESTS_PER_STEP + block] * rows, rows)
+        widened = tok_ref[pl.ds(first_row, rows), :].astype(jnp.float32)
+        scaled = (widened * gain_ref[...].astype(jnp.float32)).astype(jnp.bfloat16)
+        projected = jnp.dot(scaled, weight_ref[...], preferred_element_type=jnp.float32)
+        route = route_ref[pl.ds(first_row, rows), :]
+        first = route[:, 0:1]
+        second = route[:, 1:2]
+        query_first = jnp.zeros((rows, head_dim), jnp.float32)
+        query_second = jnp.zeros((rows, head_dim), jnp.float32)
+        for expert in range(experts):
+            part = projected[:, expert * head_dim : (expert + 1) * head_dim]
+            query_first = query_first + jnp.where(first == expert, part, 0.0)
+            query_second = query_second + jnp.where(second == expert, part, 0.0)
         top = block * block_rows
-        out_ref[top : top + rows, 0:head_dim] = query_first[low : low + rows]
-        out_ref[top : top + rows, head_dim : 2 * head_dim] = query_second[low : low + rows]
-        out_ref[top : top + rows, 2 * head_dim :] = keyval[low : low + rows]
-        widened_t = jnp.transpose(widened[low : low + rows])
+        out_ref[top : top + rows, 0:head_dim] = query_first
+        out_ref[top : top + rows, head_dim : 2 * head_dim] = query_second
+        out_ref[top : top + rows, 2 * head_dim :] = projected[:, experts * head_dim :]
+        widened_t = jnp.transpose(widened)
         squares_row = jnp.sum(widened_t * widened_t, axis=0, keepdims=True)
         logits_t = lax.dot_general(
-            router_ref[...], scaled[low : low + rows], contract_last, preferred_element_type=jnp.float32
+            router_ref[...], scaled, contract_last, preferred_element_type=jnp.float32
         )
         expert_row = lax.broadcasted_iota(jnp.int32, logits_t.shape, 0)
-        route_t = route_t_ref[block]
+        route_t = route_t_ref[:, pl.ds(first_row, rows)]
         chosen_first = jnp.sum(
             jnp.where(expert_row == route_t[0:1, :], logits_t, 0.0), axis=0, keepdims=True
         )
@@ -87,37 +87,43 @@
 REQUESTS_PER_STEP = 4
 
 
-def packed_partials(ordered, gain, w_router, query_weight, keyval_weight, route, requests):
-    total_rows, width = ordered.shape
+def packed_partials(order, gathered, gain, w_router, query_weight, keyval_weight, route):
+    total_rows, width = gathered.shape
+    requests = order.shape[0]
     rows = total_rows // requests
     experts, _, head_dim = query_weight.shape
     keyval_cols = keyval_weight.shape[1]
     packed_cols = 2 * head_dim + keyval_cols
     assert 3 * rows <= packed_cols and keyval_cols == 2 * head_dim
     block_rows = rows + EXTRA_ROWS
-    step_rows = REQUESTS_PER_STEP * rows
     weight = jnp.concatenate(
         [jnp.transpose(query_weight, (1, 0, 2)).reshape(width, experts * head_dim), keyval_weight],
         axis=1,
     )
-    route_t = jnp.transpose(route.reshape(requests, rows, route.shape[1]), (0, 2, 1))
     flops = 2 * total_rows * width * (weight.shape[1] + w_router.shape[1])
     moved = 2 * total_rows * width + 4 * requests * block_rows * packed_cols + 2 * weight.size
+    whole = lambda shape: pl.BlockSpec(shape, lambda s, order_ref: (0,) * len(shape))
+    route_t = jnp.transpose(route)
     return pl.pallas_call(
         pack_kernel,
         out_shape=jax.ShapeDtypeStruct((requests * block_rows, packed_cols), jnp.float32),
-        grid=(requests // REQUESTS_PER_STEP,),
-        in_specs=[
-            pl.BlockSpec((step_rows, width), lambda s: (s, 0)),
-            pl.BlockSpec((1, width), lambda s: (0, 0)),
-            pl.BlockSpec((w_router.shape[1], width), lambda s: (0, 0)),
-            pl.BlockSpec(weight.shape, lambda s: (0, 0)),
-            pl.BlockSpec((step_rows, route.shape[1]), lambda s: (s, 0)),
-            pl.BlockSpec((REQUESTS_PER_STEP, route.shape[1], rows), lambda s: (s, 0, 0)),
-        ],
-        out_specs=pl.BlockSpec((REQUESTS_PER_STEP * block_rows, packed_cols), lambda s: (s, 0)),
+        grid_spec=pltpu.PrefetchScalarGridSpec(
+            num_scalar_prefetch=1,
+            grid=(requests // REQUESTS_PER_STEP,),
+            in_specs=[
+                whole(gathered.shape),
+                whole((1, width)),
+                whole((w_router.shape[1], width)),
+                whole(weight.shape),
+                whole(route.shape),
+                whole(route_t.shape),
+            ],
+            out_specs=pl.BlockSpec(
+                (REQUESTS_PER_STEP * block_rows, packed_cols), lambda s, order_ref: (s, 0)
+            ),
+        ),
         cost_estimate=pl.CostEstimate(flops=flops, transcendentals=0, bytes_accessed=moved),
-    )(ordered, gain.reshape(1, width), jnp.transpose(w_router), weight, route, route_t)
+    )(order, gathered, gain.reshape(1, width), jnp.transpose(w_router), weight, route, route_t)
 
 
 def attend_kernel(length_ref, blocks_ref, cache_k_ref, cache_v_ref, out_ref):
@@ -227,20 +233,14 @@
     slot_index = lax.axis_index("gx")
     inverse = jnp.zeros((requests,), jnp.int32).at[deal].set(jnp.arange(requests, dtype=jnp.int32))
     assert heads_local == 1
-    ordered = jnp.take(gathered.reshape(requests, new_len, local_width), inverse, axis=0).reshape(
-        total_rows, local_width
-    )
-    slot_route = jnp.take(route.reshape(requests, new_len, top_count), inverse, axis=0).reshape(
-        total_rows, top_count
-    )
     packed = packed_partials(
-        ordered,
+        inverse,
+        gathered,
         gain,
         w_router,
         expert_query_weight.reshape(experts, local_width, head_dim),
         key_value_weight.reshape(local_width, 2 * head_dim),
-        slot_route,
-        requests,
+        route,
     )
     query_cols = top_count * heads_local * head_dim
     keyval_cols = heads_local * 2 * head_dim

time: 176 us -> 176 us (level)
  other arithmetic: 4.41 us -> 2.47 us
    unnamed x14 -> x17, local copies, waits for them, and re-layouts: 0.03 us -> 2.09 us
    gather x2 -> x0, local copies, waits for them, and re-layouts: 1.96 us -> none  [the longest x1 1.31 us: per_device(): jnp.take(route.reshape(requests, new_len, top_count), inverse, axis=0)]
where the time goes in v10:
time: 176 us; the launch traced here: 175 us
  waiting for transfers between devices  70.2 us (40%)
  blocking collectives  51.5 us (29%)
  starting transfers between devices  21.4 us (12%)
  Pallas kernels  15.2 us (9%)
  local copies, waits for them, and re-layouts  7.09 us (4%)
  matrix products  6.08 us (3%)
  other arithmetic  2.47 us (1%)
    all_to_all x1, waiting for transfers between devices, per_device(): lax.all_to_all(packed.reshape(members, packed.shape[0] // members, packed...  54.9 us
    all_to_all x2, blocking collectives, scatter_sum(): lax.all_to_all(part.reshape((members, part.shape[0] // members) + part.sh...  27.3 us
    all_gather x1, blocking collectives, per_device(): gathered = lax.all_gather(tokens, TOKEN_AXES, axis=0, tiled=True)  24.1 us
    all_to_all x1, waiting for transfers between devices, per_device(): lax.all_to_all(copies, 'gx', 0, 0, tiled=True)  15.3 us
    all_to_all x1, starting transfers between devices, per_device(): lax.all_to_all(copies, 'gx', 0, 0, tiled=True)  14.4 us
    pallas_call x1, Pallas kernels, packed_partials(): pl.pallas_call(pack_kernel, out_shape=jax.ShapeDtypeStruct((requests * bl...  8.75 us
    all_to_all x1, starting transfers between devices, per_device(): lax.all_to_all(packed.reshape(members, packed.shape[0] // members, packed...  6.94 us
    pallas_call x1, Pallas kernels, attend(): pl.pallas_call(attend_kernel, out_shape=jax.ShapeDtypeStruct(out_shape, j...  6.42 us
  transfers between devices with their start and end apart: 2, of which 2 were waited for; matrix products, arithmetic and copies ran while one was open for 2% of the time, Pallas kernels for 0%

profile of v10, /device:TPU:1, one launch (start us, length us, event | category | flops | bytes accessed | tf_op | source)
XLA Modules:
  0.0 175.3 jit_solution(14921252736626718050)
XLA Ops:
  0.0 0.0 copy-start
  0.0 0.0 copy-start.3
  0.0 0.0 copy-start.5
  0.0 0.0 copy-start.4
  0.0 0.7 compare_select_fusion.1
  0.7 2.1 %copy.19.route_ref = s32[2048,2]{1,0:T(8,128)} copy(s32[2048,2]{0,1:T(2,128)} %param.21) | data formatting | bytes 32768 | tf_op args[10]
  2.8 0.0 copy-done.3
  2.8 0.0 copy-done.5
  2.9 24.1 %all_gather.3.tok_ref = bf16[2048,128]{1,0:T(8,128)(2,1)} all-gather(bf16[128,128]{1,0:T(8,128)(2,1)S(1)} %copy-done.5), channel_id=1, replica_groups=mesh['gx'=16,'zz'=8,'cc'=2] {'zz','cc'}, dimensions={0}, use_global_device_ids=true | all-gather | bytes 557056 | tf_op jit(solution)/shard_map/all_gather | solution.py:229
  27.0 0.0 copy-done.4
  27.0 0.8 pad_maximum_fusion.weight_ref
  27.8 1.1 scatter_custom_fusion.order_ref
  28.9 8.8 %shard_map.109 = f32[2176,512]{1,0:T(8,128)} custom-call(s32[16]{0:T(128)} %scatter_custom_fusion.order_ref, bf16[2048,128]{1,0:T(8,128)(2,1)} %all_gather.3.tok_ref, bf16[1,128]{1,0:T(2,128)(2,1)} %bitcast.59, bf16[8,128]{1,0:T(8,128)(2,1)} %bitcast.58, bf16[128,1280]{1,0:T(8,128)(2,1)} %pad_maximum_fusion.weight_ref, s32[2048,2]{1,0:T(8,128)} %copy.19.route_ref, ...), custom_call_target="tpu_custom_call" | custom-call | flops 675282944 | bytes 5308416 | tf_op jit(solution)/shard_map/pallas_call | solution.py:107
  37.6 0.0 copy-start.6
  37.6 0.0 copy-start.7
  37.6 0.0 copy-start.1
  37.6 6.9 %all-to-all-start = ((f32[16,136,512]{2,1,0:T(8,128)}), f32[16,136,512]{2,1,0:T(8,128)}, u32[]{:S(2)}, u32[]{:S(2)}) async-start(f32[16,136,512]{2,1,0:T(8,128)} %bitcast.51), calls=%async_computation | async-start | bytes 8912896 | tf_op jit(solution)/shard_map/all_to_all | solution.py:248
  44.6 0.0 copy-done.6
  44.6 0.6 dynamic-slice.4
  45.9 0.1 reshape.197
  45.9 0.1 reshape.196
  46.0 0.0 copy-done.7
  46.0 0.6 dynamic-slice.5
  46.6 0.0 copy-done.1
  46.7 0.7 gather_fusion
  48.0 0.1 broadcast_bitcast_fusion
  48.1 54.9 %all-to-all-done.blocks_ref = f32[16,136,512]{2,1,0:T(8,128)} async-done(((f32[16,136,512]{2,1,0:T(8,128)}), f32[16,136,512]{2,1,0:T(8,128)}, u32[]{:S(2)}, u32[]{:S(2)}) %all-to-all-start) | async-done | bytes 4456480 | tf_op jit(solution)/shard_map/all_to_all | solution.py:248
  103.0 6.4 %shard_map.110 = bf16[16,136,256]{2,1,0:T(8,128)(2,1)} custom-call(s32[1]{0:T(128)S(6)} %select_n.104.length_ref, f32[16,136,512]{2,1,0:T(8,128)} %all-to-all-done.blocks_ref, bf16[4096,128]{1,0:T(8,128)(2,1)} %bitcast.54, bf16[4096,128]{1,0:T(8,128)(2,1)} %bitcast.55), custom_call_target="tpu_custom_call" | custom-call | flops 553648128 | bytes 7667712 | tf_op jit(solution)/shard_map/pallas_call | solution.py:194
  109.4 0.0 copy-start.2
  109.4 14.4 %all-to-all-start.1 = ((bf16[16,136,256]{2,1,0:T(8,128)(2,1)}), bf16[16,136,256]{2,1,0:T(8,128)(2,1)S(1)}, u32[]{:S(2)}, u32[]{:S(2)}) async-start(bf16[16,136,256]{2,1,0:T(8,128)(2,1)} %shard_map.110), calls=%async_computation.1 | async-start | bytes 2228224 | tf_op jit(solution)/shard_map/all_to_all | solution.py:254
  123.9 0.0 copy-done.2
  123.9 0.6 gather_fusion.2
  124.5 15.3 %all-to-all-done.1 = bf16[16,136,256]{2,1,0:T(8,128)(2,1)S(1)} async-done(((bf16[16,136,256]{2,1,0:T(8,128)(2,1)}), bf16[16,136,256]{2,1,0:T(8,128)(2,1)S(1)}, u32[]{:S(2)}, u32[]{:S(2)}) %all-to-all-start.1) | async-done | bytes 1114144 | tf_op jit(solution)/shard_map/all_to_all | solution.py:254
  139.8 0.6 gather_fusion.1
  140.4 0.2 broadcast_select_fusion
  140.6 0.1 slice.25
  140.7 0.3 mul.27
  141.0 0.1 copy.20
  141.2 0.0 copy-done
  141.2 6.1 %fusion.10 = f32[2048,128]{1,0:T(8,128)S(1)} fusion(bf16[2048,2,8]{0,2,1:T(8,128)(2,1)S(1)} %convert_convert_fusion, bf16[2048,2,128]{2,0,1:T(8,128)(2,1)S(1)} %copy.20, f32[2048,2]{0,1:T(2,128)S(1)} %bitcast.57, bf16[8,1,128,128]{3,2,1,0:T(8,128)(2,1)S(1)} %copy-done), kind=kOutput, calls=%fused_computation.10 | convolution fusion | flops 1078722560 | bytes 2441216 | tf_op jit(solution)/shard_map/tsehk,ehko->tso/dot_general | solution.py:277
  147.3 7.4 %all_to_all.20 = f32[2,1024,128]{2,1,0:T(8,128)S(1)} all-to-all(f32[2,1024,128]{2,1,0:T(8,128)S(1)} %bitcast.53), channel_id=1, replica_groups=mesh['gx'=16,'zz'=8,'cc'=2] {'cc'}, dimensions={0} | all-to-all | bytes 2097152 | tf_op jit(solution)/shard_map/all_to_all | solution.py:25
  154.7 0.1 reduce_sum.28
  154.8 19.9 %all_to_all.21 = f32[8,128,128]{2,1,0:T(8,128)S(1)} all-to-all(f32[8,128,128]{2,1,0:T(8,128)S(1)} %bitcast.52), channel_id=1, replica_groups=mesh['gx'=16,'zz'=8,'cc'=2] {'zz'}, dimensions={0} | all-to-all | bytes 1048576 | tf_op jit(solution)/shard_map/all_to_all | solution.py:25
  174.7 0.6 reduce_sum.29
  (11 shorter events, 0.1 us)
Async XLA Ops:
  0.0 141.2 %copy-start = (bf16[8,1,128,128]{3,2,1,0:T(8,128)(2,1)S(1)}, bf16[8,1,128,128]{3,2,1,0:T(8,128)(2,1)}, u32[]{:S(2)}) copy-start(bf16[8,1,128,128]{3,2,1,0:T(8,128)(2,1)} %param.16) | copy-start | bytes 786436
  0.0 2.8 %copy-start.3 = (bf16[8,128,1,128]{3,1,2,0:T(8,128)(2,1)S(1)}, bf16[8,128,1,128]{3,1,2,0:T(8,128)(2,1)}, u32[]{:S(2)}) copy-start(bf16[8,128,1,128]{3,1,2,0:T(8,128)(2,1)} %param.14) | copy-start | bytes 786436
  0.0 2.8 %copy-start.5 = (bf16[128,128]{1,0:T(8,128)(2,1)S(1)}, bf16[128,128]{1,0:T(8,128)(2,1)}, u32[]{:S(2)}) copy-start(bf16[128,128]{1,0:T(8,128)(2,1)} %param.11) | copy-start | bytes 98308
  0.0 27.0 %copy-start.4 = (bf16[128,1,256]{2,0,1:T(8,128)(2,1)S(1)}, bf16[128,1,256]{2,0,1:T(8,128)(2,1)}, u32[]{:S(2)}) copy-start(bf16[128,1,256]{2,0,1:T(8,128)(2,1)} %param.15) | copy-start | bytes 196612
  37.6 7.0 %copy-start.6 = (s32[16]{0:T(128)S(1)}, s32[16]{0:T(128)}, u32[]{:S(2)}) copy-start(s32[16]{0:T(128)} %scatter_custom_fusion.order_ref) | copy-start | bytes 196
  37.6 8.4 %copy-start.7 = (s32[16]{0:T(128)S(1)}, s32[16]{0:T(128)}, u32[]{:S(2)}) copy-start(s32[16]{0:T(128)} %param.19) | copy-start | bytes 196
  37.6 9.0 %copy-start.1 = (s32[16]{0:T(128)S(1)}, s32[16]{0:T(128)}, u32[]{:S(2)}) copy-start(s32[16]{0:T(128)} %param.20) | copy-start | bytes 196
  37.6 65.4 %all-to-all-start = ((f32[16,136,512]{2,1,0:T(8,128)}), f32[16,136,512]{2,1,0:T(8,128)}, u32[]{:S(2)}, u32[]{:S(2)}) async-start(f32[16,136,512]{2,1,0:T(8,128)} %bitcast.51), calls=%async_computation | async-start | bytes 8912896 | tf_op jit(solution)/shard_map/all_to_all | solution.py:248
  109.4 14.5 %copy-start.2 = (s32[2048,2]{0,1:T(2,128)S(1)}, s32[2048,2]{0,1:T(2,128)}, u32[]{:S(2)}) copy-start(s32[2048,2]{0,1:T(2,128)} %param.21) | copy-start | bytes 49156
  109.4 30.4 %all-to-all-start.1 = ((bf16[16,136,256]{2,1,0:T(8,128)(2,1)}), bf16[16,136,256]{2,1,0:T(8,128)(2,1)S(1)}, u32[]{:S(2)}, u32[]{:S(2)}) async-start(bf16[16,136,256]{2,1,0:T(8,128)(2,1)} %shard_map.110), calls=%async_computation.1 | async-start | bytes 2228224 | tf_op jit(solution)/shard_map/all_to_all | solution.py:254

commit v11 on v10

--- a/solution.py
+++ b/solution.py
@@ -226,7 +226,9 @@
     heads_local = expert_query_weight.shape[2]
     head_dim = expert_query_weight.shape[3]
     top_count = route.shape[1]
-    gathered = lax.all_gather(tokens, TOKEN_AXES, axis=0, tiled=True)
+    gathered = lax.all_gather(
+        lax.all_gather(tokens, TOKEN_AXES[1], axis=0, tiled=True), TOKEN_AXES[0], axis=0, tiled=True
+    )
     total_rows, local_width = gathered.shape
     new_len = total_rows // requests
     full_width = local_width * lax.axis_size("gx")

time: 176 us -> 171 us (0.972)
  blocking collectives: 51.5 us -> 59.5 us
  waiting for transfers between devices: 70.2 us -> 63.1 us
  starting transfers between devices: 21.4 us -> 15.5 us
    all_to_all x1, starting transfers between devices: 14.4 us -> 8.54 us  [per_device(): lax.all_to_all(copies, 'gx', 0, 0, tiled=True)]
    all_gather x1 -> x2, blocking collectives: 24.1 us -> 28.2 us  [the longest x1 23.3 us: per_device(): lax.all_gather(lax.all_gather(tokens, TOKEN_AXES[1], axis=0, tiled=True),...]
    all_to_all x2, blocking collectives: 27.3 us -> 31.3 us  [scatter_sum(): lax.all_to_all(part.reshape((members, part.shape[0] // members) + part.sh...]
    all_to_all x1, waiting for transfers between devices: 54.9 us -> 51.3 us  [per_device(): lax.all_to_all(packed.reshape(members, packed.shape[0] // members, packed...]
    all_to_all x1, waiting for transfers between devices: 15.3 us -> 11.8 us  [per_device(): lax.all_to_all(copies, 'gx', 0, 0, tiled=True)]
where the time goes in v11:
time: 171 us; the launch traced here: 170 us
  waiting for transfers between devices  63.1 us (37%)
  blocking collectives  59.5 us (35%)
  starting transfers between devices  15.5 us (9%)
  Pallas kernels  15.2 us (9%)
  local copies, waits for them, and re-layouts  7.08 us (4%)
  matrix products  6.08 us (4%)
  other arithmetic  2.45 us (1%)
    all_to_all x1, waiting for transfers between devices, per_device(): lax.all_to_all(packed.reshape(members, packed.shape[0] // members, packed...  51.3 us
    all_to_all x2, blocking collectives, scatter_sum(): lax.all_to_all(part.reshape((members, part.shape[0] // members) + part.sh...  31.3 us
    all_gather x1, blocking collectives, per_device(): lax.all_gather(lax.all_gather(tokens, TOKEN_AXES[1], axis=0, tiled=True),...  23.3 us
    all_to_all x1, waiting for transfers between devices, per_device(): lax.all_to_all(copies, 'gx', 0, 0, tiled=True)  11.8 us
    pallas_call x1, Pallas kernels, packed_partials(): pl.pallas_call(pack_kernel, out_shape=jax.ShapeDtypeStruct((requests * bl...  8.76 us
    all_to_all x1, starting transfers between devices, per_device(): lax.all_to_all(copies, 'gx', 0, 0, tiled=True)  8.54 us
    all_to_all x1, starting transfers between devices, per_device(): lax.all_to_all(packed.reshape(members, packed.shape[0] // members, packed...  6.95 us
    pallas_call x1, Pallas kernels, attend(): pl.pallas_call(attend_kernel, out_shape=jax.ShapeDtypeStruct(out_shape, j...  6.42 us
  transfers between devices with their start and end apart: 2, of which 2 were waited for; matrix products, arithmetic and copies ran while one was open for 2% of the time, Pallas kernels for 0%

profile of v11, /device:TPU:1, one launch (start us, length us, event | category | flops | bytes accessed | tf_op | source)
XLA Modules:
  0.0 170.2 jit_solution(7604152194881149483)
XLA Ops:
  0.0 0.0 copy-start
  0.0 0.0 copy-start.3
  0.0 0.7 compare_select_fusion.1
  0.7 0.0 copy-start.4
  0.7 2.1 %copy.19.route_ref = s32[2048,2]{1,0:T(8,128)} copy(s32[2048,2]{0,1:T(2,128)} %param.21) | data formatting | bytes 32768 | tf_op args[10]
  2.8 4.9 %all_gather.6 = bf16[256,128]{1,0:T(8,128)(2,1)S(1)} all-gather(bf16[128,128]{1,0:T(8,128)(2,1)} %param.11), channel_id=1, replica_groups=mesh['gx'=16,'zz'=8,'cc'=2] {'cc'}, dimensions={0}, use_global_device_ids=true | all-gather | bytes 98304 | tf_op jit(solution)/shard_map/all_gather | solution.py:230
  7.7 23.3 %all_gather.7.tok_ref = bf16[2048,128]{1,0:T(8,128)(2,1)} all-gather(bf16[256,128]{1,0:T(8,128)(2,1)S(1)} %all_gather.6), channel_id=1, replica_groups=mesh['gx'=16,'zz'=8,'cc'=2] {'zz'}, dimensions={0}, use_global_device_ids=true | all-gather | bytes 589824 | tf_op jit(solution)/shard_map/all_gather | solution.py:229
  31.0 0.0 copy-done.3
  31.0 0.0 copy-done.4
  31.0 0.7 pad_maximum_fusion.weight_ref
  31.8 1.1 scatter_custom_fusion.order_ref
  32.9 8.8 %shard_map.109 = f32[2176,512]{1,0:T(8,128)} custom-call(s32[16]{0:T(128)} %scatter_custom_fusion.order_ref, bf16[2048,128]{1,0:T(8,128)(2,1)} %all_gather.7.tok_ref, bf16[1,128]{1,0:T(2,128)(2,1)} %bitcast.59, bf16[8,128]{1,0:T(8,128)(2,1)} %bitcast.58, bf16[128,1280]{1,0:T(8,128)(2,1)} %pad_maximum_fusion.weight_ref, s32[2048,2]{1,0:T(8,128)} %copy.19.route_ref, ...), custom_call_target="tpu_custom_call" | custom-call | flops 675282944 | bytes 5308416 | tf_op jit(solution)/shard_map/pallas_call | solution.py:107
  41.7 0.0 copy-start.5
  41.7 0.0 copy-start.6
  41.7 0.0 copy-start.1
  41.7 6.9 %all-to-all-start = ((f32[16,136,512]{2,1,0:T(8,128)}), f32[16,136,512]{2,1,0:T(8,128)}, u32[]{:S(2)}, u32[]{:S(2)}) async-start(f32[16,136,512]{2,1,0:T(8,128)} %bitcast.51), calls=%async_computation | async-start | bytes 8912896 | tf_op jit(solution)/shard_map/all_to_all | solution.py:250
  48.6 0.0 copy-done.5
  48.6 0.6 dynamic-slice.4
  49.8 0.1 reshape.197
  49.9 0.1 reshape.196
  50.0 0.0 copy-done.6
  50.0 0.6 dynamic-slice.5
  50.6 0.0 copy-done.1
  50.6 0.7 gather_fusion
  51.9 0.1 broadcast_bitcast_fusion
  51.9 51.3 %all-to-all-done.blocks_ref = f32[16,136,512]{2,1,0:T(8,128)} async-done(((f32[16,136,512]{2,1,0:T(8,128)}), f32[16,136,512]{2,1,0:T(8,128)}, u32[]{:S(2)}, u32[]{:S(2)}) %all-to-all-start) | async-done | bytes 4456480 | tf_op jit(solution)/shard_map/all_to_all | solution.py:250
  103.2 6.4 %shard_map.110 = bf16[16,136,256]{2,1,0:T(8,128)(2,1)} custom-call(s32[1]{0:T(128)S(6)} %select_n.104.length_ref, f32[16,136,512]{2,1,0:T(8,128)} %all-to-all-done.blocks_ref, bf16[4096,128]{1,0:T(8,128)(2,1)} %bitcast.54, bf16[4096,128]{1,0:T(8,128)(2,1)} %bitcast.55), custom_call_target="tpu_custom_call" | custom-call | flops 553648128 | bytes 7667712 | tf_op jit(solution)/shard_map/pallas_call | solution.py:194
  109.7 0.0 copy-start.2
  109.7 8.5 %all-to-all-start.1 = ((bf16[16,136,256]{2,1,0:T(8,128)(2,1)}), bf16[16,136,256]{2,1,0:T(8,128)(2,1)S(1)}, u32[]{:S(2)}, u32[]{:S(2)}) async-start(bf16[16,136,256]{2,1,0:T(8,128)(2,1)} %shard_map.110), calls=%async_computation.1 | async-start | bytes 2228224 | tf_op jit(solution)/shard_map/all_to_all | solution.py:256
  118.2 0.0 copy-done.2
  118.2 0.6 gather_fusion.2
  118.9 11.8 %all-to-all-done.1 = bf16[16,136,256]{2,1,0:T(8,128)(2,1)S(1)} async-done(((bf16[16,136,256]{2,1,0:T(8,128)(2,1)}), bf16[16,136,256]{2,1,0:T(8,128)(2,1)S(1)}, u32[]{:S(2)}, u32[]{:S(2)}) %all-to-all-start.1) | async-done | bytes 1114144 | tf_op jit(solution)/shard_map/all_to_all | solution.py:256
  130.7 0.6 gather_fusion.1
  131.3 0.2 broadcast_select_fusion
  131.5 0.1 slice.25
  131.6 0.3 mul.27
  131.9 0.1 copy.20
  132.1 0.0 copy-done
  132.1 6.1 %fusion.10 = f32[2048,128]{1,0:T(8,128)S(1)} fusion(bf16[2048,2,8]{0,2,1:T(8,128)(2,1)S(1)} %convert_convert_fusion, bf16[2048,2,128]{2,0,1:T(8,128)(2,1)S(1)} %copy.20, f32[2048,2]{0,1:T(2,128)S(1)} %bitcast.57, bf16[8,1,128,128]{3,2,1,0:T(8,128)(2,1)S(1)} %copy-done), kind=kOutput, calls=%fused_computation.10 | convolution fusion | flops 1078722560 | bytes 2441216 | tf_op jit(solution)/shard_map/tsehk,ehko->tso/dot_general | solution.py:279
  138.2 10.6 %all_to_all.20 = f32[2,1024,128]{2,1,0:T(8,128)S(1)} all-to-all(f32[2,1024,128]{2,1,0:T(8,128)S(1)} %bitcast.53), channel_id=1, replica_groups=mesh['gx'=16,'zz'=8,'cc'=2] {'cc'}, dimensions={0} | all-to-all | bytes 2097152 | tf_op jit(solution)/shard_map/all_to_all | solution.py:25
  148.8 0.1 reduce_sum.28
  148.9 20.7 %all_to_all.21 = f32[8,128,128]{2,1,0:T(8,128)S(1)} all-to-all(f32[8,128,128]{2,1,0:T(8,128)S(1)} %bitcast.52), channel_id=1, replica_groups=mesh['gx'=16,'zz'=8,'cc'=2] {'zz'}, dimensions={0} | all-to-all | bytes 1048576 | tf_op jit(solution)/shard_map/all_to_all | solution.py:25
  169.6 0.6 reduce_sum.29
  (11 shorter events, 0.1 us)
Async XLA Ops:
  0.0 132.1 %copy-start = (bf16[8,1,128,128]{3,2,1,0:T(8,128)(2,1)S(1)}, bf16[8,1,128,128]{3,2,1,0:T(8,128)(2,1)}, u32[]{:S(2)}) copy-start(bf16[8,1,128,128]{3,2,1,0:T(8,128)(2,1)} %param.16) | copy-start | bytes 786436
  0.0 31.0 %copy-start.3 = (bf16[8,128,1,128]{3,1,2,0:T(8,128)(2,1)S(1)}, bf16[8,128,1,128]{3,1,2,0:T(8,128)(2,1)}, u32[]{:S(2)}) copy-start(bf16[8,128,1,128]{3,1,2,0:T(8,128)(2,1)} %param.14) | copy-start | bytes 786436
  0.7 30.3 %copy-start.4 = (bf16[128,1,256]{2,0,1:T(8,128)(2,1)S(1)}, bf16[128,1,256]{2,0,1:T(8,128)(2,1)}, u32[]{:S(2)}) copy-start(bf16[128,1,256]{2,0,1:T(8,128)(2,1)} %param.15) | copy-start | bytes 196612
  41.7 7.0 %copy-start.5 = (s32[16]{0:T(128)S(1)}, s32[16]{0:T(128)}, u32[]{:S(2)}) copy-start(s32[16]{0:T(128)} %scatter_custom_fusion.order_ref) | copy-start | bytes 196
  41.7 8.3 %copy-start.6 = (s32[16]{0:T(128)S(1)}, s32[16]{0:T(128)}, u32[]{:S(2)}) copy-start(s32[16]{0:T(128)} %param.19) | copy-start | bytes 196
  41.7 8.9 %copy-start.1 = (s32[16]{0:T(128)S(1)}, s32[16]{0:T(128)}, u32[]{:S(2)}) copy-start(s32[16]{0:T(128)} %param.20) | copy-start | bytes 196
  41.7 61.6 %all-to-all-start = ((f32[16,136,512]{2,1,0:T(8,128)}), f32[16,136,512]{2,1,0:T(8,128)}, u32[]{:S(2)}, u32[]{:S(2)}) async-start(f32[16,136,512]{2,1,0:T(8,128)} %bitcast.51), calls=%async_computation | async-start | bytes 8912896 | tf_op jit(solution)/shard_map/all_to_all | solution.py:250
  109.7 8.6 %copy-start.2 = (s32[2048,2]{0,1:T(2,128)S(1)}, s32[2048,2]{0,1:T(2,128)}, u32[]{:S(2)}) copy-start(s32[2048,2]{0,1:T(2,128)} %param.21) | copy-start | bytes 49156
  109.7 21.0 %all-to-all-start.1 = ((bf16[16,136,256]{2,1,0:T(8,128)(2,1)}), bf16[16,136,256]{2,1,0:T(8,128)(2,1)S(1)}, u32[]{:S(2)}, u32[]{:S(2)}) async-start(bf16[16,136,256]{2,1,0:T(8,128)(2,1)} %shard_map.110), calls=%async_computation.1 | async-start | bytes 2228224 | tf_op jit(solution)/shard_map/all_to_all | solution.py:256

commit v12 on v11

--- a/solution.py
+++ b/solution.py
@@ -39,7 +39,9 @@
     return gathered.reshape((members * piece.shape[0],) + piece.shape[1:])
 
 
-def pack_kernel(order_ref, tok_ref, gain_ref, router_ref, weight_ref, route_ref, route_t_ref, out_ref):
+def pack_kernel(
+    order_ref, token_order_ref, tok_ref, gain_ref, router_ref, weight_ref, route_ref, route_t_ref, out_ref
+):
     rows = tok_ref.shape[0] // order_ref.shape[0]
     block_rows = rows + EXTRA_ROWS
     head_dim = out_ref.shape[1] // 4
@@ -48,7 +50,8 @@
     step = pl.program_id(0)
     for block in range(REQUESTS_PER_STEP):
         first_row = pl.multiple_of(order_ref[step * REQUESTS_PER_STEP + block] * rows, rows)
-        widened = tok_ref[pl.ds(first_row, rows), :].astype(jnp.float32)
+        token_row = pl.multiple_of(token_order_ref[step * REQUESTS_PER_STEP + block] * rows, rows)
+        widened = tok_ref[pl.ds(token_row, rows), :].astype(jnp.float32)
         scaled = (widened * gain_ref[...].astype(jnp.float32)).astype(jnp.bfloat16)
         projected = jnp.dot(scaled, weight_ref[...], preferred_element_type=jnp.float32)
         route = route_ref[pl.ds(first_row, rows), :]
@@ -87,7 +90,7 @@
 REQUESTS_PER_STEP = 4
 
 
-def packed_partials(order, gathered, gain, w_router, query_weight, keyval_weight, route):
+def packed_partials(order, token_order, gathered, gain, w_router, query_weight, keyval_weight, route):
     total_rows, width = gathered.shape
     requests = order.shape[0]
     rows = total_rows // requests
@@ -102,13 +105,13 @@
     )
     flops = 2 * total_rows * width * (weight.shape[1] + w_router.shape[1])
     moved = 2 * total_rows * width + 4 * requests * block_rows * packed_cols + 2 * weight.size
-    whole = lambda shape: pl.BlockSpec(shape, lambda s, order_ref: (0,) * len(shape))
+    whole = lambda shape: pl.BlockSpec(shape, lambda s, order_ref, token_ref: (0,) * len(shape))
     route_t = jnp.transpose(route)
     return pl.pallas_call(
         pack_kernel,
         out_shape=jax.ShapeDtypeStruct((requests * block_rows, packed_cols), jnp.float32),
         grid_spec=pltpu.PrefetchScalarGridSpec(
-            num_scalar_prefetch=1,
+            num_scalar_prefetch=2,
             grid=(requests // REQUESTS_PER_STEP,),
             in_specs=[
                 whole(gathered.shape),
@@ -119,11 +122,11 @@
                 whole(route_t.shape),
             ],
             out_specs=pl.BlockSpec(
-                (REQUESTS_PER_STEP * block_rows, packed_cols), lambda s, order_ref: (s, 0)
+                (REQUESTS_PER_STEP * block_rows, packed_cols), lambda s, order_ref, token_ref: (s, 0)
             ),
         ),
         cost_estimate=pl.CostEstimate(flops=flops, transcendentals=0, bytes_accessed=moved),
-    )(order, gathered, gain.reshape(1, width), jnp.transpose(w_router), weight, route, route_t)
+    )(order, token_order, gathered, gain.reshape(1, width), jnp.transpose(w_router), weight, route, route_t)
 
 
 def attend_kernel(length_ref, blocks_ref, cache_k_ref, cache_v_ref, out_ref):
@@ -227,7 +230,7 @@
     head_dim = expert_query_weight.shape[3]
     top_count = route.shape[1]
     gathered = lax.all_gather(
-        lax.all_gather(tokens, TOKEN_AXES[1], axis=0, tiled=True), TOKEN_AXES[0], axis=0, tiled=True
+        lax.all_gather(tokens, TOKEN_AXES[0], axis=0, tiled=True), TOKEN_AXES[1], axis=0, tiled=True
     )
     total_rows, local_width = gathered.shape
     new_len = total_rows // requests
@@ -235,8 +238,12 @@
     slot_index = lax.axis_index("gx")
     inverse = jnp.zeros((requests,), jnp.int32).at[deal].set(jnp.arange(requests, dtype=jnp.int32))
     assert heads_local == 1
+    gather_cores = lax.axis_size(TOKEN_AXES[1])
+    gather_chips = lax.axis_size(TOKEN_AXES[0])
+    token_order = (inverse % gather_cores) * gather_chips + inverse // gather_cores
     packed = packed_partials(
         inverse,
+        token_order,
         gathered,
         gain,
         w_router,

time: 171 us -> 186 us (1.088)
  waiting for transfers between devices: 63.1 us -> 72.1 us
  starting transfers between devices: 15.5 us -> 20 us
    all_to_all x1, waiting for transfers between devices: 51.3 us -> 56.8 us  [per_device(): lax.all_to_all(packed.reshape(members, packed.shape[0] // members, packed...]
    all_to_all x1, starting transfers between devices: 8.54 us -> 13.1 us  [per_device(): lax.all_to_all(copies, 'gx', 0, 0, tiled=True)]
    all_gather x2, blocking collectives: 28.2 us -> 32.2 us  [the longest x1 23.5 us: per_device(): lax.all_gather(tokens, TOKEN_AXES[0], axis=0, tiled=True)]
    all_to_all x1, waiting for transfers between devices: 11.8 us -> 15.3 us  [per_device(): lax.all_to_all(copies, 'gx', 0, 0, tiled=True)]
    all_to_all x2, blocking collectives: 31.3 us -> 28.5 us  [scatter_sum(): lax.all_to_all(part.reshape((members, part.shape[0] // members) + part.sh...]
  transfers between devices with their start and end apart: 2 -> 2, of which waited for: 2 -> 2; matrix products, arithmetic and copies ran while one was open for 2% -> 1% of each run, Pallas kernels for 0% -> 0%
where the time goes in v12:
time: 186 us; the launch traced here: 185 us
  waiting for transfers between devices  72.1 us (39%)
  blocking collectives  60.7 us (33%)
  starting transfers between devices  20 us (11%)
  Pallas kernels  15.1 us (8%)
  local copies, waits for them, and re-layouts  6.63 us (4%)
  matrix products  6.08 us (3%)
  other arithmetic  3.01 us (2%)
    all_to_all x1, waiting for transfers between devices, per_device(): lax.all_to_all(packed.reshape(members, packed.shape[0] // members, packed...  56.8 us
    all_to_all x2, blocking collectives, scatter_sum(): lax.all_to_all(part.reshape((members, part.shape[0] // members) + part.sh...  28.5 us
    all_gather x1, blocking collectives, per_device(): lax.all_gather(tokens, TOKEN_AXES[0], axis=0, tiled=True)  23.5 us
    all_to_all x1, waiting for transfers between devices, per_device(): lax.all_to_all(copies, 'gx', 0, 0, tiled=True)  15.3 us
    all_to_all x1, starting transfers between devices, per_device(): lax.all_to_all(copies, 'gx', 0, 0, tiled=True)  13.1 us
    all_gather x1, blocking collectives, per_device(): lax.all_gather(lax.all_gather(tokens, TOKEN_AXES[0], axis=0, tiled=True),...  8.72 us
    pallas_call x1, Pallas kernels, packed_partials(): pl.pallas_call(pack_kernel, out_shape=jax.ShapeDtypeStruct((requests * bl...  8.72 us
    all_to_all x1, starting transfers between devices, per_device(): lax.all_to_all(packed.reshape(members, packed.shape[0] // members, packed...  6.94 us
  transfers between devices with their start and end apart: 2, of which 2 were waited for; matrix products, arithmetic and copies ran while one was open for 1% of the time, Pallas kernels for 0%

profile of v12, /device:TPU:1, one launch (start us, length us, event | category | flops | bytes accessed | tf_op | source)
XLA Modules:
  0.0 185.1 jit_solution(5176881058313392938)
XLA Ops:
  0.0 0.0 copy-start
  0.0 0.0 copy-start.3
  0.0 0.7 compare_select_fusion.1
  0.7 0.6 scatter_custom_fusion.order_ref
  1.4 0.0 copy-start.5
  1.4 0.5 fusion.15.token_order_ref
  1.9 0.0 copy-start.4
  1.9 2.1 %copy.19.route_ref = s32[2048,2]{1,0:T(8,128)} copy(s32[2048,2]{0,1:T(2,128)} %param.21) | data formatting | bytes 32768 | tf_op args[10]
  4.0 23.5 %all_gather.6 = bf16[1024,128]{1,0:T(8,128)(2,1)S(1)} all-gather(bf16[128,128]{1,0:T(8,128)(2,1)} %param.11), channel_id=1, replica_groups=mesh['gx'=16,'zz'=8,'cc'=2] {'zz'}, dimensions={0}, use_global_device_ids=true | all-gather | bytes 294912 | tf_op jit(solution)/shard_map/all_gather | solution.py:233
  27.5 8.7 %all_gather.7.tok_ref = bf16[2048,128]{1,0:T(8,128)(2,1)} all-gather(bf16[1024,128]{1,0:T(8,128)(2,1)S(1)} %all_gather.6), channel_id=1, replica_groups=mesh['gx'=16,'zz'=8,'cc'=2] {'cc'}, dimensions={0}, use_global_device_ids=true | all-gather | bytes 786432 | tf_op jit(solution)/shard_map/all_gather | solution.py:232
  36.2 0.0 copy-done.3
  36.2 0.0 copy-done.5
  36.2 0.0 copy-done.4
  36.3 0.8 pad_maximum_fusion.weight_ref
  37.0 8.7 %shard_map.109 = f32[2176,512]{1,0:T(8,128)} custom-call(s32[16]{0:T(128)} %copy-done.5, s32[16]{0:T(128)} %fusion.15.token_order_ref, bf16[2048,128]{1,0:T(8,128)(2,1)} %all_gather.7.tok_ref, bf16[1,128]{1,0:T(2,128)(2,1)} %bitcast.59, bf16[8,128]{1,0:T(8,128)(2,1)} %bitcast.58, bf16[128,1280]{1,0:T(8,128)(2,1)} %pad_maximum_fusion.weight_ref, ...), custom_call_target="tpu_custom_call" | custom-call | flops 675282944 | bytes 5308416 | tf_op jit(solution)/shard_map/pallas_call | solution.py:110
  45.7 0.0 copy-start.6
  45.7 0.0 copy-start.7
  45.7 0.0 copy-start.1
  45.7 6.9 %all-to-all-start = ((f32[16,136,512]{2,1,0:T(8,128)}), f32[16,136,512]{2,1,0:T(8,128)}, u32[]{:S(2)}, u32[]{:S(2)}) async-start(f32[16,136,512]{2,1,0:T(8,128)} %bitcast.51), calls=%async_computation | async-start | bytes 8912896 | tf_op jit(solution)/shard_map/all_to_all | solution.py:257
  52.7 0.0 copy-done.6
  52.7 0.6 dynamic-slice.4
  54.0 0.1 reshape.199
  54.1 0.1 reshape.198
  54.1 0.0 copy-done.7
  54.1 0.6 dynamic-slice.5
  54.8 0.0 copy-done.1
  54.8 0.7 gather_fusion
  56.1 0.1 broadcast_bitcast_fusion
  56.2 56.8 %all-to-all-done.blocks_ref = f32[16,136,512]{2,1,0:T(8,128)} async-done(((f32[16,136,512]{2,1,0:T(8,128)}), f32[16,136,512]{2,1,0:T(8,128)}, u32[]{:S(2)}, u32[]{:S(2)}) %all-to-all-start) | async-done | bytes 4456480 | tf_op jit(solution)/shard_map/all_to_all | solution.py:257
  113.0 6.4 %shard_map.110 = bf16[16,136,256]{2,1,0:T(8,128)(2,1)} custom-call(s32[1]{0:T(128)S(6)} %select_n.116.length_ref, f32[16,136,512]{2,1,0:T(8,128)} %all-to-all-done.blocks_ref, bf16[4096,128]{1,0:T(8,128)(2,1)} %bitcast.54, bf16[4096,128]{1,0:T(8,128)(2,1)} %bitcast.55), custom_call_target="tpu_custom_call" | custom-call | flops 553648128 | bytes 7667712 | tf_op jit(solution)/shard_map/pallas_call | solution.py:197
  119.4 0.0 copy-start.2
  119.4 13.1 %all-to-all-start.1 = ((bf16[16,136,256]{2,1,0:T(8,128)(2,1)}), bf16[16,136,256]{2,1,0:T(8,128)(2,1)S(1)}, u32[]{:S(2)}, u32[]{:S(2)}) async-start(bf16[16,136,256]{2,1,0:T(8,128)(2,1)} %shard_map.110), calls=%async_computation.1 | async-start | bytes 2228224 | tf_op jit(solution)/shard_map/all_to_all | solution.py:263
  132.5 0.0 copy-done.2
  132.5 0.6 gather_fusion.2
  133.1 15.3 %all-to-all-done.1 = bf16[16,136,256]{2,1,0:T(8,128)(2,1)S(1)} async-done(((bf16[16,136,256]{2,1,0:T(8,128)(2,1)}), bf16[16,136,256]{2,1,0:T(8,128)(2,1)S(1)}, u32[]{:S(2)}, u32[]{:S(2)}) %all-to-all-start.1) | async-done | bytes 1114144 | tf_op jit(solution)/shard_map/all_to_all | solution.py:263
  148.4 0.6 gather_fusion.1
  149.0 0.2 broadcast_select_fusion
  149.2 0.1 slice.25
  149.3 0.3 mul.31
  149.6 0.1 copy.20
  149.8 0.0 copy-done
  149.8 6.1 %fusion.10 = f32[2048,128]{1,0:T(8,128)S(1)} fusion(bf16[2048,2,8]{0,2,1:T(8,128)(2,1)S(1)} %convert_convert_fusion, bf16[2048,2,128]{2,0,1:T(8,128)(2,1)S(1)} %copy.20, f32[2048,2]{0,1:T(2,128)S(1)} %bitcast.57, bf16[8,1,128,128]{3,2,1,0:T(8,128)(2,1)S(1)} %copy-done), kind=kOutput, calls=%fused_computation.10 | convolution fusion | flops 1078722560 | bytes 2441216 | tf_op jit(solution)/shard_map/tsehk,ehko->tso/dot_general | solution.py:286
  155.9 7.4 %all_to_all.20 = f32[2,1024,128]{2,1,0:T(8,128)S(1)} all-to-all(f32[2,1024,128]{2,1,0:T(8,128)S(1)} %bitcast.53), channel_id=1, replica_groups=mesh['gx'=16,'zz'=8,'cc'=2] {'cc'}, dimensions={0} | all-to-all | bytes 2097152 | tf_op jit(solution)/shard_map/all_to_all | solution.py:25
  163.2 0.1 reduce_sum.28
  163.3 21.1 %all_to_all.21 = f32[8,128,128]{2,1,0:T(8,128)S(1)} all-to-all(f32[8,128,128]{2,1,0:T(8,128)S(1)} %bitcast.52), channel_id=1, replica_groups=mesh['gx'=16,'zz'=8,'cc'=2] {'zz'}, dimensions={0} | all-to-all | bytes 1048576 | tf_op jit(solution)/shard_map/all_to_all | solution.py:25
  184.5 0.6 reduce_sum.29
  (11 shorter events, 0.1 us)
Async XLA Ops:
  0.0 149.8 %copy-start = (bf16[8,1,128,128]{3,2,1,0:T(8,128)(2,1)S(1)}, bf16[8,1,128,128]{3,2,1,0:T(8,128)(2,1)}, u32[]{:S(2)}) copy-start(bf16[8,1,128,128]{3,2,1,0:T(8,128)(2,1)} %param.16) | copy-start | bytes 786436
  0.0 36.2 %copy-start.3 = (bf16[8,128,1,128]{3,1,2,0:T(8,128)(2,1)S(1)}, bf16[8,128,1,128]{3,1,2,0:T(8,128)(2,1)}, u32[]{:S(2)}) copy-start(bf16[8,128,1,128]{3,1,2,0:T(8,128)(2,1)} %param.14) | copy-start | bytes 786436
  1.4 34.9 %copy-start.5 = (s32[16]{0:T(128)}, s32[16]{0:T(128)S(1)}, u32[]{:S(2)}) copy-start(s32[16]{0:T(128)S(1)} %scatter_custom_fusion.order_ref) | copy-start | bytes 196
  1.9 34.3 %copy-start.4 = (bf16[128,1,256]{2,0,1:T(8,128)(2,1)S(1)}, bf16[128,1,256]{2,0,1:T(8,128)(2,1)}, u32[]{:S(2)}) copy-start(bf16[128,1,256]{2,0,1:T(8,128)(2,1)} %param.15) | copy-start | bytes 196612
  45.7 7.0 %copy-start.6 = (s32[16]{0:T(128)S(1)}, s32[16]{0:T(128)}, u32[]{:S(2)}) copy-start(s32[16]{0:T(128)} %copy-done.5) | copy-start | bytes 196
  45.7 8.4 %copy-start.7 = (s32[16]{0:T(128)S(1)}, s32[16]{0:T(128)}, u32[]{:S(2)}) copy-start(s32[16]{0:T(128)} %param.19) | copy-start | bytes 196
  45.7 9.0 %copy-start.1 = (s32[16]{0:T(128)S(1)}, s32[16]{0:T(128)}, u32[]{:S(2)}) copy-start(s32[16]{0:T(128)} %param.20) | copy-start | bytes 196
  45.7 67.2 %all-to-all-start = ((f32[16,136,512]{2,1,0:T(8,128)}), f32[16,136,512]{2,1,0:T(8,128)}, u32[]{:S(2)}, u32[]{:S(2)}) async-start(f32[16,136,512]{2,1,0:T(8,128)} %bitcast.51), calls=%async_computation | async-start | bytes 8912896 | tf_op jit(solution)/shard_map/all_to_all | solution.py:257
  119.4 13.1 %copy-start.2 = (s32[2048,2]{0,1:T(2,128)S(1)}, s32[2048,2]{0,1:T(2,128)}, u32[]{:S(2)}) copy-start(s32[2048,2]{0,1:T(2,128)} %param.21) | copy-start | bytes 49156
  119.4 29.0 %all-to-all-start.1 = ((bf16[16,136,256]{2,1,0:T(8,128)(2,1)}), bf16[16,136,256]{2,1,0:T(8,128)(2,1)S(1)}, u32[]{:S(2)}, u32[]{:S(2)}) async-start(bf16[16,136,256]{2,1,0:T(8,128)(2,1)} %shard_map.110), calls=%async_computation.1 | async-start | bytes 2228224 | tf_op jit(solution)/shard_map/all_to_all | solution.py:263

commit v13 on v11

--- a/solution.py
+++ b/solution.py
@@ -46,11 +46,20 @@
     experts = (weight_ref.shape[1] - 2 * head_dim) // head_dim
     contract_last = (((1,), (1,)), ((), ()))
     step = pl.program_id(0)
+    first_rows = [
+        pl.multiple_of(order_ref[step * REQUESTS_PER_STEP + block] * rows, rows)
+        for block in range(REQUESTS_PER_STEP)
+    ]
+    widened_all = jnp.concatenate(
+        [tok_ref[pl.ds(first_row, rows), :] for first_row in first_rows], axis=0
+    ).astype(jnp.float32)
+    scaled_all = (widened_all * gain_ref[...].astype(jnp.float32)).astype(jnp.bfloat16)
+    projected_all = jnp.dot(scaled_all, weight_ref[...], preferred_element_type=jnp.float32)
     for block in range(REQUESTS_PER_STEP):
-        first_row = pl.multiple_of(order_ref[step * REQUESTS_PER_STEP + block] * rows, rows)
-        widened = tok_ref[pl.ds(first_row, rows), :].astype(jnp.float32)
-        scaled = (widened * gain_ref[...].astype(jnp.float32)).astype(jnp.bfloat16)
-        projected = jnp.dot(scaled, weight_ref[...], preferred_element_type=jnp.float32)
+        first_row = first_rows[block]
+        widened = widened_all[block * rows : (block + 1) * rows]
+        scaled = scaled_all[block * rows : (block + 1) * rows]
+        projected = projected_all[block * rows : (block + 1) * rows]
         route = route_ref[pl.ds(first_row, rows), :]
         first = route[:, 0:1]
         second = route[:, 1:2]

time: 171 us -> 171 us (level)
  no operation moved by 1% of the time
where the time goes in v13:
time: 171 us; the launch traced here: 170 us
  waiting for transfers between devices  63.2 us (37%)
  blocking collectives  59.4 us (35%)
  starting transfers between devices  15.5 us (9%)
  Pallas kernels  15.1 us (9%)
  local copies, waits for them, and re-layouts  7.07 us (4%)
  matrix products  6.08 us (4%)
  other arithmetic  2.45 us (1%)
    all_to_all x1, waiting for transfers between devices, per_device(): lax.all_to_all(packed.reshape(members, packed.shape[0] // members, packed...  51.3 us
    all_to_all x2, blocking collectives, scatter_sum(): lax.all_to_all(part.reshape((members, part.shape[0] // members) + part.sh...  31.3 us
    all_gather x1, blocking collectives, per_device(): lax.all_gather(lax.all_gather(tokens, TOKEN_AXES[1], axis=0, tiled=True),...  23.3 us
    all_to_all x1, waiting for transfers between devices, per_device(): lax.all_to_all(copies, 'gx', 0, 0, tiled=True)  11.8 us
    pallas_call x1, Pallas kernels, packed_partials(): pl.pallas_call(pack_kernel, out_shape=jax.ShapeDtypeStruct((requests * bl...  8.64 us
    all_to_all x1, starting transfers between devices, per_device(): lax.all_to_all(copies, 'gx', 0, 0, tiled=True)  8.54 us
    all_to_all x1, starting transfers between devices, per_device(): lax.all_to_all(packed.reshape(members, packed.shape[0] // members, packed...  6.92 us
    pallas_call x1, Pallas kernels, attend(): pl.pallas_call(attend_kernel, out_shape=jax.ShapeDtypeStruct(out_shape, j...  6.42 us
  transfers between devices with their start and end apart: 2, of which 2 were waited for; matrix products, arithmetic and copies ran while one was open for 2% of the time, Pallas kernels for 0%

profile of v13, /device:TPU:1, one launch (start us, length us, event | category | flops | bytes accessed | tf_op | source)
XLA Modules:
  0.0 170.1 jit_solution(5775200058136997549)
XLA Ops:
  0.0 0.0 copy-start
  0.0 0.0 copy-start.3
  0.0 0.7 compare_select_fusion.1
  0.7 0.0 copy-start.4
  0.7 2.1 %copy.19.route_ref = s32[2048,2]{1,0:T(8,128)} copy(s32[2048,2]{0,1:T(2,128)} %param.21) | data formatting | bytes 32768 | tf_op args[10]
  2.8 4.9 %all_gather.6 = bf16[256,128]{1,0:T(8,128)(2,1)S(1)} all-gather(bf16[128,128]{1,0:T(8,128)(2,1)} %param.11), channel_id=1, replica_groups=mesh['gx'=16,'zz'=8,'cc'=2] {'cc'}, dimensions={0}, use_global_device_ids=true | all-gather | bytes 98304 | tf_op jit(solution)/shard_map/all_gather | solution.py:239
  7.7 23.3 %all_gather.7.tok_ref = bf16[2048,128]{1,0:T(8,128)(2,1)} all-gather(bf16[256,128]{1,0:T(8,128)(2,1)S(1)} %all_gather.6), channel_id=1, replica_groups=mesh['gx'=16,'zz'=8,'cc'=2] {'zz'}, dimensions={0}, use_global_device_ids=true | all-gather | bytes 589824 | tf_op jit(solution)/shard_map/all_gather | solution.py:238
  31.0 0.0 copy-done.3
  31.0 0.0 copy-done.4
  31.0 0.7 pad_maximum_fusion.weight_ref
  31.8 1.1 scatter_custom_fusion.order_ref
  32.9 8.6 %shard_map.109 = f32[2176,512]{1,0:T(8,128)} custom-call(s32[16]{0:T(128)} %scatter_custom_fusion.order_ref, bf16[2048,128]{1,0:T(8,128)(2,1)} %all_gather.7.tok_ref, bf16[1,128]{1,0:T(2,128)(2,1)} %bitcast.59, bf16[8,128]{1,0:T(8,128)(2,1)} %bitcast.58, bf16[128,1280]{1,0:T(8,128)(2,1)} %pad_maximum_fusion.weight_ref, s32[2048,2]{1,0:T(8,128)} %copy.19.route_ref, ...), custom_call_target="tpu_custom_call" | custom-call | flops 675282944 | bytes 5308416 | tf_op jit(solution)/shard_map/pallas_call | solution.py:116
  41.5 0.0 copy-start.5
  41.5 0.0 copy-start.6
  41.5 0.0 copy-start.1
  41.5 6.9 %all-to-all-start = ((f32[16,136,512]{2,1,0:T(8,128)}), f32[16,136,512]{2,1,0:T(8,128)}, u32[]{:S(2)}, u32[]{:S(2)}) async-start(f32[16,136,512]{2,1,0:T(8,128)} %bitcast.51), calls=%async_computation | async-start | bytes 8912896 | tf_op jit(solution)/shard_map/all_to_all | solution.py:259
  48.5 0.0 copy-done.5
  48.5 0.6 dynamic-slice.4
  49.7 0.1 reshape.197
  49.8 0.1 reshape.196
  49.8 0.0 copy-done.6
  49.8 0.6 dynamic-slice.5
  50.4 0.0 copy-done.1
  50.5 0.7 gather_fusion
  51.7 0.1 broadcast_bitcast_fusion
  51.8 51.3 %all-to-all-done.blocks_ref = f32[16,136,512]{2,1,0:T(8,128)} async-done(((f32[16,136,512]{2,1,0:T(8,128)}), f32[16,136,512]{2,1,0:T(8,128)}, u32[]{:S(2)}, u32[]{:S(2)}) %all-to-all-start) | async-done | bytes 4456480 | tf_op jit(solution)/shard_map/all_to_all | solution.py:259
  103.1 6.4 %shard_map.110 = bf16[16,136,256]{2,1,0:T(8,128)(2,1)} custom-call(s32[1]{0:T(128)S(6)} %select_n.104.length_ref, f32[16,136,512]{2,1,0:T(8,128)} %all-to-all-done.blocks_ref, bf16[4096,128]{1,0:T(8,128)(2,1)} %bitcast.54, bf16[4096,128]{1,0:T(8,128)(2,1)} %bitcast.55), custom_call_target="tpu_custom_call" | custom-call | flops 553648128 | bytes 7667712 | tf_op jit(solution)/shard_map/pallas_call | solution.py:203
  109.5 0.0 copy-start.2
  109.6 8.5 %all-to-all-start.1 = ((bf16[16,136,256]{2,1,0:T(8,128)(2,1)}), bf16[16,136,256]{2,1,0:T(8,128)(2,1)S(1)}, u32[]{:S(2)}, u32[]{:S(2)}) async-start(bf16[16,136,256]{2,1,0:T(8,128)(2,1)} %shard_map.110), calls=%async_computation.1 | async-start | bytes 2228224 | tf_op jit(solution)/shard_map/all_to_all | solution.py:265
  118.1 0.0 copy-done.2
  118.1 0.6 gather_fusion.2
  118.8 11.8 %all-to-all-done.1 = bf16[16,136,256]{2,1,0:T(8,128)(2,1)S(1)} async-done(((bf16[16,136,256]{2,1,0:T(8,128)(2,1)}), bf16[16,136,256]{2,1,0:T(8,128)(2,1)S(1)}, u32[]{:S(2)}, u32[]{:S(2)}) %all-to-all-start.1) | async-done | bytes 1114144 | tf_op jit(solution)/shard_map/all_to_all | solution.py:265
  130.6 0.6 gather_fusion.1
  131.2 0.2 broadcast_select_fusion
  131.4 0.1 slice.25
  131.5 0.3 mul.27
  131.8 0.1 copy.20
  132.0 0.0 copy-done
  132.0 6.1 %fusion.10 = f32[2048,128]{1,0:T(8,128)S(1)} fusion(bf16[2048,2,8]{0,2,1:T(8,128)(2,1)S(1)} %convert_convert_fusion, bf16[2048,2,128]{2,0,1:T(8,128)(2,1)S(1)} %copy.20, f32[2048,2]{0,1:T(2,128)S(1)} %bitcast.57, bf16[8,1,128,128]{3,2,1,0:T(8,128)(2,1)S(1)} %copy-done), kind=kOutput, calls=%fused_computation.10 | convolution fusion | flops 1078722560 | bytes 2441216 | tf_op jit(solution)/shard_map/tsehk,ehko->tso/dot_general | solution.py:288
  138.1 10.6 %all_to_all.20 = f32[2,1024,128]{2,1,0:T(8,128)S(1)} all-to-all(f32[2,1024,128]{2,1,0:T(8,128)S(1)} %bitcast.53), channel_id=1, replica_groups=mesh['gx'=16,'zz'=8,'cc'=2] {'cc'}, dimensions={0} | all-to-all | bytes 2097152 | tf_op jit(solution)/shard_map/all_to_all | solution.py:25
  148.6 0.1 reduce_sum.28
  148.7 20.7 %all_to_all.21 = f32[8,128,128]{2,1,0:T(8,128)S(1)} all-to-all(f32[8,128,128]{2,1,0:T(8,128)S(1)} %bitcast.52), channel_id=1, replica_groups=mesh['gx'=16,'zz'=8,'cc'=2] {'zz'}, dimensions={0} | all-to-all | bytes 1048576 | tf_op jit(solution)/shard_map/all_to_all | solution.py:25
  169.4 0.6 reduce_sum.29
  (11 shorter events, 0.1 us)
Async XLA Ops:
  0.0 132.0 %copy-start = (bf16[8,1,128,128]{3,2,1,0:T(8,128)(2,1)S(1)}, bf16[8,1,128,128]{3,2,1,0:T(8,128)(2,1)}, u32[]{:S(2)}) copy-start(bf16[8,1,128,128]{3,2,1,0:T(8,128)(2,1)} %param.16) | copy-start | bytes 786436
  0.0 31.0 %copy-start.3 = (bf16[8,128,1,128]{3,1,2,0:T(8,128)(2,1)S(1)}, bf16[8,128,1,128]{3,1,2,0:T(8,128)(2,1)}, u32[]{:S(2)}) copy-start(bf16[8,128,1,128]{3,1,2,0:T(8,128)(2,1)} %param.14) | copy-start | bytes 786436
  0.7 30.3 %copy-start.4 = (bf16[128,1,256]{2,0,1:T(8,128)(2,1)S(1)}, bf16[128,1,256]{2,0,1:T(8,128)(2,1)}, u32[]{:S(2)}) copy-start(bf16[128,1,256]{2,0,1:T(8,128)(2,1)} %param.15) | copy-start | bytes 196612
  41.5 6.9 %copy-start.5 = (s32[16]{0:T(128)S(1)}, s32[16]{0:T(128)}, u32[]{:S(2)}) copy-start(s32[16]{0:T(128)} %scatter_custom_fusion.order_ref) | copy-start | bytes 196
  41.5 8.3 %copy-start.6 = (s32[16]{0:T(128)S(1)}, s32[16]{0:T(128)}, u32[]{:S(2)}) copy-start(s32[16]{0:T(128)} %param.19) | copy-start | bytes 196
  41.5 8.9 %copy-start.1 = (s32[16]{0:T(128)S(1)}, s32[16]{0:T(128)}, u32[]{:S(2)}) copy-start(s32[16]{0:T(128)} %param.20) | copy-start | bytes 196
  41.5 61.6 %all-to-all-start = ((f32[16,136,512]{2,1,0:T(8,128)}), f32[16,136,512]{2,1,0:T(8,128)}, u32[]{:S(2)}, u32[]{:S(2)}) async-start(f32[16,136,512]{2,1,0:T(8,128)} %bitcast.51), calls=%async_computation | async-start | bytes 8912896 | tf_op jit(solution)/shard_map/all_to_all | solution.py:259
  109.5 8.6 %copy-start.2 = (s32[2048,2]{0,1:T(2,128)S(1)}, s32[2048,2]{0,1:T(2,128)}, u32[]{:S(2)}) copy-start(s32[2048,2]{0,1:T(2,128)} %param.21) | copy-start | bytes 49156
  109.6 21.1 %all-to-all-start.1 = ((bf16[16,136,256]{2,1,0:T(8,128)(2,1)}), bf16[16,136,256]{2,1,0:T(8,128)(2,1)S(1)}, u32[]{:S(2)}, u32[]{:S(2)}) async-start(bf16[16,136,256]{2,1,0:T(8,128)(2,1)} %shard_map.110), calls=%async_computation.1 | async-start | bytes 2228224 | tf_op jit(solution)/shard_map/all_to_all | solution.py:265

commit v14 on v11

--- a/solution.py
+++ b/solution.py
@@ -84,7 +84,7 @@
 
 
 EXTRA_ROWS = 8
-REQUESTS_PER_STEP = 4
+REQUESTS_PER_STEP = 8
 
 
 def packed_partials(order, gathered, gain, w_router, query_weight, keyval_weight, route):

time: 171 us -> 171 us (level)
  no operation moved by 1% of the time
where the time goes in v14:
time: 171 us; the launch traced here: 170 us
  waiting for transfers between devices  63.1 us (37%)
  blocking collectives  59.5 us (35%)
  starting transfers between devices  15.5 us (9%)
  Pallas kernels  15.3 us (9%)
  local copies, waits for them, and re-layouts  7.07 us (4%)
  matrix products  6.08 us (4%)
  other arithmetic  2.45 us (1%)
    all_to_all x1, waiting for transfers between devices, per_device(): lax.all_to_all(packed.reshape(members, packed.shape[0] // members, packed...  51.3 us
    all_to_all x2, blocking collectives, scatter_sum(): lax.all_to_all(part.reshape((members, part.shape[0] // members) + part.sh...  31.3 us
    all_gather x1, blocking collectives, per_device(): lax.all_gather(lax.all_gather(tokens, TOKEN_AXES[1], axis=0, tiled=True),...  23.3 us
    all_to_all x1, waiting for transfers between devices, per_device(): lax.all_to_all(copies, 'gx', 0, 0, tiled=True)  11.8 us
    pallas_call x1, Pallas kernels, packed_partials(): pl.pallas_call(pack_kernel, out_shape=jax.ShapeDtypeStruct((requests * bl...  8.91 us
    all_to_all x1, starting transfers between devices, per_device(): lax.all_to_all(copies, 'gx', 0, 0, tiled=True)  8.55 us
    all_to_all x1, starting transfers between devices, per_device(): lax.all_to_all(packed.reshape(members, packed.shape[0] // members, packed...  6.94 us
    pallas_call x1, Pallas kernels, attend(): pl.pallas_call(attend_kernel, out_shape=jax.ShapeDtypeStruct(out_shape, j...  6.42 us
  transfers between devices with their start and end apart: 2, of which 2 were waited for; matrix products, arithmetic and copies ran while one was open for 2% of the time, Pallas kernels for 0%

profile of v14, /device:TPU:1, one launch (start us, length us, event | category | flops | bytes accessed | tf_op | source)
XLA Modules:
  0.0 170.4 jit_solution(7001792683961343051)
XLA Ops:
  0.0 0.0 copy-start
  0.0 0.0 copy-start.3
  0.0 0.7 compare_select_fusion.1
  0.7 0.0 copy-start.4
  0.7 2.1 %copy.19.route_ref = s32[2048,2]{1,0:T(8,128)} copy(s32[2048,2]{0,1:T(2,128)} %param.21) | data formatting | bytes 32768 | tf_op args[10]
  2.8 4.9 %all_gather.6 = bf16[256,128]{1,0:T(8,128)(2,1)S(1)} all-gather(bf16[128,128]{1,0:T(8,128)(2,1)} %param.11), channel_id=1, replica_groups=mesh['gx'=16,'zz'=8,'cc'=2] {'cc'}, dimensions={0}, use_global_device_ids=true | all-gather | bytes 98304 | tf_op jit(solution)/shard_map/all_gather | solution.py:230
  7.7 23.3 %all_gather.7.tok_ref = bf16[2048,128]{1,0:T(8,128)(2,1)} all-gather(bf16[256,128]{1,0:T(8,128)(2,1)S(1)} %all_gather.6), channel_id=1, replica_groups=mesh['gx'=16,'zz'=8,'cc'=2] {'zz'}, dimensions={0}, use_global_device_ids=true | all-gather | bytes 589824 | tf_op jit(solution)/shard_map/all_gather | solution.py:229
  31.0 0.0 copy-done.3
  31.0 0.0 copy-done.4
  31.0 0.7 pad_maximum_fusion.weight_ref
  31.8 1.1 scatter_custom_fusion.order_ref
  32.9 8.9 %shard_map.109 = f32[2176,512]{1,0:T(8,128)} custom-call(s32[16]{0:T(128)} %scatter_custom_fusion.order_ref, bf16[2048,128]{1,0:T(8,128)(2,1)} %all_gather.7.tok_ref, bf16[1,128]{1,0:T(2,128)(2,1)} %bitcast.59, bf16[8,128]{1,0:T(8,128)(2,1)} %bitcast.58, bf16[128,1280]{1,0:T(8,128)(2,1)} %pad_maximum_fusion.weight_ref, s32[2048,2]{1,0:T(8,128)} %copy.19.route_ref, ...), custom_call_target="tpu_custom_call" | custom-call | flops 675282944 | bytes 5308416 | tf_op jit(solution)/shard_map/pallas_call | solution.py:107
  41.8 0.0 copy-start.5
  41.8 0.0 copy-start.6
  41.8 0.0 copy-start.1
  41.8 6.9 %all-to-all-start = ((f32[16,136,512]{2,1,0:T(8,128)}), f32[16,136,512]{2,1,0:T(8,128)}, u32[]{:S(2)}, u32[]{:S(2)}) async-start(f32[16,136,512]{2,1,0:T(8,128)} %bitcast.51), calls=%async_computation | async-start | bytes 8912896 | tf_op jit(solution)/shard_map/all_to_all | solution.py:250
  48.8 0.0 copy-done.5
  48.8 0.6 dynamic-slice.4
  50.0 0.1 reshape.197
  50.1 0.1 reshape.196
  50.1 0.0 copy-done.6
  50.1 0.6 dynamic-slice.5
  50.7 0.0 copy-done.1
  50.7 0.7 gather_fusion
  52.0 0.1 broadcast_bitcast_fusion
  52.1 51.3 %all-to-all-done.blocks_ref = f32[16,136,512]{2,1,0:T(8,128)} async-done(((f32[16,136,512]{2,1,0:T(8,128)}), f32[16,136,512]{2,1,0:T(8,128)}, u32[]{:S(2)}, u32[]{:S(2)}) %all-to-all-start) | async-done | bytes 4456480 | tf_op jit(solution)/shard_map/all_to_all | solution.py:250
  103.4 6.4 %shard_map.110 = bf16[16,136,256]{2,1,0:T(8,128)(2,1)} custom-call(s32[1]{0:T(128)S(6)} %select_n.104.length_ref, f32[16,136,512]{2,1,0:T(8,128)} %all-to-all-done.blocks_ref, bf16[4096,128]{1,0:T(8,128)(2,1)} %bitcast.54, bf16[4096,128]{1,0:T(8,128)(2,1)} %bitcast.55), custom_call_target="tpu_custom_call" | custom-call | flops 553648128 | bytes 7667712 | tf_op jit(solution)/shard_map/pallas_call | solution.py:194
  109.8 0.0 copy-start.2
  109.8 8.5 %all-to-all-start.1 = ((bf16[16,136,256]{2,1,0:T(8,128)(2,1)}), bf16[16,136,256]{2,1,0:T(8,128)(2,1)S(1)}, u32[]{:S(2)}, u32[]{:S(2)}) async-start(bf16[16,136,256]{2,1,0:T(8,128)(2,1)} %shard_map.110), calls=%async_computation.1 | async-start | bytes 2228224 | tf_op jit(solution)/shard_map/all_to_all | solution.py:256
  118.4 0.0 copy-done.2
  118.4 0.6 gather_fusion.2
  119.0 11.8 %all-to-all-done.1 = bf16[16,136,256]{2,1,0:T(8,128)(2,1)S(1)} async-done(((bf16[16,136,256]{2,1,0:T(8,128)(2,1)}), bf16[16,136,256]{2,1,0:T(8,128)(2,1)S(1)}, u32[]{:S(2)}, u32[]{:S(2)}) %all-to-all-start.1) | async-done | bytes 1114144 | tf_op jit(solution)/shard_map/all_to_all | solution.py:256
  130.9 0.6 gather_fusion.1
  131.5 0.2 broadcast_select_fusion
  131.7 0.1 slice.25
  131.8 0.3 mul.27
  132.1 0.1 copy.20
  132.2 0.0 copy-done
  132.3 6.1 %fusion.10 = f32[2048,128]{1,0:T(8,128)S(1)} fusion(bf16[2048,2,8]{0,2,1:T(8,128)(2,1)S(1)} %convert_convert_fusion, bf16[2048,2,128]{2,0,1:T(8,128)(2,1)S(1)} %copy.20, f32[2048,2]{0,1:T(2,128)S(1)} %bitcast.57, bf16[8,1,128,128]{3,2,1,0:T(8,128)(2,1)S(1)} %copy-done), kind=kOutput, calls=%fused_computation.10 | convolution fusion | flops 1078722560 | bytes 2441216 | tf_op jit(solution)/shard_map/tsehk,ehko->tso/dot_general | solution.py:279
  138.3 10.6 %all_to_all.20 = f32[2,1024,128]{2,1,0:T(8,128)S(1)} all-to-all(f32[2,1024,128]{2,1,0:T(8,128)S(1)} %bitcast.53), channel_id=1, replica_groups=mesh['gx'=16,'zz'=8,'cc'=2] {'cc'}, dimensions={0} | all-to-all | bytes 2097152 | tf_op jit(solution)/shard_map/all_to_all | solution.py:25
  148.9 0.1 reduce_sum.28
  149.0 20.7 %all_to_all.21 = f32[8,128,128]{2,1,0:T(8,128)S(1)} all-to-all(f32[8,128,128]{2,1,0:T(8,128)S(1)} %bitcast.52), channel_id=1, replica_groups=mesh['gx'=16,'zz'=8,'cc'=2] {'zz'}, dimensions={0} | all-to-all | bytes 1048576 | tf_op jit(solution)/shard_map/all_to_all | solution.py:25
  169.7 0.6 reduce_sum.29
  (11 shorter events, 0.1 us)
Async XLA Ops:
  0.0 132.2 %copy-start = (bf16[8,1,128,128]{3,2,1,0:T(8,128)(2,1)S(1)}, bf16[8,1,128,128]{3,2,1,0:T(8,128)(2,1)}, u32[]{:S(2)}) copy-start(bf16[8,1,128,128]{3,2,1,0:T(8,128)(2,1)} %param.16) | copy-start | bytes 786436
  0.0 31.0 %copy-start.3 = (bf16[8,128,1,128]{3,1,2,0:T(8,128)(2,1)S(1)}, bf16[8,128,1,128]{3,1,2,0:T(8,128)(2,1)}, u32[]{:S(2)}) copy-start(bf16[8,128,1,128]{3,1,2,0:T(8,128)(2,1)} %param.14) | copy-start | bytes 786436
  0.7 30.3 %copy-start.4 = (bf16[128,1,256]{2,0,1:T(8,128)(2,1)S(1)}, bf16[128,1,256]{2,0,1:T(8,128)(2,1)}, u32[]{:S(2)}) copy-start(bf16[128,1,256]{2,0,1:T(8,128)(2,1)} %param.15) | copy-start | bytes 196612
  41.8 7.0 %copy-start.5 = (s32[16]{0:T(128)S(1)}, s32[16]{0:T(128)}, u32[]{:S(2)}) copy-start(s32[16]{0:T(128)} %scatter_custom_fusion.order_ref) | copy-start | bytes 196
  41.8 8.3 %copy-start.6 = (s32[16]{0:T(128)S(1)}, s32[16]{0:T(128)}, u32[]{:S(2)}) copy-start(s32[16]{0:T(128)} %param.19) | copy-start | bytes 196
  41.8 8.9 %copy-start.1 = (s32[16]{0:T(128)S(1)}, s32[16]{0:T(128)}, u32[]{:S(2)}) copy-start(s32[16]{0:T(128)} %param.20) | copy-start | bytes 196
  41.8 61.6 %all-to-all-start = ((f32[16,136,512]{2,1,0:T(8,128)}), f32[16,136,512]{2,1,0:T(8,128)}, u32[]{:S(2)}, u32[]{:S(2)}) async-start(f32[16,136,512]{2,1,0:T(8,128)} %bitcast.51), calls=%async_computation | async-start | bytes 8912896 | tf_op jit(solution)/shard_map/all_to_all | solution.py:250
  109.8 8.6 %copy-start.2 = (s32[2048,2]{0,1:T(2,128)S(1)}, s32[2048,2]{0,1:T(2,128)}, u32[]{:S(2)}) copy-start(s32[2048,2]{0,1:T(2,128)} %param.21) | copy-start | bytes 49156
  109.8 21.1 %all-to-all-start.1 = ((bf16[16,136,256]{2,1,0:T(8,128)(2,1)}), bf16[16,136,256]{2,1,0:T(8,128)(2,1)S(1)}, u32[]{:S(2)}, u32[]{:S(2)}) async-start(bf16[16,136,256]{2,1,0:T(8,128)(2,1)} %shard_map.110), calls=%async_computation.1 | async-start | bytes 2228224 | tf_op jit(solution)/shard_map/all_to_all | solution.py:256

commit v15 on v14

--- a/solution.py
+++ b/solution.py
@@ -84,7 +84,7 @@
 
 
 EXTRA_ROWS = 8
-REQUESTS_PER_STEP = 8
+REQUESTS_PER_STEP = 2
 
 
 def packed_partials(order, gathered, gain, w_router, query_weight, keyval_weight, route):

time: 171 us -> 171 us (level)
  no operation moved by 1% of the time
where the time goes in v15:
time: 171 us
  waiting for transfers between devices  63.2 us (37%)
  blocking collectives  59.4 us (35%)
  Pallas kernels  15.5 us (9%)
  starting transfers between devices  15.5 us (9%)
  local copies, waits for them, and re-layouts  7.08 us (4%)
  matrix products  6.08 us (4%)
  other arithmetic  2.45 us (1%)
    all_to_all x1, waiting for transfers between devices, per_device(): lax.all_to_all(packed.reshape(members, packed.shape[0] // members, packed...  51.3 us
    all_to_all x2, blocking collectives, scatter_sum(): lax.all_to_all(part.reshape((members, part.shape[0] // members) + part.sh...  31.3 us
    all_gather x1, blocking collectives, per_device(): lax.all_gather(lax.all_gather(tokens, TOKEN_AXES[1], axis=0, tiled=True),...  23.3 us
    all_to_all x1, waiting for transfers between devices, per_device(): lax.all_to_all(copies, 'gx', 0, 0, tiled=True)  11.9 us
    pallas_call x1, Pallas kernels, packed_partials(): pl.pallas_call(pack_kernel, out_shape=jax.ShapeDtypeStruct((requests * bl...  9.06 us
    all_to_all x1, starting transfers between devices, per_device(): lax.all_to_all(copies, 'gx', 0, 0, tiled=True)  8.54 us
    all_to_all x1, starting transfers between devices, per_device(): lax.all_to_all(packed.reshape(members, packed.shape[0] // members, packed...  6.94 us
    pallas_call x1, Pallas kernels, attend(): pl.pallas_call(attend_kernel, out_shape=jax.ShapeDtypeStruct(out_shape, j...  6.42 us
  transfers between devices with their start and end apart: 2, of which 2 were waited for; matrix products, arithmetic and copies ran while one was open for 2% of the time, Pallas kernels for 0%

profile of v15, /device:TPU:1, one launch (start us, length us, event | category | flops | bytes accessed | tf_op | source)
XLA Modules:
  0.0 170.5 jit_solution(15316652711914166458)
XLA Ops:
  0.0 0.0 copy-start
  0.0 0.0 copy-start.3
  0.0 0.7 compare_select_fusion.1
  0.7 0.0 copy-start.4
  0.7 2.1 %copy.19.route_ref = s32[2048,2]{1,0:T(8,128)} copy(s32[2048,2]{0,1:T(2,128)} %param.21) | data formatting | bytes 32768 | tf_op args[10]
  2.8 4.9 %all_gather.6 = bf16[256,128]{1,0:T(8,128)(2,1)S(1)} all-gather(bf16[128,128]{1,0:T(8,128)(2,1)} %param.11), channel_id=1, replica_groups=mesh['gx'=16,'zz'=8,'cc'=2] {'cc'}, dimensions={0}, use_global_device_ids=true | all-gather | bytes 98304 | tf_op jit(solution)/shard_map/all_gather | solution.py:230
  7.7 23.3 %all_gather.7.tok_ref = bf16[2048,128]{1,0:T(8,128)(2,1)} all-gather(bf16[256,128]{1,0:T(8,128)(2,1)S(1)} %all_gather.6), channel_id=1, replica_groups=mesh['gx'=16,'zz'=8,'cc'=2] {'zz'}, dimensions={0}, use_global_device_ids=true | all-gather | bytes 589824 | tf_op jit(solution)/shard_map/all_gather | solution.py:229
  31.0 0.0 copy-done.3
  31.0 0.0 copy-done.4
  31.0 0.7 pad_maximum_fusion.weight_ref
  31.8 1.1 scatter_custom_fusion.order_ref
  32.9 9.1 %shard_map.109 = f32[2176,512]{1,0:T(8,128)} custom-call(s32[16]{0:T(128)} %scatter_custom_fusion.order_ref, bf16[2048,128]{1,0:T(8,128)(2,1)} %all_gather.7.tok_ref, bf16[1,128]{1,0:T(2,128)(2,1)} %bitcast.59, bf16[8,128]{1,0:T(8,128)(2,1)} %bitcast.58, bf16[128,1280]{1,0:T(8,128)(2,1)} %pad_maximum_fusion.weight_ref, s32[2048,2]{1,0:T(8,128)} %copy.19.route_ref, ...), custom_call_target="tpu_custom_call" | custom-call | flops 675282944 | bytes 5308416 | tf_op jit(solution)/shard_map/pallas_call | solution.py:107
  42.0 0.0 copy-start.5
  42.0 0.0 copy-start.6
  42.0 0.0 copy-start.1
  42.0 6.9 %all-to-all-start = ((f32[16,136,512]{2,1,0:T(8,128)}), f32[16,136,512]{2,1,0:T(8,128)}, u32[]{:S(2)}, u32[]{:S(2)}) async-start(f32[16,136,512]{2,1,0:T(8,128)} %bitcast.51), calls=%async_computation | async-start | bytes 8912896 | tf_op jit(solution)/shard_map/all_to_all | solution.py:250
  48.9 0.0 copy-done.5
  48.9 0.6 dynamic-slice.4
  50.1 0.1 reshape.197
  50.2 0.1 reshape.196
  50.3 0.0 copy-done.6
  50.3 0.6 dynamic-slice.5
  50.9 0.0 copy-done.1
  50.9 0.7 gather_fusion
  52.2 0.1 broadcast_bitcast_fusion
  52.2 51.3 %all-to-all-done.blocks_ref = f32[16,136,512]{2,1,0:T(8,128)} async-done(((f32[16,136,512]{2,1,0:T(8,128)}), f32[16,136,512]{2,1,0:T(8,128)}, u32[]{:S(2)}, u32[]{:S(2)}) %all-to-all-start) | async-done | bytes 4456480 | tf_op jit(solution)/shard_map/all_to_all | solution.py:250
  103.5 6.4 %shard_map.110 = bf16[16,136,256]{2,1,0:T(8,128)(2,1)} custom-call(s32[1]{0:T(128)S(6)} %select_n.104.length_ref, f32[16,136,512]{2,1,0:T(8,128)} %all-to-all-done.blocks_ref, bf16[4096,128]{1,0:T(8,128)(2,1)} %bitcast.54, bf16[4096,128]{1,0:T(8,128)(2,1)} %bitcast.55), custom_call_target="tpu_custom_call" | custom-call | flops 553648128 | bytes 7667712 | tf_op jit(solution)/shard_map/pallas_call | solution.py:194
  110.0 0.0 copy-start.2
  110.0 8.5 %all-to-all-start.1 = ((bf16[16,136,256]{2,1,0:T(8,128)(2,1)}), bf16[16,136,256]{2,1,0:T(8,128)(2,1)S(1)}, u32[]{:S(2)}, u32[]{:S(2)}) async-start(bf16[16,136,256]{2,1,0:T(8,128)(2,1)} %shard_map.110), calls=%async_computation.1 | async-start | bytes 2228224 | tf_op jit(solution)/shard_map/all_to_all | solution.py:256
  118.5 0.0 copy-done.2
  118.5 0.6 gather_fusion.2
  119.2 11.9 %all-to-all-done.1 = bf16[16,136,256]{2,1,0:T(8,128)(2,1)S(1)} async-done(((bf16[16,136,256]{2,1,0:T(8,128)(2,1)}), bf16[16,136,256]{2,1,0:T(8,128)(2,1)S(1)}, u32[]{:S(2)}, u32[]{:S(2)}) %all-to-all-start.1) | async-done | bytes 1114144 | tf_op jit(solution)/shard_map/all_to_all | solution.py:256
  131.1 0.6 gather_fusion.1
  131.7 0.2 broadcast_select_fusion
  131.9 0.1 slice.25
  132.0 0.3 mul.27
  132.3 0.1 copy.20
  132.4 0.0 copy-done
  132.4 6.1 %fusion.10 = f32[2048,128]{1,0:T(8,128)S(1)} fusion(bf16[2048,2,8]{0,2,1:T(8,128)(2,1)S(1)} %convert_convert_fusion, bf16[2048,2,128]{2,0,1:T(8,128)(2,1)S(1)} %copy.20, f32[2048,2]{0,1:T(2,128)S(1)} %bitcast.57, bf16[8,1,128,128]{3,2,1,0:T(8,128)(2,1)S(1)} %copy-done), kind=kOutput, calls=%fused_computation.10 | convolution fusion | flops 1078722560 | bytes 2441216 | tf_op jit(solution)/shard_map/tsehk,ehko->tso/dot_general | solution.py:279
  138.5 10.5 %all_to_all.20 = f32[2,1024,128]{2,1,0:T(8,128)S(1)} all-to-all(f32[2,1024,128]{2,1,0:T(8,128)S(1)} %bitcast.53), channel_id=1, replica_groups=mesh['gx'=16,'zz'=8,'cc'=2] {'cc'}, dimensions={0} | all-to-all | bytes 2097152 | tf_op jit(solution)/shard_map/all_to_all | solution.py:25
  149.1 0.1 reduce_sum.28
  149.2 20.7 %all_to_all.21 = f32[8,128,128]{2,1,0:T(8,128)S(1)} all-to-all(f32[8,128,128]{2,1,0:T(8,128)S(1)} %bitcast.52), channel_id=1, replica_groups=mesh['gx'=16,'zz'=8,'cc'=2] {'zz'}, dimensions={0} | all-to-all | bytes 1048576 | tf_op jit(solution)/shard_map/all_to_all | solution.py:25
  169.9 0.6 reduce_sum.29
  (11 shorter events, 0.1 us)
Async XLA Ops:
  0.0 132.4 %copy-start = (bf16[8,1,128,128]{3,2,1,0:T(8,128)(2,1)S(1)}, bf16[8,1,128,128]{3,2,1,0:T(8,128)(2,1)}, u32[]{:S(2)}) copy-start(bf16[8,1,128,128]{3,2,1,0:T(8,128)(2,1)} %param.16) | copy-start | bytes 786436
  0.0 31.0 %copy-start.3 = (bf16[8,128,1,128]{3,1,2,0:T(8,128)(2,1)S(1)}, bf16[8,128,1,128]{3,1,2,0:T(8,128)(2,1)}, u32[]{:S(2)}) copy-start(bf16[8,128,1,128]{3,1,2,0:T(8,128)(2,1)} %param.14) | copy-start | bytes 786436
  0.7 30.3 %copy-start.4 = (bf16[128,1,256]{2,0,1:T(8,128)(2,1)S(1)}, bf16[128,1,256]{2,0,1:T(8,128)(2,1)}, u32[]{:S(2)}) copy-start(bf16[128,1,256]{2,0,1:T(8,128)(2,1)} %param.15) | copy-start | bytes 196612
  42.0 7.0 %copy-start.5 = (s32[16]{0:T(128)S(1)}, s32[16]{0:T(128)}, u32[]{:S(2)}) copy-start(s32[16]{0:T(128)} %scatter_custom_fusion.order_ref) | copy-start | bytes 196
  42.0 8.3 %copy-start.6 = (s32[16]{0:T(128)S(1)}, s32[16]{0:T(128)}, u32[]{:S(2)}) copy-start(s32[16]{0:T(128)} %param.19) | copy-start | bytes 196
  42.0 8.9 %copy-start.1 = (s32[16]{0:T(128)S(1)}, s32[16]{0:T(128)}, u32[]{:S(2)}) copy-start(s32[16]{0:T(128)} %param.20) | copy-start | bytes 196
  42.0 61.6 %all-to-all-start = ((f32[16,136,512]{2,1,0:T(8,128)}), f32[16,136,512]{2,1,0:T(8,128)}, u32[]{:S(2)}, u32[]{:S(2)}) async-start(f32[16,136,512]{2,1,0:T(8,128)} %bitcast.51), calls=%async_computation | async-start | bytes 8912896 | tf_op jit(solution)/shard_map/all_to_all | solution.py:250
  110.0 8.6 %copy-start.2 = (s32[2048,2]{0,1:T(2,128)S(1)}, s32[2048,2]{0,1:T(2,128)}, u32[]{:S(2)}) copy-start(s32[2048,2]{0,1:T(2,128)} %param.21) | copy-start | bytes 49156
  110.0 21.1 %all-to-all-start.1 = ((bf16[16,136,256]{2,1,0:T(8,128)(2,1)}), bf16[16,136,256]{2,1,0:T(8,128)(2,1)S(1)}, u32[]{:S(2)}, u32[]{:S(2)}) async-start(bf16[16,136,256]{2,1,0:T(8,128)(2,1)} %shard_map.110), calls=%async_computation.1 | async-start | bytes 2228224 | tf_op jit(solution)/shard_map/all_to_all | solution.py:256
